TPU v7x, 32 devices: a whole 2x2x4 slice. The times are simulated.
32 devices in a mesh: trait: 4 (over y, x), tile: 8 (over z, core).
Axes of the slice: x: 2, y: 2, z: 4, core: 2. Of those that a mesh axis runs over, the one named last changes fastest.
Arguments:
- probe_signs: int32 [4, 16, 64, 2048], P(None, 'trait', 'tile'), may hold values from 0 to 1
- land_mask: int32 [64, 2048], P('tile'), may hold values from 0 to 1
- kappa_sq: float32 [64, 2048], P('tile'), may hold values from 0.2 to 4.5
- trait_covariance: float32 [16, 16], replicated, may hold values from -0.025 to 3, as said below
Outputs:
- alphas: float32 [4, 3], replicated
- betas: float32 [4, 3], replicated
- last_vector: float32 [4, 16, 64, 2048], P(None, 'trait', 'tile')
Inputs may be any that keep to these rules, and one draw needn't show every extreme that they name: `trait_covariance`: symmetric.
All inputs are finite; a program needn't handle non-finite values.
Results may differ from a plain program's by a relative error of at most 0.0003.
Values may be sent and summed in bfloat16 or wider, within the bound.
No kernel may reach another device: no remote copies, remote signals or barrier semaphores. Data moves between devices by JAX's collectives and lax.ppermute only.
A program may use at most 64 MiB of HBM per device.

v0:
```python
import jax
import jax.numpy as jnp
from jax import lax
from jax.sharding import PartitionSpec as P


along_cols = 0.25
along_rows = 0.15
cross_term = 0.1
epsilon = 1e-06

HALO = 6


def nine_valid(x, kappa_rows):
    padded = jnp.pad(x, [(0, 0)] * (x.ndim - 1) + [(1, 1)])
    center = padded[..., 1:-1, 1:-1]
    sideways = padded[..., 1:-1, :-2] + padded[..., 1:-1, 2:]
    vertical = padded[..., :-2, 1:-1] + padded[..., 2:, 1:-1]
    diag_main = padded[..., 2:, 2:] + padded[..., :-2, :-2]
    diag_anti = padded[..., 2:, :-2] + padded[..., :-2, 2:]
    return (
        (kappa_rows + 2.0 * along_cols + 2.0 * along_rows) * center
        - along_cols * sideways
        - along_rows * vertical
        - 0.5 * cross_term * (diag_main - diag_anti)
    )


def butterfly_sum(v, axis, work=()):
    n = lax.axis_size(axis)
    carry = None
    if n & (n - 1):
        for stage in work:
            carry = stage(carry)
        return lax.psum(v, axis), carry
    s = 1
    r = 0
    while s < n:
        got = lax.ppermute(v, axis, [(i, i ^ s) for i in range(n)])
        if r < len(work):
            carry = work[r](carry)
            v, carry = lax.optimization_barrier((v + got, carry))
        else:
            v = v + got
        s *= 2
        r += 1
    for stage in work[r:]:
        carry = stage(carry)
    return v, carry


def halo_rows(block, width):
    n = lax.axis_size("tile")
    dim = block.ndim - 2
    rows = block.shape[dim]
    assert rows >= width and n % 2 == 0
    top = lax.slice_in_dim(block, 0, width, axis=dim)
    bottom = lax.slice_in_dim(block, rows - width, rows, axis=dim)
    odd = lax.axis_index("tile") % 2 == 1
    across = [(i, i + 1) for i in range(1, n - 1, 2)] + [(i + 1, i) for i in range(1, n - 1, 2)]
    within = [(i, i + 1) for i in range(0, n - 1, 2)] + [(i + 1, i) for i in range(0, n - 1, 2)]
    send = jnp.where(odd, bottom, top)
    pieces = 2 if width % 2 == 0 else 1
    step = width // pieces
    got_across = jnp.concatenate(
        [
            lax.ppermute(lax.slice_in_dim(send, k * step, (k + 1) * step, axis=dim), "tile", across)
            for k in range(pieces)
        ],
        axis=dim,
    )
    got_within = lax.ppermute(jnp.where(odd, top, bottom), "tile", within)
    low = jnp.where(odd, got_within, got_across)
    high = jnp.where(odd, got_across, got_within)
    return jnp.concatenate([low, block, high], axis=dim)


def shards(probe_signs, land_mask, kappa_sq, trait_covariance):
    rows = land_mask.shape[0]
    h = HALO
    signed = (land_mask[None, None] * (2 * probe_signs - 1)).astype(jnp.bfloat16)
    exchanged = lax.all_to_all(signed, "trait", split_axis=0, concat_axis=1, tiled=True)
    field_ext = halo_rows(exchanged, h).astype(jnp.float32)
    kappa_ext = halo_rows(kappa_sq, h)
    land_ext = field_ext[0, 0] * field_ext[0, 0]
    variances = jnp.diagonal(trait_covariance)
    z = field_ext * variances[None, :, None, None]

    def mix(x):
        return jnp.einsum("ts,psrc->ptrc", trait_covariance, x, precision=lax.Precision.HIGHEST)

    def stencil(x, off):
        r = x.shape[2]
        return land_ext[off + 1 : off + r - 1] * nine_valid(x, kappa_ext[off + 1 : off + r - 1])

    def apply_a(x, off):
        return mix(stencil(stencil(x, off), off + 1))

    def a_stages(x, off):
        return (lambda _: stencil(x, off), lambda first: mix(stencil(first, off + 1)))

    def own(x, off):
        return x[:, :, h - off : h - off + rows]

    def crop(x, k):
        return x[:, :, k : x.shape[2] - k]

    def reduce_tile(pairs, off, work=()):
        prods = jnp.stack([own(a, off) * own(b, off) for a, b in pairs], axis=-1)
        return butterfly_sum(jnp.sum(prods, axis=(1, 2, 3)), "tile", work)

    az = apply_a(z, 0)
    z2 = crop(z, 2)
    sums, aaz = reduce_tile([(z2, z2), (az, z2)], 2, a_stages(az, 2))
    norm = jnp.sqrt(sums[:, 0] + epsilon)
    alpha = sums[:, 1] / (norm * norm)
    q = z2 / norm[:, None, None, None]
    aq = az / norm[:, None, None, None]
    w = aq - alpha[:, None, None, None] * q
    aw = aaz / norm[:, None, None, None] - alpha[:, None, None, None] * crop(aq, 2)
    aq = crop(aq, 2)
    q = crop(q, 2)
    w = crop(w, 2)
    off = 4
    alphas = [alpha]
    betas = []
    iters = 3
    for step in range(1, iters):
        last_step = step == iters - 1
        sums, aaw = reduce_tile([(w, w), (aw, w), (q, w)], off, () if last_step else a_stages(aw, off))
        beta = jnp.sqrt(sums[:, 0] + epsilon)
        alpha = sums[:, 1] / (beta * beta) - sums[:, 2]
        q_next = w / beta[:, None, None, None]
        w_next = aw / beta[:, None, None, None] - beta[:, None, None, None] * q - alpha[:, None, None, None] * q_next
        if not last_step:
            aw_next = (
                aaw / beta[:, None, None, None]
                - beta[:, None, None, None] * crop(aq, 2)
                - alpha[:, None, None, None] * crop(aw, 2) / beta[:, None, None, None]
            )
            aq = crop(aw, 2) / beta[:, None, None, None]
            q = crop(q_next, 2)
            w = crop(w_next, 2)
            aw = aw_next
            off += 2
        else:
            q = q_next
            w = w_next
        betas.append(beta)
        alphas.append(alpha)
    w_own = own(w, off)
    w_back = lax.all_to_all(w_own, "trait", split_axis=1, concat_axis=0, tiled=True)
    partial = jnp.sum(w_own * w_own, axis=(1, 2, 3))[:, None]
    first = (lax.axis_index("tile") == 0).astype(jnp.float32)
    known = jnp.concatenate([jnp.stack(alphas, axis=1), jnp.stack(betas, axis=1)], axis=1)
    mine = jnp.concatenate([known * first, partial, norm[:, None] * first], axis=1)
    probes_local = mine.shape[0]
    n_trait = lax.axis_size("trait")
    spread = lax.dynamic_update_slice(
        jnp.zeros((probes_local * n_trait, mine.shape[1]), jnp.float32),
        mine,
        (lax.axis_index("trait") * probes_local, 0),
    )
    scalars = butterfly_sum(butterfly_sum(spread, "tile")[0], "trait")[0]
    beta = jnp.sqrt(scalars[:, 2 * iters - 1] + epsilon)
    norm_all = scalars[:, 2 * iters]
    last = (w_back / beta[:, None, None, None]) * norm_all[:, None, None, None]
    betas_all = jnp.concatenate([scalars[:, iters : 2 * iters - 1], beta[:, None]], axis=1)
    return scalars[:, :iters], betas_all, last


def solution(mesh):
    in_specs = (P(None, "trait", "tile", None), P("tile", None), P("tile", None), P())
    out_specs = (P(), P(), P(None, "trait", "tile", None))

    return jax.shard_map(shards, mesh=mesh, in_specs=in_specs, out_specs=out_specs, check_vma=False)
```

profile of v0, /device:TPU:0, one launch (start us, length us, event | category | flops | bytes accessed | tf_op | source)
XLA Modules:
  0.0 110.3 jit_solution(15179768525880213874)
XLA Ops:
  0.7 2.2 %multiply_convert_fusion = bf16[4,4,8,2048]{3,2,1,0:T(8,128)(2,1)} fusion(s32[4,4,8,2048]{3,2,1,0:T(8,128)} %param.4, s32[8,2048]{1,0:T(8,128)} %param.5), kind=kLoop, calls=%fused_computation.163 | loop fusion | flops 1048576 | bytes 1638400 | tf_op jit(solution)/shard_map/convert_element_type | solution.py:82
  2.9 5.2 %all-to-all-start = ((bf16[4,4,8,2048]{3,2,1,0:T(8,128)(2,1)}), bf16[4,4,8,2048]{3,2,1,0:T(8,128)(2,1)S(1)}, u32[]{:S(2)}, u32[]{:S(2)}) async-start(bf16[4,4,8,2048]{3,2,1,0:T(8,128)(2,1)} %multiply_convert_fusion), calls=%async_computation | async-start | bytes 1048576 | tf_op jit(solution)/shard_map/all_to_all | solution.py:83
  10.4 5.6 %all-to-all-done = bf16[4,4,8,2048]{3,2,1,0:T(8,128)(2,1)S(1)} async-done(((bf16[4,4,8,2048]{3,2,1,0:T(8,128)(2,1)}), bf16[4,4,8,2048]{3,2,1,0:T(8,128)(2,1)S(1)}, u32[]{:S(2)}, u32[]{:S(2)}) %all-to-all-start) | async-done | bytes 524320 | tf_op jit(solution)/shard_map/all_to_all | solution.py:83
  17.2 3.0 %collective-permute-start = (bf16[1,16,6,2048]{3,1,2,0:T(8,128)(2,1)S(1)}, bf16[1,16,6,2048]{3,1,2,0:T(8,128)(2,1)S(1)}, u32[]{:S(2)}, u32[]{:S(2)}) collective-permute-start(bf16[1,16,6,2048]{3,1,2,0:T(8,128)(2,1)S(1)} %get-tuple-element.38), channel_id=1, source_target_pairs={{0,1},{2,3},{4,5},{6,7},{1,0},{3,2},{5,4},{7,6},{8,9},{10,11},{12,... | collective-permute-start | bytes 1179656 | tf_op jit(solution)/shard_map/ppermute | solution.py:73
  22.7 4.4 %fusion.5 = f32[1,16,18,2048]{3,1,2,0:T(8,128)S(1)} fusion(f32[1,16,20,2048]{3,1,2,0:T(8,128)S(1)} %broadcast_multiply_fusion, f32[18,2048]{1,0:T(8,128)S(1)} %slice_add_fusion.4, f32[18,2048]{1,0:T(8,128)S(1)} %bitcast.83), kind=kLoop, calls=%fused_computation.17 | loop fusion | flops 7667712 | bytes 12451840 | tf_op jit(solution)/shard_map/mul | solution.py:95
  27.1 5.6 %convolution_bitcast_fusion = f32[1,16,16,2048]{3,1,2,0:T(8,128)S(1)} fusion(f32[1,16,18,2048]{3,1,2,0:T(8,128)S(1)} %fusion.5, f32[16,2048]{1,0:T(8,128)S(1)} %slice_add_fusion.8, f32[16,2048]{1,0:T(8,128)S(1)} %bitcast.87, f32[16,16]{1,0:T(8,128)S(1)} %copy-done), kind=kOutput, calls=%fused_computation.3 | convolution fusion | flops 107479040 | bytes 11018240 | tf_op jit(solution)/shard_map/ts,psrc->ptrc/dot_general | solution.py:91
  33.3 5.7 %collective-permute-start.6 = (f32[1,2]{1,0:T(1,128)S(1)}, f32[1,2]{1,0:T(1,128)S(1)}, u32[]{:S(2)}, u32[]{:S(2)}) collective-permute-start(f32[1,2]{1,0:T(1,128)S(1)} %bitcast.90), channel_id=1, source_target_pairs={{0,1},{1,0},{2,3},{3,2},{4,5},{5,4},{6,7},{7,6},{8,9},{9,8},{10,11... | collective-permute-start | bytes 32 | tf_op jit(solution)/shard_map/ppermute | solution.py:40
  39.1 3.5 %fusion.33 = f32[1,16,14,2048]{3,1,2,0:T(8,128)S(1)} fusion(f32[1,16,16,2048]{3,1,2,0:T(8,128)S(1)} %convolution_bitcast_fusion, f32[14,2048]{1,0:T(8,128)S(1)} %slice_add_fusion.7, f32[14,2048]{1,0:T(8,128)S(1)} %bitcast.85), kind=kLoop, calls=%fused_computation.60 | loop fusion | flops 5963776 | bytes 9699328 | tf_op jit(solution)/shard_map/mul | solution.py:95
  42.7 2.1 %collective-permute-start.7 = (f32[1,2]{1,0:T(1,128)S(1)}, f32[1,2]{1,0:T(1,128)S(1)}, u32[]{:S(2)}, u32[]{:S(2)}) collective-permute-start(f32[1,2]{1,0:T(1,128)S(1)} %bitcast_add_fusion.2), channel_id=1, source_target_pairs={{0,2},{1,3},{2,0},{3,1},{4,6},{5,7},{6,4},{7,5},{8,10},{9,11},{10,... | collective-permute-start | bytes 32 | tf_op jit(solution)/shard_map/ppermute | solution.py:40
  44.8 4.3 %convolution_bitcast_fusion.1 = f32[1,16,12,2048]{3,1,2,0:T(8,128)S(1)} fusion(f32[1,16,14,2048]{3,1,2,0:T(8,128)S(1)} %fusion.33, f32[12,2048]{1,0:T(8,128)S(1)} %slice_add_fusion.6, f32[12,2048]{1,0:T(8,128)S(1)} %bitcast.86, f32[16,16]{1,0:T(8,128)S(1)} %copy-done), kind=kOutput, calls=%fused_computation.4 | convolution fusion | flops 80609280 | bytes 8396800 | tf_op jit(solution)/shard_map/ts,psrc->ptrc/dot_general | solution.py:91
  49.1 2.2 %collective-permute-start.8 = (f32[1,2]{1,0:T(1,128)S(1)}, f32[1,2]{1,0:T(1,128)S(1)}, u32[]{:S(2)}, u32[]{:S(2)}) collective-permute-start(f32[1,2]{1,0:T(1,128)S(1)} %add.241), channel_id=1, source_target_pairs={{0,4},{1,5},{2,6},{3,7},{4,0},{5,1},{6,2},{7,3},{8,12},{9,13},{10,... | collective-permute-start | bytes 32 | tf_op jit(solution)/shard_map/ppermute | solution.py:40
  51.3 2.3 %collective-permute-done.8 = f32[1,2]{1,0:T(1,128)S(1)} collective-permute-done((f32[1,2]{1,0:T(1,128)S(1)}, f32[1,2]{1,0:T(1,128)S(1)}, u32[]{:S(2)}, u32[]{:S(2)}) %collective-permute-start.8) | collective-permute-done | bytes 40 | tf_op jit(solution)/shard_map/ppermute | solution.py:40
  57.4 2.1 %fusion.65 = f32[1,16,10,2048]{3,1,2,0:T(8,128)S(1)} fusion(f32[1,16,12,2048]{3,1,2,0:T(8,128)S(1)} %fusion.53, f32[10,2048]{1,0:T(8,128)S(1)} %slice_add_fusion.5, f32[10,2048]{1,0:T(8,128)S(1)} %bitcast.84), kind=kLoop, calls=%fused_computation.105 | loop fusion | flops 4259840 | bytes 7077888 | tf_op jit(solution)/shard_map/mul | solution.py:95
  59.7 2.5 %convolution_bitcast_fusion.2 = f32[1,16,8,2048]{3,1,2,0:T(8,128)S(1)} fusion(f32[1,16,10,2048]{3,1,2,0:T(8,128)S(1)} %fusion.65, f32[8,2048]{1,0:T(8,128)S(1)} %broadcast_add_fusion, f32[8,2048]{1,0:T(8,128)S(1)} %bitcast.88, f32[16,16]{1,0:T(8,128)S(1)} %copy-done), kind=kOutput, calls=%fused_computation.5 | convolution fusion | flops 53739520 | bytes 5644288 | tf_op jit(solution)/shard_map/ts,psrc->ptrc/dot_general | solution.py:91
  63.1 2.1 %collective-permute-start.11 = (f32[1,3]{1,0:T(1,128)S(1)}, f32[1,3]{1,0:T(1,128)S(1)}, u32[]{:S(2)}, u32[]{:S(2)}) collective-permute-start(f32[1,3]{1,0:T(1,128)S(1)} %add.257), channel_id=1, source_target_pairs={{0,4},{1,5},{2,6},{3,7},{4,0},{5,1},{6,2},{7,3},{8,12},{9,13},{10,... | collective-permute-start | bytes 44 | tf_op jit(solution)/shard_map/ppermute | solution.py:40
  65.2 2.3 %collective-permute-done.11 = f32[1,3]{1,0:T(1,128)S(1)} collective-permute-done((f32[1,3]{1,0:T(1,128)S(1)}, f32[1,3]{1,0:T(1,128)S(1)}, u32[]{:S(2)}, u32[]{:S(2)}) %collective-permute-start.11) | collective-permute-done | bytes 44 | tf_op jit(solution)/shard_map/ppermute | solution.py:40
  71.7 1.1 %collective-permute-done.12 = f32[1,3]{1,0:T(1,128)S(1)} collective-permute-done((f32[1,3]{1,0:T(1,128)S(1)}, f32[1,3]{1,0:T(1,128)S(1)}, u32[]{:S(2)}, u32[]{:S(2)}) %collective-permute-start.12) | collective-permute-done | bytes 44 | tf_op jit(solution)/shard_map/ppermute | solution.py:40
  73.9 2.5 %collective-permute-done.13 = f32[1,3]{1,0:T(1,128)S(1)} collective-permute-done((f32[1,3]{1,0:T(1,128)S(1)}, f32[1,3]{1,0:T(1,128)S(1)}, u32[]{:S(2)}, u32[]{:S(2)}) %collective-permute-start.13) | collective-permute-done | bytes 44 | tf_op jit(solution)/shard_map/ppermute | solution.py:40
  76.4 2.1 %collective-permute-start.14 = (f32[1,3]{1,0:T(1,128)S(1)}, f32[1,3]{1,0:T(1,128)S(1)}, u32[]{:S(2)}, u32[]{:S(2)}) collective-permute-start(f32[1,3]{1,0:T(1,128)S(1)} %add.267), channel_id=1, source_target_pairs={{0,4},{1,5},{2,6},{3,7},{4,0},{5,1},{6,2},{7,3},{8,12},{9,13},{10,... | collective-permute-start | bytes 44 | tf_op jit(solution)/shard_map/ppermute | solution.py:40
  78.6 2.3 %collective-permute-done.14 = f32[1,3]{1,0:T(1,128)S(1)} collective-permute-done((f32[1,3]{1,0:T(1,128)S(1)}, f32[1,3]{1,0:T(1,128)S(1)}, u32[]{:S(2)}, u32[]{:S(2)}) %collective-permute-start.14) | collective-permute-done | bytes 44 | tf_op jit(solution)/shard_map/ppermute | solution.py:40
  84.3 1.6 %copy.12 = f32[1,16,8,2048]{3,2,0,1:T(8,128)} copy(f32[1,16,8,2048]{3,1,2,0:T(8,128)S(1)} %get-tuple-element.22) | data formatting | bytes 2097152 | tf_op jit(solution)/shard_map/sub | solution.py:135
  85.9 4.2 %all-to-all-start.1 = ((f32[1,16,8,2048]{3,2,0,1:T(8,128)}), f32[1,16,8,2048]{3,2,0,1:T(8,128)S(1)}, u32[]{:S(2)}, u32[]{:S(2)}) async-start(f32[1,16,8,2048]{3,2,0,1:T(8,128)} %copy.12), calls=%async_computation.1 | async-start | bytes 2097152 | tf_op jit(solution)/shard_map/all_to_all | solution.py:153
  91.0 1.1 %collective-permute-done.15 = f32[4,7]{1,0:T(4,128)S(1)} collective-permute-done((f32[4,7]{1,0:T(4,128)S(1)}, f32[4,7]{1,0:T(4,128)S(1)}, u32[]{:S(2)}, u32[]{:S(2)}) %collective-permute-start.15) | collective-permute-done | bytes 144 | tf_op jit(solution)/shard_map/ppermute | solution.py:40
  92.9 1.1 %collective-permute-start.16 = (f32[4,7]{1,0:T(4,128)S(1)}, f32[4,7]{1,0:T(4,128)S(1)}, u32[]{:S(2)}, u32[]{:S(2)}) collective-permute-start(f32[4,7]{1,0:T(4,128)S(1)} %add.271), channel_id=1, source_target_pairs={{0,2},{1,3},{2,0},{3,1},{4,6},{5,7},{6,4},{7,5},{8,10},{9,11},{10,... | collective-permute-start | bytes 344 | tf_op jit(solution)/shard_map/ppermute | solution.py:40
  94.0 2.5 %collective-permute-done.16 = f32[4,7]{1,0:T(4,128)S(1)} collective-permute-done((f32[4,7]{1,0:T(4,128)S(1)}, f32[4,7]{1,0:T(4,128)S(1)}, u32[]{:S(2)}, u32[]{:S(2)}) %collective-permute-start.16) | collective-permute-done | bytes 144 | tf_op jit(solution)/shard_map/ppermute | solution.py:40
  96.5 2.1 %collective-permute-start.17 = (f32[4,7]{1,0:T(4,128)S(1)}, f32[4,7]{1,0:T(4,128)S(1)}, u32[]{:S(2)}, u32[]{:S(2)}) collective-permute-start(f32[4,7]{1,0:T(4,128)S(1)} %add.272), channel_id=1, source_target_pairs={{0,4},{1,5},{2,6},{3,7},{4,0},{5,1},{6,2},{7,3},{8,12},{9,13},{10,... | collective-permute-start | bytes 344 | tf_op jit(solution)/shard_map/ppermute | solution.py:40
  98.6 2.4 %collective-permute-done.17 = f32[4,7]{1,0:T(4,128)S(1)} collective-permute-done((f32[4,7]{1,0:T(4,128)S(1)}, f32[4,7]{1,0:T(4,128)S(1)}, u32[]{:S(2)}, u32[]{:S(2)}) %collective-permute-start.17) | collective-permute-done | bytes 144 | tf_op jit(solution)/shard_map/ppermute | solution.py:40
  101.0 2.0 %collective-permute-start.18 = (f32[4,7]{1,0:T(4,128)S(1)}, f32[4,7]{1,0:T(4,128)S(1)}, u32[]{:S(2)}, u32[]{:S(2)}) collective-permute-start(f32[4,7]{1,0:T(4,128)S(1)} %add.273), channel_id=1, source_target_pairs={{0,8},{8,0},{16,24},{24,16},{1,9},{9,1},{17,25},{25,17},{2,10},{10... | collective-permute-start | bytes 344 | tf_op jit(solution)/shard_map/ppermute | solution.py:40
  103.0 1.6 %collective-permute-done.18 = f32[4,7]{1,0:T(4,128)S(1)} collective-permute-done((f32[4,7]{1,0:T(4,128)S(1)}, f32[4,7]{1,0:T(4,128)S(1)}, u32[]{:S(2)}, u32[]{:S(2)}) %collective-permute-start.18) | collective-permute-done | bytes 144 | tf_op jit(solution)/shard_map/ppermute | solution.py:40
  104.6 2.0 %collective-permute-start.19 = (f32[4,7]{1,0:T(4,128)S(1)}, f32[4,7]{1,0:T(4,128)S(1)}, u32[]{:S(2)}, u32[]{:S(2)}) collective-permute-start(f32[4,7]{1,0:T(4,128)S(1)} %add.274), channel_id=1, source_target_pairs={{0,16},{8,24},{16,0},{24,8},{1,17},{9,25},{17,1},{25,9},{2,18},{10... | collective-permute-start | bytes 344 | tf_op jit(solution)/shard_map/ppermute | solution.py:40
  106.6 1.6 %collective-permute-done.19 = f32[4,7]{1,0:T(4,128)S(1)} collective-permute-done((f32[4,7]{1,0:T(4,128)S(1)}, f32[4,7]{1,0:T(4,128)S(1)}, u32[]{:S(2)}, u32[]{:S(2)}) %collective-permute-start.19) | collective-permute-done | bytes 144 | tf_op jit(solution)/shard_map/ppermute | solution.py:40
  109.1 1.2 %divide_multiply_fusion = f32[4,4,8,2048]{3,2,1,0:T(8,128)} fusion(f32[4,4,8,2048]{3,2,1,0:T(8,128)S(1)} %bitcast.81, f32[4]{0:T(128)S(1)} %get-tuple-element.20, f32[4]{0:T(128)S(1)} %get-tuple-element.19), kind=kLoop, calls=%fused_computation.142 | loop fusion | flops 524288 | bytes 2097184 | tf_op jit(solution)/shard_map/mul | solution.py:168
  (104 shorter events, 17.1 us)
Async XLA Ops:
  0.6 8.9 %copy-start = (f32[16,16]{1,0:T(8,128)S(1)}, f32[16,16]{1,0:T(8,128)}, u32[]{:S(2)}) copy-start(f32[16,16]{1,0:T(8,128)} %param.7) | copy-start | bytes 3076
  0.6 7.4 %copy-start.2 = (f32[8,2048]{1,0:T(8,128)S(1)}, f32[8,2048]{1,0:T(8,128)}, u32[]{:S(2)}) copy-start(f32[8,2048]{1,0:T(8,128)} %param.6) | copy-start | bytes 196612
  2.9 13.2 %all-to-all-start = ((bf16[4,4,8,2048]{3,2,1,0:T(8,128)(2,1)}), bf16[4,4,8,2048]{3,2,1,0:T(8,128)(2,1)S(1)}, u32[]{:S(2)}, u32[]{:S(2)}) async-start(bf16[4,4,8,2048]{3,2,1,0:T(8,128)(2,1)} %multiply_convert_fusion), calls=%async_computation | async-start | bytes 1048576 | tf_op jit(solution)/shard_map/all_to_all | solution.py:83
  8.1 2.2 %collective-permute-start.3 = (f32[6,2048]{1,0:T(8,128)S(1)}, f32[6,2048]{1,0:T(8,128)S(1)}, u32[]{:S(2)}, u32[]{:S(2)}) collective-permute-start(f32[6,2048]{1,0:T(8,128)S(1)} %get-tuple-element.47), channel_id=1, source_target_pairs={{0,1},{2,3},{4,5},{6,7},{1,0},{3,2},{5,4},{7,6},{8,9},{10,11},{12,... | collective-permute-start | bytes 147464 | tf_op jit(solution)/shard_map/ppermute | solution.py:73
  8.2 2.0 %collective-permute-start.5 = (f32[3,2048]{1,0:T(4,128)S(1)}, f32[3,2048]{1,0:T(4,128)S(1)}, u32[]{:S(2)}, u32[]{:S(2)}) collective-permute-start(f32[3,2048]{1,0:T(4,128)S(1)} %get-tuple-element.45), channel_id=1, source_target_pairs={{1,2},{3,4},{5,6},{2,1},{4,3},{6,5},{9,10},{11,12},{13,14},{10,9},... | collective-permute-start | bytes 73736 | tf_op jit(solution)/shard_map/ppermute | solution.py:68
  8.9 1.4 %collective-permute-start.4 = (f32[3,2048]{1,0:T(4,128)S(1)}, f32[3,2048]{1,0:T(4,128)S(1)}, u32[]{:S(2)}, u32[]{:S(2)}) collective-permute-start(f32[3,2048]{1,0:T(4,128)S(1)} %get-tuple-element.44), channel_id=1, source_target_pairs={{1,2},{3,4},{5,6},{2,1},{4,3},{6,5},{9,10},{11,12},{13,14},{10,9},... | collective-permute-start | bytes 73736 | tf_op jit(solution)/shard_map/ppermute | solution.py:68
  16.5 4.4 %collective-permute-start.1 = (bf16[1,16,3,2048]{3,1,2,0:T(8,128)(2,1)S(1)}, bf16[1,16,3,2048]{3,1,2,0:T(8,128)(2,1)S(1)}, u32[]{:S(2)}, u32[]{:S(2)}) collective-permute-start(bf16[1,16,3,2048]{3,1,2,0:T(8,128)(2,1)S(1)} %get-tuple-element.41), channel_id=1, source_target_pairs={{1,2},{3,4},{5,6},{2,1},{4,3},{6,5},{9,10},{11,12},{13,14},{10,9},... | collective-permute-start | bytes 589832 | tf_op jit(solution)/shard_map/ppermute | solution.py:68
  17.2 4.4 %collective-permute-start = (bf16[1,16,6,2048]{3,1,2,0:T(8,128)(2,1)S(1)}, bf16[1,16,6,2048]{3,1,2,0:T(8,128)(2,1)S(1)}, u32[]{:S(2)}, u32[]{:S(2)}) collective-permute-start(bf16[1,16,6,2048]{3,1,2,0:T(8,128)(2,1)S(1)} %get-tuple-element.38), channel_id=1, source_target_pairs={{0,1},{2,3},{4,5},{6,7},{1,0},{3,2},{5,4},{7,6},{8,9},{10,11},{12,... | collective-permute-start | bytes 1179656 | tf_op jit(solution)/shard_map/ppermute | solution.py:73
  20.2 0.7 collective-permute-start.2
  21.9 0.7 copy-start.1
  32.8 6.1 %slice-start = ((f32[1,1,20,2048]{3,1,2,0:T(1,128)}), f32[1,1,14,2048]{3,1,2,0:T(1,128)S(1)}, s32[]{:S(2)}) async-start(f32[1,1,20,2048]{3,1,2,0:T(1,128)} %copy-done.1), calls=%async_computation.2 | async-start | bytes 229376 | tf_op jit(solution)/shard_map/slice | solution.py:95
  32.9 6.1 %slice-start.1 = ((f32[1,1,20,2048]{3,1,2,0:T(1,128)}), f32[1,1,12,2048]{3,1,2,0:T(1,128)S(1)}, s32[]{:S(2)}) async-start(f32[1,1,20,2048]{3,1,2,0:T(1,128)} %copy-done.1), calls=%async_computation.3 | async-start | bytes 196608 | tf_op jit(solution)/shard_map/slice | solution.py:95
  32.9 6.2 %slice-start.2 = ((f32[1,1,20,2048]{3,1,2,0:T(1,128)}), f32[1,1,10,2048]{3,1,2,0:T(1,128)S(1)}, s32[]{:S(2)}) async-start(f32[1,1,20,2048]{3,1,2,0:T(1,128)} %copy-done.1), calls=%async_computation.4 | async-start | bytes 163840 | tf_op jit(solution)/shard_map/slice | solution.py:95
  32.9 6.2 %slice-start.3 = ((f32[1,1,20,2048]{3,1,2,0:T(1,128)}), f32[1,1,8,2048]{3,1,2,0:T(1,128)S(1)}, s32[]{:S(2)}) async-start(f32[1,1,20,2048]{3,1,2,0:T(1,128)} %copy-done.1), calls=%async_computation.5 | async-start | bytes 131072 | tf_op jit(solution)/shard_map/slice | solution.py:95
  33.3 9.4 %collective-permute-start.6 = (f32[1,2]{1,0:T(1,128)S(1)}, f32[1,2]{1,0:T(1,128)S(1)}, u32[]{:S(2)}, u32[]{:S(2)}) collective-permute-start(f32[1,2]{1,0:T(1,128)S(1)} %bitcast.90), channel_id=1, source_target_pairs={{0,1},{1,0},{2,3},{3,2},{4,5},{5,4},{6,7},{7,6},{8,9},{9,8},{10,11... | collective-permute-start | bytes 32 | tf_op jit(solution)/shard_map/ppermute | solution.py:40
  42.7 6.4 %collective-permute-start.7 = (f32[1,2]{1,0:T(1,128)S(1)}, f32[1,2]{1,0:T(1,128)S(1)}, u32[]{:S(2)}, u32[]{:S(2)}) collective-permute-start(f32[1,2]{1,0:T(1,128)S(1)} %bitcast_add_fusion.2), channel_id=1, source_target_pairs={{0,2},{1,3},{2,0},{3,1},{4,6},{5,7},{6,4},{7,5},{8,10},{9,11},{10,... | collective-permute-start | bytes 32 | tf_op jit(solution)/shard_map/ppermute | solution.py:40
  49.1 4.5 %collective-permute-start.8 = (f32[1,2]{1,0:T(1,128)S(1)}, f32[1,2]{1,0:T(1,128)S(1)}, u32[]{:S(2)}, u32[]{:S(2)}) collective-permute-start(f32[1,2]{1,0:T(1,128)S(1)} %add.241), channel_id=1, source_target_pairs={{0,4},{1,5},{2,6},{3,7},{4,0},{5,1},{6,2},{7,3},{8,12},{9,13},{10,... | collective-permute-start | bytes 32 | tf_op jit(solution)/shard_map/ppermute | solution.py:40
  57.3 2.1 %collective-permute-start.9 = (f32[1,3]{1,0:T(1,128)S(1)}, f32[1,3]{1,0:T(1,128)S(1)}, u32[]{:S(2)}, u32[]{:S(2)}) collective-permute-start(f32[1,3]{1,0:T(1,128)S(1)} %bitcast.91), channel_id=1, source_target_pairs={{0,1},{1,0},{2,3},{3,2},{4,5},{5,4},{6,7},{7,6},{8,9},{9,8},{10,11... | collective-permute-start | bytes 44 | tf_op jit(solution)/shard_map/ppermute | solution.py:40
  59.5 3.6 %collective-permute-start.10 = (f32[1,3]{1,0:T(1,128)S(1)}, f32[1,3]{1,0:T(1,128)S(1)}, u32[]{:S(2)}, u32[]{:S(2)}) collective-permute-start(f32[1,3]{1,0:T(1,128)S(1)} %bitcast_add_fusion.1), channel_id=1, source_target_pairs={{0,2},{1,3},{2,0},{3,1},{4,6},{5,7},{6,4},{7,5},{8,10},{9,11},{10,... | collective-permute-start | bytes 44 | tf_op jit(solution)/shard_map/ppermute | solution.py:40
  63.1 4.5 %collective-permute-start.11 = (f32[1,3]{1,0:T(1,128)S(1)}, f32[1,3]{1,0:T(1,128)S(1)}, u32[]{:S(2)}, u32[]{:S(2)}) collective-permute-start(f32[1,3]{1,0:T(1,128)S(1)} %add.257), channel_id=1, source_target_pairs={{0,4},{1,5},{2,6},{3,7},{4,0},{5,1},{6,2},{7,3},{8,12},{9,13},{10,... | collective-permute-start | bytes 44 | tf_op jit(solution)/shard_map/ppermute | solution.py:40
  71.7 1.2 %collective-permute-start.12 = (f32[1,3]{1,0:T(1,128)S(1)}, f32[1,3]{1,0:T(1,128)S(1)}, u32[]{:S(2)}, u32[]{:S(2)}) collective-permute-start(f32[1,3]{1,0:T(1,128)S(1)} %bitcast.92), channel_id=1, source_target_pairs={{0,1},{1,0},{2,3},{3,2},{4,5},{5,4},{6,7},{7,6},{8,9},{9,8},{10,11... | collective-permute-start | bytes 44 | tf_op jit(solution)/shard_map/ppermute | solution.py:40
  72.9 3.6 %collective-permute-start.13 = (f32[1,3]{1,0:T(1,128)S(1)}, f32[1,3]{1,0:T(1,128)S(1)}, u32[]{:S(2)}, u32[]{:S(2)}) collective-permute-start(f32[1,3]{1,0:T(1,128)S(1)} %bitcast_add_fusion), channel_id=1, source_target_pairs={{0,2},{1,3},{2,0},{3,1},{4,6},{5,7},{6,4},{7,5},{8,10},{9,11},{10,... | collective-permute-start | bytes 44 | tf_op jit(solution)/shard_map/ppermute | solution.py:40
  76.4 4.5 %collective-permute-start.14 = (f32[1,3]{1,0:T(1,128)S(1)}, f32[1,3]{1,0:T(1,128)S(1)}, u32[]{:S(2)}, u32[]{:S(2)}) collective-permute-start(f32[1,3]{1,0:T(1,128)S(1)} %add.267), channel_id=1, source_target_pairs={{0,4},{1,5},{2,6},{3,7},{4,0},{5,1},{6,2},{7,3},{8,12},{9,13},{10,... | collective-permute-start | bytes 44 | tf_op jit(solution)/shard_map/ppermute | solution.py:40
  85.9 23.2 %all-to-all-start.1 = ((f32[1,16,8,2048]{3,2,0,1:T(8,128)}), f32[1,16,8,2048]{3,2,0,1:T(8,128)S(1)}, u32[]{:S(2)}, u32[]{:S(2)}) async-start(f32[1,16,8,2048]{3,2,0,1:T(8,128)} %copy.12), calls=%async_computation.1 | async-start | bytes 2097152 | tf_op jit(solution)/shard_map/all_to_all | solution.py:153
  90.9 1.2 %collective-permute-start.15 = (f32[4,7]{1,0:T(4,128)S(1)}, f32[4,7]{1,0:T(4,128)S(1)}, u32[]{:S(2)}, u32[]{:S(2)}) collective-permute-start(f32[4,7]{1,0:T(4,128)S(1)} %dynamic_update_slice.5), channel_id=1, source_target_pairs={{0,1},{1,0},{2,3},{3,2},{4,5},{5,4},{6,7},{7,6},{8,9},{9,8},{10,11... | collective-permute-start | bytes 344 | tf_op jit(solution)/shard_map/ppermute | solution.py:40
  92.9 3.6 %collective-permute-start.16 = (f32[4,7]{1,0:T(4,128)S(1)}, f32[4,7]{1,0:T(4,128)S(1)}, u32[]{:S(2)}, u32[]{:S(2)}) collective-permute-start(f32[4,7]{1,0:T(4,128)S(1)} %add.271), channel_id=1, source_target_pairs={{0,2},{1,3},{2,0},{3,1},{4,6},{5,7},{6,4},{7,5},{8,10},{9,11},{10,... | collective-permute-start | bytes 344 | tf_op jit(solution)/shard_map/ppermute | solution.py:40
  96.5 4.5 %collective-permute-start.17 = (f32[4,7]{1,0:T(4,128)S(1)}, f32[4,7]{1,0:T(4,128)S(1)}, u32[]{:S(2)}, u32[]{:S(2)}) collective-permute-start(f32[4,7]{1,0:T(4,128)S(1)} %add.272), channel_id=1, source_target_pairs={{0,4},{1,5},{2,6},{3,7},{4,0},{5,1},{6,2},{7,3},{8,12},{9,13},{10,... | collective-permute-start | bytes 344 | tf_op jit(solution)/shard_map/ppermute | solution.py:40
  101.0 3.6 %collective-permute-start.18 = (f32[4,7]{1,0:T(4,128)S(1)}, f32[4,7]{1,0:T(4,128)S(1)}, u32[]{:S(2)}, u32[]{:S(2)}) collective-permute-start(f32[4,7]{1,0:T(4,128)S(1)} %add.273), channel_id=1, source_target_pairs={{0,8},{8,0},{16,24},{24,16},{1,9},{9,1},{17,25},{25,17},{2,10},{10... | collective-permute-start | bytes 344 | tf_op jit(solution)/shard_map/ppermute | solution.py:40
  104.6 3.6 %collective-permute-start.19 = (f32[4,7]{1,0:T(4,128)S(1)}, f32[4,7]{1,0:T(4,128)S(1)}, u32[]{:S(2)}, u32[]{:S(2)}) collective-permute-start(f32[4,7]{1,0:T(4,128)S(1)} %add.274), channel_id=1, source_target_pairs={{0,16},{8,24},{16,0},{24,8},{1,17},{9,25},{17,1},{25,9},{2,18},{10... | collective-permute-start | bytes 344 | tf_op jit(solution)/shard_map/ppermute | solution.py:40
  108.2 2.2 %copy-start.3 = (f32[4,7]{1,0:T(4,128)}, f32[4,7]{1,0:T(4,128)S(1)}, u32[]{:S(2)}) copy-start(f32[4,7]{1,0:T(4,128)S(1)} %add.275) | copy-start | bytes 340
where the time goes:
time: 111 us; the launch traced here: 110 us
  starting transfers between devices  38 us (34%)
  waiting for transfers between devices  27 us (24%)
  other arithmetic  21 us (19%)
  matrix products  12.4 us (11%)
  between operations  6.47 us (6%)
  local copies, waits for them, and re-layouts  5.4 us (5%)
    ppermute x14, starting transfers between devices, butterfly_sum(): got = lax.ppermute(v, axis, [(i, i ^ s) for i in range(n)])  22.9 us
    ppermute x14, waiting for transfers between devices, butterfly_sum(): got = lax.ppermute(v, axis, [(i, i ^ s) for i in range(n)])  20.8 us
    dot_general x3, matrix products, mix(): jnp.einsum('ts,psrc->ptrc', trait_covariance, x, precision=lax.Precision....  12.4 us
    mul x3, other arithmetic, stencil(): land_ext[off + 1:off + r - 1]  9.99 us
    all_to_all x1, waiting for transfers between devices, shards(): lax.all_to_all(signed, 'trait', split_axis=0, concat_axis=1, tiled=True)  5.64 us
    all_to_all x1, starting transfers between devices, shards(): lax.all_to_all(signed, 'trait', split_axis=0, concat_axis=1, tiled=True)  5.19 us
    all_to_all x1, starting transfers between devices, shards(): lax.all_to_all(w_own, 'trait', split_axis=1, concat_axis=0, tiled=True)  4.19 us
    ppermute x2, starting transfers between devices, halo_rows(): got_within = lax.ppermute(jnp.where(odd, top, bottom), 'tile', within)  3.07 us
  transfers between devices with their start and end apart: 22, of which 13 were waited for; matrix products, arithmetic and copies ran while one was open for 14% of the time, Pallas kernels for 0%

commit v1 on v0

--- a/solution.py
+++ b/solution.py
@@ -60,16 +60,7 @@
     odd = lax.axis_index("tile") % 2 == 1
     across = [(i, i + 1) for i in range(1, n - 1, 2)] + [(i + 1, i) for i in range(1, n - 1, 2)]
     within = [(i, i + 1) for i in range(0, n - 1, 2)] + [(i + 1, i) for i in range(0, n - 1, 2)]
-    send = jnp.where(odd, bottom, top)
-    pieces = 2 if width % 2 == 0 else 1
-    step = width // pieces
-    got_across = jnp.concatenate(
-        [
-            lax.ppermute(lax.slice_in_dim(send, k * step, (k + 1) * step, axis=dim), "tile", across)
-            for k in range(pieces)
-        ],
-        axis=dim,
-    )
+    got_across = lax.ppermute(jnp.where(odd, bottom, top), "tile", across)
     got_within = lax.ppermute(jnp.where(odd, top, bottom), "tile", within)
     low = jnp.where(odd, got_within, got_across)
     high = jnp.where(odd, got_across, got_within)
@@ -110,9 +101,21 @@
         prods = jnp.stack([own(a, off) * own(b, off) for a, b in pairs], axis=-1)
         return butterfly_sum(jnp.sum(prods, axis=(1, 2, 3)), "tile", work)
 
-    az = apply_a(z, 0)
+    az_own = apply_a(z[:, :, h - 2 : h + rows + 2], h - 2)
+    zo = z[:, :, h : h + rows]
+
+    def az_rest(_):
+        low = apply_a(z[:, :, : h + 2], 0)
+        high = apply_a(z[:, :, h + rows - 2 :], h + rows - 2)
+        return jnp.concatenate([low, az_own, high], axis=2)
+
+    stages = (
+        az_rest,
+        lambda az: (az, stencil(az, 2)),
+        lambda got: (got[0], mix(stencil(got[1], 3))),
+    )
+    sums, (az, aaz) = reduce_tile([(zo, zo), (az_own, zo)], h, stages)
     z2 = crop(z, 2)
-    sums, aaz = reduce_tile([(z2, z2), (az, z2)], 2, a_stages(az, 2))
     norm = jnp.sqrt(sums[:, 0] + epsilon)
     alpha = sums[:, 1] / (norm * norm)
     q = z2 / norm[:, None, None, None]

time: 111 us -> 111 us (level)
  starting transfers between devices: 38 us -> 29 us
  waiting for transfers between devices: 27 us -> 35.7 us
    ppermute x14, waiting for transfers between devices: 20.8 us -> 28.4 us  [butterfly_sum(): got = lax.ppermute(v, axis, [(i, i ^ s) for i in range(n)])]
    ppermute x14, starting transfers between devices: 22.9 us -> 18.8 us  [butterfly_sum(): got = lax.ppermute(v, axis, [(i, i ^ s) for i in range(n)])]
    ppermute x2, starting transfers between devices: 3.07 us -> 0.14 us  [halo_rows(): got_within = lax.ppermute(jnp.where(odd, top, bottom), 'tile', within)]
    ppermute x4 -> x2, starting transfers between devices: 2.66 us -> 1.35 us  [halo_rows(): got_across = lax.ppermute(jnp.where(odd, bottom, top), 'tile', across)]
    dot_general x3 -> x5, matrix products: 12.4 us -> 11.9 us  [mix(): jnp.einsum('ts,psrc->ptrc', trait_covariance, x, precision=lax.Precision....]
    mul x3 -> x4, other arithmetic: 9.99 us -> 10.1 us  [stencil(): land_ext[off + 1:off + r - 1]]
  transfers between devices with their start and end apart: 22 -> 20, of which waited for: 13 -> 13; matrix products, arithmetic and copies ran while one was open for 14% -> 15% of each run, Pallas kernels for 0% -> 0%
where the time goes in v1:
time: 111 us; the launch traced here: 110 us
  waiting for transfers between devices  35.7 us (32%)
  starting transfers between devices  29 us (26%)
  other arithmetic  21.8 us (20%)
  matrix products  11.9 us (11%)
  between operations  6.45 us (6%)
  local copies, waits for them, and re-layouts  5.3 us (5%)
    ppermute x14, waiting for transfers between devices, butterfly_sum(): got = lax.ppermute(v, axis, [(i, i ^ s) for i in range(n)])  28.4 us
    ppermute x14, starting transfers between devices, butterfly_sum(): got = lax.ppermute(v, axis, [(i, i ^ s) for i in range(n)])  18.8 us
    dot_general x5, matrix products, mix(): jnp.einsum('ts,psrc->ptrc', trait_covariance, x, precision=lax.Precision....  11.9 us
    mul x4, other arithmetic, stencil(): land_ext[off + 1:off + r - 1]  10.1 us
    all_to_all x1, waiting for transfers between devices, shards(): lax.all_to_all(signed, 'trait', split_axis=0, concat_axis=1, tiled=True)  6.35 us
    all_to_all x1, starting transfers between devices, shards(): lax.all_to_all(signed, 'trait', split_axis=0, concat_axis=1, tiled=True)  5.19 us
    all_to_all x1, starting transfers between devices, shards(): lax.all_to_all(w_own, 'trait', split_axis=1, concat_axis=0, tiled=True)  3.52 us
  transfers between devices with their start and end apart: 20, of which 13 were waited for; matrix products, arithmetic and copies ran while one was open for 15% of the time, Pallas kernels for 0%

profile of v1, /device:TPU:0, one launch (start us, length us, event | category | flops | bytes accessed | tf_op | source)
XLA Modules:
  0.0 110.2 jit_solution(7858224212275999400)
XLA Ops:
  0.7 2.2 %multiply_convert_fusion = bf16[4,4,8,2048]{3,2,1,0:T(8,128)(2,1)} fusion(s32[4,4,8,2048]{3,2,1,0:T(8,128)} %param.4, s32[8,2048]{1,0:T(8,128)} %param.5), kind=kLoop, calls=%fused_computation.157 | loop fusion | flops 1048576 | bytes 1638400 | tf_op jit(solution)/shard_map/convert_element_type | solution.py:73
  2.9 5.2 %all-to-all-start = ((bf16[4,4,8,2048]{3,2,1,0:T(8,128)(2,1)}), bf16[4,4,8,2048]{3,2,1,0:T(8,128)(2,1)S(1)}, u32[]{:S(2)}, u32[]{:S(2)}) async-start(bf16[4,4,8,2048]{3,2,1,0:T(8,128)(2,1)} %multiply_convert_fusion), calls=%async_computation | async-start | bytes 1048576 | tf_op jit(solution)/shard_map/all_to_all | solution.py:74
  9.7 6.3 %all-to-all-done = bf16[4,4,8,2048]{3,2,1,0:T(8,128)(2,1)S(1)} async-done(((bf16[4,4,8,2048]{3,2,1,0:T(8,128)(2,1)}), bf16[4,4,8,2048]{3,2,1,0:T(8,128)(2,1)S(1)}, u32[]{:S(2)}, u32[]{:S(2)}) %all-to-all-start) | async-done | bytes 524320 | tf_op jit(solution)/shard_map/all_to_all | solution.py:74
  17.3 1.0 collective-permute-done
  19.4 2.1 %fusion.36 = f32[1,16,10,2048]{3,1,2,0:T(8,128)S(1)} fusion(f32[1,16,12,2048]{3,1,2,0:T(8,128)S(1)} %slice.639, f32[1,16,20,2048]{3,1,2,0:T(8,128)S(1)} %broadcast_multiply_fusion, f32[10,2048]{1,0:T(8,128)S(1)} %slice_add_fusion.9, f32[10,2048]{1,0:T(8,128)S(1)} %bitcast.103), kind=kLoop, calls=%fused_computation.71 | loop fusion | flops 4259840 | bytes 6979584 | tf_op jit(solution)/shard_map/mul | solution.py:86
  21.6 2.5 %convolution_bitcast_fusion.2 = f32[1,16,8,2048]{3,1,2,0:T(8,128)S(1)} fusion(f32[1,16,10,2048]{3,1,2,0:T(8,128)S(1)} %fusion.36, f32[8,2048]{1,0:T(8,128)S(1)} %broadcast_add_fusion, f32[8,2048]{1,0:T(8,128)S(1)} %bitcast.107, f32[16,16]{1,0:T(8,128)S(1)} %copy-done), kind=kOutput, calls=%fused_computation.5 | convolution fusion | flops 53739520 | bytes 5644288 | tf_op jit(solution)/shard_map/ts,psrc->ptrc/dot_general | solution.py:82
  25.1 7.9 %collective-permute-start.4 = (f32[1,2]{1,0:T(1,128)S(1)}, f32[1,2]{1,0:T(1,128)S(1)}, u32[]{:S(2)}, u32[]{:S(2)}) collective-permute-start(f32[1,2]{1,0:T(1,128)S(1)} %bitcast.110), channel_id=1, source_target_pairs={{0,1},{1,0},{2,3},{3,2},{4,5},{5,4},{6,7},{7,6},{8,9},{9,8},{10,11... | collective-permute-start | bytes 32 | tf_op jit(solution)/shard_map/ppermute | solution.py:40
  33.2 2.5 %fusion.100 = (f32[1,16,6,2048]{3,1,2,0:T(8,128)S(1)}, f32[1,16,6,2048]{3,1,2,0:T(8,128)S(1)}) fusion(f32[1,16,8,2048]{3,1,2,0:T(8,128)S(1)} %get-tuple-element.40, f32[1,16,20,2048]{3,1,2,0:T(8,128)S(1)} %broadcast_multiply_fusion, f32[6,2048]{1,0:T(8,128)S(1)} %get-tuple-element.58, f32[6,2048]{1,0:T(8,128)S(1)} %get-tuple-element.74, ...), kind=kLoop, calls=%fused_computation.175 | loop fusion | flops 5111808 | bytes 8585216 | tf_op jit(solution)/shard_map/mul | solution.py:86
  35.7 1.4 %convolution_bitcast_fusion.4 = f32[1,16,4,2048]{3,1,2,0:T(8,128)S(1)} fusion(f32[1,16,6,2048]{3,1,2,0:T(8,128)S(1)} %get-tuple-element.38, f32[4,2048]{1,0:T(4,128)S(1)} %get-tuple-element.72, f32[4,2048]{1,0:T(4,128)S(1)} %get-tuple-element.76, f32[16,16]{1,0:T(8,128)S(1)} %copy-done), kind=kOutput, calls=%fused_computation.7 | convolution fusion | flops 26869760 | bytes 2957312 | tf_op jit(solution)/shard_map/ts,psrc->ptrc/dot_general | solution.py:82
  37.1 1.4 %convolution_bitcast_fusion.3 = f32[1,16,4,2048]{3,1,2,0:T(8,128)S(1)} fusion(f32[1,16,6,2048]{3,1,2,0:T(8,128)S(1)} %get-tuple-element.39, f32[4,2048]{1,0:T(4,128)S(1)} %get-tuple-element.71, f32[4,2048]{1,0:T(4,128)S(1)} %get-tuple-element.75, f32[16,16]{1,0:T(8,128)S(1)} %copy-done), kind=kOutput, calls=%fused_computation.6 | convolution fusion | flops 26869760 | bytes 2957312 | tf_op jit(solution)/shard_map/ts,psrc->ptrc/dot_general | solution.py:82
  38.6 1.7 %collective-permute-start.5 = (f32[1,2]{1,0:T(1,128)S(1)}, f32[1,2]{1,0:T(1,128)S(1)}, u32[]{:S(2)}, u32[]{:S(2)}) collective-permute-start(f32[1,2]{1,0:T(1,128)S(1)} %bitcast_add_fusion.2), channel_id=1, source_target_pairs={{0,2},{1,3},{2,0},{3,1},{4,6},{5,7},{6,4},{7,5},{8,10},{9,11},{10,... | collective-permute-start | bytes 32 | tf_op jit(solution)/shard_map/ppermute | solution.py:40
  40.3 3.4 %fusion.5 = f32[1,16,14,2048]{3,1,2,0:T(8,128)S(1)} fusion(f32[1,16,16,2048]{3,1,2,0:T(8,128)S(1)} %pad_maximum_fusion, f32[14,2048]{1,0:T(8,128)S(1)} %slice_add_fusion.8, f32[14,2048]{1,0:T(8,128)S(1)} %bitcast.105), kind=kLoop, calls=%fused_computation.23 | loop fusion | flops 5963776 | bytes 9699328 | tf_op jit(solution)/shard_map/mul | solution.py:86
  43.8 2.7 %collective-permute-start.6 = (f32[1,2]{1,0:T(1,128)S(1)}, f32[1,2]{1,0:T(1,128)S(1)}, u32[]{:S(2)}, u32[]{:S(2)}) collective-permute-start(f32[1,2]{1,0:T(1,128)S(1)} %add.321), channel_id=1, source_target_pairs={{0,4},{1,5},{2,6},{3,7},{4,0},{5,1},{6,2},{7,3},{8,12},{9,13},{10,... | collective-permute-start | bytes 32 | tf_op jit(solution)/shard_map/ppermute | solution.py:40
  46.4 4.1 %convolution_bitcast_fusion = f32[1,16,12,2048]{3,1,2,0:T(8,128)S(1)} fusion(f32[1,16,14,2048]{3,1,2,0:T(8,128)S(1)} %fusion.5, f32[12,2048]{1,0:T(8,128)S(1)} %slice_add_fusion.7, f32[12,2048]{1,0:T(8,128)S(1)} %bitcast.106, f32[16,16]{1,0:T(8,128)S(1)} %copy-done), kind=kOutput, calls=%fused_computation.3 | convolution fusion | flops 80609280 | bytes 8396800 | tf_op jit(solution)/shard_map/ts,psrc->ptrc/dot_general | solution.py:82
  53.4 2.1 %fusion.46 = f32[1,16,10,2048]{3,1,2,0:T(8,128)S(1)} fusion(f32[1,16,12,2048]{3,1,2,0:T(8,128)S(1)} %fusion.24, f32[10,2048]{1,0:T(8,128)S(1)} %slice_add_fusion.9, f32[10,2048]{1,0:T(8,128)S(1)} %bitcast.104), kind=kLoop, calls=%fused_computation.81 | loop fusion | flops 4259840 | bytes 7077888 | tf_op jit(solution)/shard_map/mul | solution.py:86
  56.4 1.1 %collective-permute-done.7 = f32[1,3]{1,0:T(1,128)S(1)} collective-permute-done((f32[1,3]{1,0:T(1,128)S(1)}, f32[1,3]{1,0:T(1,128)S(1)}, u32[]{:S(2)}, u32[]{:S(2)}) %collective-permute-start.7) | collective-permute-done | bytes 44 | tf_op jit(solution)/shard_map/ppermute | solution.py:40
  57.5 2.5 %convolution_bitcast_fusion.1 = f32[1,16,8,2048]{3,1,2,0:T(8,128)S(1)} fusion(f32[1,16,10,2048]{3,1,2,0:T(8,128)S(1)} %fusion.46, f32[8,2048]{1,0:T(8,128)S(1)} %broadcast_add_fusion, f32[8,2048]{1,0:T(8,128)S(1)} %bitcast.108, f32[16,16]{1,0:T(8,128)S(1)} %copy-done), kind=kOutput, calls=%fused_computation.4 | convolution fusion | flops 53739520 | bytes 5644288 | tf_op jit(solution)/shard_map/ts,psrc->ptrc/dot_general | solution.py:82
  60.6 3.1 %collective-permute-done.8 = f32[1,3]{1,0:T(1,128)S(1)} collective-permute-done((f32[1,3]{1,0:T(1,128)S(1)}, f32[1,3]{1,0:T(1,128)S(1)}, u32[]{:S(2)}, u32[]{:S(2)}) %collective-permute-start.8) | collective-permute-done | bytes 44 | tf_op jit(solution)/shard_map/ppermute | solution.py:40
  64.0 4.1 %collective-permute-done.9 = f32[1,3]{1,0:T(1,128)S(1)} collective-permute-done((f32[1,3]{1,0:T(1,128)S(1)}, f32[1,3]{1,0:T(1,128)S(1)}, u32[]{:S(2)}, u32[]{:S(2)}) %collective-permute-start.9) | collective-permute-done | bytes 44 | tf_op jit(solution)/shard_map/ppermute | solution.py:40
  72.1 1.1 %collective-permute-done.10 = f32[1,3]{1,0:T(1,128)S(1)} collective-permute-done((f32[1,3]{1,0:T(1,128)S(1)}, f32[1,3]{1,0:T(1,128)S(1)}, u32[]{:S(2)}, u32[]{:S(2)}) %collective-permute-start.10) | collective-permute-done | bytes 44 | tf_op jit(solution)/shard_map/ppermute | solution.py:40
  73.7 3.1 %collective-permute-done.11 = f32[1,3]{1,0:T(1,128)S(1)} collective-permute-done((f32[1,3]{1,0:T(1,128)S(1)}, f32[1,3]{1,0:T(1,128)S(1)}, u32[]{:S(2)}, u32[]{:S(2)}) %collective-permute-start.11) | collective-permute-done | bytes 44 | tf_op jit(solution)/shard_map/ppermute | solution.py:40
  77.2 4.1 %collective-permute-done.12 = f32[1,3]{1,0:T(1,128)S(1)} collective-permute-done((f32[1,3]{1,0:T(1,128)S(1)}, f32[1,3]{1,0:T(1,128)S(1)}, u32[]{:S(2)}, u32[]{:S(2)}) %collective-permute-start.12) | collective-permute-done | bytes 44 | tf_op jit(solution)/shard_map/ppermute | solution.py:40
  84.9 1.6 %copy.12 = f32[1,16,8,2048]{3,2,0,1:T(8,128)} copy(f32[1,16,8,2048]{3,1,2,0:T(8,128)S(1)} %get-tuple-element.30) | data formatting | bytes 2097152 | tf_op jit(solution)/shard_map/sub | solution.py:138
  86.5 3.5 %all-to-all-start.1 = ((f32[1,16,8,2048]{3,2,0,1:T(8,128)}), f32[1,16,8,2048]{3,2,0,1:T(8,128)S(1)}, u32[]{:S(2)}, u32[]{:S(2)}) async-start(f32[1,16,8,2048]{3,2,0,1:T(8,128)} %copy.12), calls=%async_computation.1 | async-start | bytes 2097152 | tf_op jit(solution)/shard_map/all_to_all | solution.py:156
  90.9 1.1 %collective-permute-done.13 = f32[4,7]{1,0:T(4,128)S(1)} collective-permute-done((f32[4,7]{1,0:T(4,128)S(1)}, f32[4,7]{1,0:T(4,128)S(1)}, u32[]{:S(2)}, u32[]{:S(2)}) %collective-permute-start.13) | collective-permute-done | bytes 144 | tf_op jit(solution)/shard_map/ppermute | solution.py:40
  93.2 3.1 %collective-permute-done.14 = f32[4,7]{1,0:T(4,128)S(1)} collective-permute-done((f32[4,7]{1,0:T(4,128)S(1)}, f32[4,7]{1,0:T(4,128)S(1)}, u32[]{:S(2)}, u32[]{:S(2)}) %collective-permute-start.14) | collective-permute-done | bytes 144 | tf_op jit(solution)/shard_map/ppermute | solution.py:40
  96.7 4.1 %collective-permute-done.15 = f32[4,7]{1,0:T(4,128)S(1)} collective-permute-done((f32[4,7]{1,0:T(4,128)S(1)}, f32[4,7]{1,0:T(4,128)S(1)}, u32[]{:S(2)}, u32[]{:S(2)}) %collective-permute-start.15) | collective-permute-done | bytes 144 | tf_op jit(solution)/shard_map/ppermute | solution.py:40
  100.8 2.0 %collective-permute-start.16 = (f32[4,7]{1,0:T(4,128)S(1)}, f32[4,7]{1,0:T(4,128)S(1)}, u32[]{:S(2)}, u32[]{:S(2)}) collective-permute-start(f32[4,7]{1,0:T(4,128)S(1)} %add.355), channel_id=1, source_target_pairs={{0,8},{8,0},{16,24},{24,16},{1,9},{9,1},{17,25},{25,17},{2,10},{10... | collective-permute-start | bytes 344 | tf_op jit(solution)/shard_map/ppermute | solution.py:40
  102.8 1.6 %collective-permute-done.16 = f32[4,7]{1,0:T(4,128)S(1)} collective-permute-done((f32[4,7]{1,0:T(4,128)S(1)}, f32[4,7]{1,0:T(4,128)S(1)}, u32[]{:S(2)}, u32[]{:S(2)}) %collective-permute-start.16) | collective-permute-done | bytes 144 | tf_op jit(solution)/shard_map/ppermute | solution.py:40
  104.4 2.0 %collective-permute-start.17 = (f32[4,7]{1,0:T(4,128)S(1)}, f32[4,7]{1,0:T(4,128)S(1)}, u32[]{:S(2)}, u32[]{:S(2)}) collective-permute-start(f32[4,7]{1,0:T(4,128)S(1)} %add.356), channel_id=1, source_target_pairs={{0,16},{8,24},{16,0},{24,8},{1,17},{9,25},{17,1},{25,9},{2,18},{10... | collective-permute-start | bytes 344 | tf_op jit(solution)/shard_map/ppermute | solution.py:40
  106.4 1.6 %collective-permute-done.17 = f32[4,7]{1,0:T(4,128)S(1)} collective-permute-done((f32[4,7]{1,0:T(4,128)S(1)}, f32[4,7]{1,0:T(4,128)S(1)}, u32[]{:S(2)}, u32[]{:S(2)}) %collective-permute-start.17) | collective-permute-done | bytes 144 | tf_op jit(solution)/shard_map/ppermute | solution.py:40
  109.0 1.2 %divide_multiply_fusion = f32[4,4,8,2048]{3,2,1,0:T(8,128)} fusion(f32[4,4,8,2048]{3,2,1,0:T(8,128)S(1)} %bitcast.101, f32[4]{0:T(128)S(1)} %get-tuple-element.28, f32[4]{0:T(128)S(1)} %get-tuple-element.27), kind=kLoop, calls=%fused_computation.140 | loop fusion | flops 524288 | bytes 2097184 | tf_op jit(solution)/shard_map/mul | solution.py:171
  (99 shorter events, 16.1 us)
Async XLA Ops:
  0.6 8.2 %copy-start = (f32[16,16]{1,0:T(8,128)S(1)}, f32[16,16]{1,0:T(8,128)}, u32[]{:S(2)}) copy-start(f32[16,16]{1,0:T(8,128)} %param.7) | copy-start | bytes 3076
  0.6 7.4 %copy-start.2 = (f32[8,2048]{1,0:T(8,128)S(1)}, f32[8,2048]{1,0:T(8,128)}, u32[]{:S(2)}) copy-start(f32[8,2048]{1,0:T(8,128)} %param.6) | copy-start | bytes 196612
  2.9 13.2 %all-to-all-start = ((bf16[4,4,8,2048]{3,2,1,0:T(8,128)(2,1)}), bf16[4,4,8,2048]{3,2,1,0:T(8,128)(2,1)S(1)}, u32[]{:S(2)}, u32[]{:S(2)}) async-start(bf16[4,4,8,2048]{3,2,1,0:T(8,128)(2,1)} %multiply_convert_fusion), calls=%async_computation | async-start | bytes 1048576 | tf_op jit(solution)/shard_map/all_to_all | solution.py:74
  8.1 1.5 %collective-permute-start.2 = (f32[6,2048]{1,0:T(8,128)S(1)}, f32[6,2048]{1,0:T(8,128)S(1)}, u32[]{:S(2)}, u32[]{:S(2)}) collective-permute-start(f32[6,2048]{1,0:T(8,128)S(1)} %get-tuple-element.60), channel_id=1, source_target_pairs={{0,1},{2,3},{4,5},{6,7},{1,0},{3,2},{5,4},{7,6},{8,9},{10,11},{12,... | collective-permute-start | bytes 147464 | tf_op jit(solution)/shard_map/ppermute | solution.py:64
  8.2 1.4 %collective-permute-start.3 = (f32[6,2048]{1,0:T(8,128)S(1)}, f32[6,2048]{1,0:T(8,128)S(1)}, u32[]{:S(2)}, u32[]{:S(2)}) collective-permute-start(f32[6,2048]{1,0:T(8,128)S(1)} %get-tuple-element.61), channel_id=1, source_target_pairs={{1,2},{3,4},{5,6},{2,1},{4,3},{6,5},{9,10},{11,12},{13,14},{10,9},... | collective-permute-start | bytes 147464 | tf_op jit(solution)/shard_map/ppermute | solution.py:63
  16.4 1.8 %collective-permute-start = (bf16[1,16,6,2048]{3,1,2,0:T(8,128)(2,1)S(1)}, bf16[1,16,6,2048]{3,1,2,0:T(8,128)(2,1)S(1)}, u32[]{:S(2)}, u32[]{:S(2)}) collective-permute-start(bf16[1,16,6,2048]{3,1,2,0:T(8,128)(2,1)S(1)} %get-tuple-element.50), channel_id=1, source_target_pairs={{0,1},{2,3},{4,5},{6,7},{1,0},{3,2},{5,4},{7,6},{8,9},{10,11},{12,... | collective-permute-start | bytes 1179656 | tf_op jit(solution)/shard_map/ppermute | solution.py:64
  16.5 1.7 %collective-permute-start.1 = (bf16[1,16,6,2048]{3,1,2,0:T(8,128)(2,1)S(1)}, bf16[1,16,6,2048]{3,1,2,0:T(8,128)(2,1)S(1)}, u32[]{:S(2)}, u32[]{:S(2)}) collective-permute-start(bf16[1,16,6,2048]{3,1,2,0:T(8,128)(2,1)S(1)} %get-tuple-element.51), channel_id=1, source_target_pairs={{1,2},{3,4},{5,6},{2,1},{4,3},{6,5},{9,10},{11,12},{13,14},{10,9},... | collective-permute-start | bytes 1179656 | tf_op jit(solution)/shard_map/ppermute | solution.py:63
  18.6 0.7 copy-start.1
  24.8 8.3 %slice-start = ((f32[1,1,20,2048]{3,1,2,0:T(1,128)}), f32[1,1,14,2048]{3,1,2,0:T(1,128)S(1)}, s32[]{:S(2)}) async-start(f32[1,1,20,2048]{3,1,2,0:T(1,128)} %copy-done.1), calls=%async_computation.2 | async-start | bytes 229376 | tf_op jit(solution)/shard_map/slice | solution.py:86
  24.8 8.3 %slice-start.1 = ((f32[1,1,20,2048]{3,1,2,0:T(1,128)}), f32[1,1,12,2048]{3,1,2,0:T(1,128)S(1)}, s32[]{:S(2)}) async-start(f32[1,1,20,2048]{3,1,2,0:T(1,128)} %copy-done.1), calls=%async_computation.3 | async-start | bytes 196608 | tf_op jit(solution)/shard_map/slice | solution.py:86
  25.1 13.5 %collective-permute-start.4 = (f32[1,2]{1,0:T(1,128)S(1)}, f32[1,2]{1,0:T(1,128)S(1)}, u32[]{:S(2)}, u32[]{:S(2)}) collective-permute-start(f32[1,2]{1,0:T(1,128)S(1)} %bitcast.110), channel_id=1, source_target_pairs={{0,1},{1,0},{2,3},{3,2},{4,5},{5,4},{6,7},{7,6},{8,9},{9,8},{10,11... | collective-permute-start | bytes 32 | tf_op jit(solution)/shard_map/ppermute | solution.py:40
  38.6 5.1 %collective-permute-start.5 = (f32[1,2]{1,0:T(1,128)S(1)}, f32[1,2]{1,0:T(1,128)S(1)}, u32[]{:S(2)}, u32[]{:S(2)}) collective-permute-start(f32[1,2]{1,0:T(1,128)S(1)} %bitcast_add_fusion.2), channel_id=1, source_target_pairs={{0,2},{1,3},{2,0},{3,1},{4,6},{5,7},{6,4},{7,5},{8,10},{9,11},{10,... | collective-permute-start | bytes 32 | tf_op jit(solution)/shard_map/ppermute | solution.py:40
  43.8 6.8 %collective-permute-start.6 = (f32[1,2]{1,0:T(1,128)S(1)}, f32[1,2]{1,0:T(1,128)S(1)}, u32[]{:S(2)}, u32[]{:S(2)}) collective-permute-start(f32[1,2]{1,0:T(1,128)S(1)} %add.321), channel_id=1, source_target_pairs={{0,4},{1,5},{2,6},{3,7},{4,0},{5,1},{6,2},{7,3},{8,12},{9,13},{10,... | collective-permute-start | bytes 32 | tf_op jit(solution)/shard_map/ppermute | solution.py:40
  56.3 1.2 %collective-permute-start.7 = (f32[1,3]{1,0:T(1,128)S(1)}, f32[1,3]{1,0:T(1,128)S(1)}, u32[]{:S(2)}, u32[]{:S(2)}) collective-permute-start(f32[1,3]{1,0:T(1,128)S(1)} %bitcast.111), channel_id=1, source_target_pairs={{0,1},{1,0},{2,3},{3,2},{4,5},{5,4},{6,7},{7,6},{8,9},{9,8},{10,11... | collective-permute-start | bytes 44 | tf_op jit(solution)/shard_map/ppermute | solution.py:40
  60.0 3.6 %collective-permute-start.8 = (f32[1,3]{1,0:T(1,128)S(1)}, f32[1,3]{1,0:T(1,128)S(1)}, u32[]{:S(2)}, u32[]{:S(2)}) collective-permute-start(f32[1,3]{1,0:T(1,128)S(1)} %bitcast_add_fusion.1), channel_id=1, source_target_pairs={{0,2},{1,3},{2,0},{3,1},{4,6},{5,7},{6,4},{7,5},{8,10},{9,11},{10,... | collective-permute-start | bytes 44 | tf_op jit(solution)/shard_map/ppermute | solution.py:40
  63.7 4.5 %collective-permute-start.9 = (f32[1,3]{1,0:T(1,128)S(1)}, f32[1,3]{1,0:T(1,128)S(1)}, u32[]{:S(2)}, u32[]{:S(2)}) collective-permute-start(f32[1,3]{1,0:T(1,128)S(1)} %add.341), channel_id=1, source_target_pairs={{0,4},{1,5},{2,6},{3,7},{4,0},{5,1},{6,2},{7,3},{8,12},{9,13},{10,... | collective-permute-start | bytes 44 | tf_op jit(solution)/shard_map/ppermute | solution.py:40
  72.1 1.2 %collective-permute-start.10 = (f32[1,3]{1,0:T(1,128)S(1)}, f32[1,3]{1,0:T(1,128)S(1)}, u32[]{:S(2)}, u32[]{:S(2)}) collective-permute-start(f32[1,3]{1,0:T(1,128)S(1)} %bitcast.112), channel_id=1, source_target_pairs={{0,1},{1,0},{2,3},{3,2},{4,5},{5,4},{6,7},{7,6},{8,9},{9,8},{10,11... | collective-permute-start | bytes 44 | tf_op jit(solution)/shard_map/ppermute | solution.py:40
  73.3 3.6 %collective-permute-start.11 = (f32[1,3]{1,0:T(1,128)S(1)}, f32[1,3]{1,0:T(1,128)S(1)}, u32[]{:S(2)}, u32[]{:S(2)}) collective-permute-start(f32[1,3]{1,0:T(1,128)S(1)} %bitcast_add_fusion), channel_id=1, source_target_pairs={{0,2},{1,3},{2,0},{3,1},{4,6},{5,7},{6,4},{7,5},{8,10},{9,11},{10,... | collective-permute-start | bytes 44 | tf_op jit(solution)/shard_map/ppermute | solution.py:40
  76.9 4.5 %collective-permute-start.12 = (f32[1,3]{1,0:T(1,128)S(1)}, f32[1,3]{1,0:T(1,128)S(1)}, u32[]{:S(2)}, u32[]{:S(2)}) collective-permute-start(f32[1,3]{1,0:T(1,128)S(1)} %add.349), channel_id=1, source_target_pairs={{0,4},{1,5},{2,6},{3,7},{4,0},{5,1},{6,2},{7,3},{8,12},{9,13},{10,... | collective-permute-start | bytes 44 | tf_op jit(solution)/shard_map/ppermute | solution.py:40
  86.5 22.5 %all-to-all-start.1 = ((f32[1,16,8,2048]{3,2,0,1:T(8,128)}), f32[1,16,8,2048]{3,2,0,1:T(8,128)S(1)}, u32[]{:S(2)}, u32[]{:S(2)}) async-start(f32[1,16,8,2048]{3,2,0,1:T(8,128)} %copy.12), calls=%async_computation.1 | async-start | bytes 2097152 | tf_op jit(solution)/shard_map/all_to_all | solution.py:156
  90.8 1.2 %collective-permute-start.13 = (f32[4,7]{1,0:T(4,128)S(1)}, f32[4,7]{1,0:T(4,128)S(1)}, u32[]{:S(2)}, u32[]{:S(2)}) collective-permute-start(f32[4,7]{1,0:T(4,128)S(1)} %dynamic_update_slice.5), channel_id=1, source_target_pairs={{0,1},{1,0},{2,3},{3,2},{4,5},{5,4},{6,7},{7,6},{8,9},{9,8},{10,11... | collective-permute-start | bytes 344 | tf_op jit(solution)/shard_map/ppermute | solution.py:40
  92.7 3.6 %collective-permute-start.14 = (f32[4,7]{1,0:T(4,128)S(1)}, f32[4,7]{1,0:T(4,128)S(1)}, u32[]{:S(2)}, u32[]{:S(2)}) collective-permute-start(f32[4,7]{1,0:T(4,128)S(1)} %add.353), channel_id=1, source_target_pairs={{0,2},{1,3},{2,0},{3,1},{4,6},{5,7},{6,4},{7,5},{8,10},{9,11},{10,... | collective-permute-start | bytes 344 | tf_op jit(solution)/shard_map/ppermute | solution.py:40
  96.3 4.5 %collective-permute-start.15 = (f32[4,7]{1,0:T(4,128)S(1)}, f32[4,7]{1,0:T(4,128)S(1)}, u32[]{:S(2)}, u32[]{:S(2)}) collective-permute-start(f32[4,7]{1,0:T(4,128)S(1)} %add.354), channel_id=1, source_target_pairs={{0,4},{1,5},{2,6},{3,7},{4,0},{5,1},{6,2},{7,3},{8,12},{9,13},{10,... | collective-permute-start | bytes 344 | tf_op jit(solution)/shard_map/ppermute | solution.py:40
  100.8 3.6 %collective-permute-start.16 = (f32[4,7]{1,0:T(4,128)S(1)}, f32[4,7]{1,0:T(4,128)S(1)}, u32[]{:S(2)}, u32[]{:S(2)}) collective-permute-start(f32[4,7]{1,0:T(4,128)S(1)} %add.355), channel_id=1, source_target_pairs={{0,8},{8,0},{16,24},{24,16},{1,9},{9,1},{17,25},{25,17},{2,10},{10... | collective-permute-start | bytes 344 | tf_op jit(solution)/shard_map/ppermute | solution.py:40
  104.4 3.6 %collective-permute-start.17 = (f32[4,7]{1,0:T(4,128)S(1)}, f32[4,7]{1,0:T(4,128)S(1)}, u32[]{:S(2)}, u32[]{:S(2)}) collective-permute-start(f32[4,7]{1,0:T(4,128)S(1)} %add.356), channel_id=1, source_target_pairs={{0,16},{8,24},{16,0},{24,8},{1,17},{9,25},{17,1},{25,9},{2,18},{10... | collective-permute-start | bytes 344 | tf_op jit(solution)/shard_map/ppermute | solution.py:40
  108.0 2.2 %copy-start.3 = (f32[4,7]{1,0:T(4,128)}, f32[4,7]{1,0:T(4,128)S(1)}, u32[]{:S(2)}) copy-start(f32[4,7]{1,0:T(4,128)S(1)} %add.357) | copy-start | bytes 340

commit v2 on v0

--- a/solution.py
+++ b/solution.py
@@ -60,16 +60,7 @@
     odd = lax.axis_index("tile") % 2 == 1
     across = [(i, i + 1) for i in range(1, n - 1, 2)] + [(i + 1, i) for i in range(1, n - 1, 2)]
     within = [(i, i + 1) for i in range(0, n - 1, 2)] + [(i + 1, i) for i in range(0, n - 1, 2)]
-    send = jnp.where(odd, bottom, top)
-    pieces = 2 if width % 2 == 0 else 1
-    step = width // pieces
-    got_across = jnp.concatenate(
-        [
-            lax.ppermute(lax.slice_in_dim(send, k * step, (k + 1) * step, axis=dim), "tile", across)
-            for k in range(pieces)
-        ],
-        axis=dim,
-    )
+    got_across = lax.ppermute(jnp.where(odd, bottom, top), "tile", across)
     got_within = lax.ppermute(jnp.where(odd, top, bottom), "tile", within)
     low = jnp.where(odd, got_within, got_across)
     high = jnp.where(odd, got_across, got_within)
@@ -162,7 +153,8 @@
         mine,
         (lax.axis_index("trait") * probes_local, 0),
     )
-    scalars = butterfly_sum(butterfly_sum(spread, "tile")[0], "trait")[0]
+    scalars = butterfly_sum(spread, "tile")[0]
+    scalars = butterfly_sum(scalars, "trait")[0]
     beta = jnp.sqrt(scalars[:, 2 * iters - 1] + epsilon)
     norm_all = scalars[:, 2 * iters]
     last = (w_back / beta[:, None, None, None]) * norm_all[:, None, None, None]

time: 111 us -> 108 us (0.973)
    ppermute x14, starting transfers between devices: 22.9 us -> 26.7 us  [butterfly_sum(): got = lax.ppermute(v, axis, [(i, i ^ s) for i in range(n)])]
    ppermute x2, starting transfers between devices: 3.07 us -> 0.14 us  [halo_rows(): got_within = lax.ppermute(jnp.where(odd, top, bottom), 'tile', within)]
    ppermute x14, waiting for transfers between devices: 20.8 us -> 18.7 us  [butterfly_sum(): got = lax.ppermute(v, axis, [(i, i ^ s) for i in range(n)])]
    ppermute x4 -> x2, starting transfers between devices: 2.66 us -> 1.35 us  [halo_rows(): got_across = lax.ppermute(jnp.where(odd, bottom, top), 'tile', across)]
  transfers between devices with their start and end apart: 22 -> 20, of which waited for: 13 -> 13; matrix products, arithmetic and copies ran while one was open for 14% -> 15% of each run, Pallas kernels for 0% -> 0%
where the time goes in v2:
time: 108 us
  starting transfers between devices  36.9 us (34%)
  waiting for transfers between devices  26 us (24%)
  other arithmetic  20.9 us (19%)
  matrix products  12.4 us (11%)
  between operations  6.37 us (6%)
  local copies, waits for them, and re-layouts  5.29 us (5%)
    ppermute x14, starting transfers between devices, butterfly_sum(): got = lax.ppermute(v, axis, [(i, i ^ s) for i in range(n)])  26.7 us
    ppermute x14, waiting for transfers between devices, butterfly_sum(): got = lax.ppermute(v, axis, [(i, i ^ s) for i in range(n)])  18.7 us
    dot_general x3, matrix products, mix(): jnp.einsum('ts,psrc->ptrc', trait_covariance, x, precision=lax.Precision....  12.4 us
    mul x3, other arithmetic, stencil(): land_ext[off + 1:off + r - 1]  9.99 us
    all_to_all x1, waiting for transfers between devices, shards(): lax.all_to_all(signed, 'trait', split_axis=0, concat_axis=1, tiled=True)  6.36 us
    all_to_all x1, starting transfers between devices, shards(): lax.all_to_all(signed, 'trait', split_axis=0, concat_axis=1, tiled=True)  5.19 us
    all_to_all x1, starting transfers between devices, shards(): lax.all_to_all(w_own, 'trait', split_axis=1, concat_axis=0, tiled=True)  3.52 us
    convert_element_type x1, other arithmetic, shards(): (land_mask[None, None] * (2 * probe_signs - 1)).astype(jnp.bfloat16)  2.22 us
  transfers between devices with their start and end apart: 20, of which 13 were waited for; matrix products, arithmetic and copies ran while one was open for 15% of the time, Pallas kernels for 0%

profile of v2, /device:TPU:0, one launch (start us, length us, event | category | flops | bytes accessed | tf_op | source)
XLA Modules:
  0.0 107.9 jit_solution(14654616165554387380)
XLA Ops:
  0.7 2.2 %multiply_convert_fusion = bf16[4,4,8,2048]{3,2,1,0:T(8,128)(2,1)} fusion(s32[4,4,8,2048]{3,2,1,0:T(8,128)} %param.4, s32[8,2048]{1,0:T(8,128)} %param.5), kind=kLoop, calls=%fused_computation.163 | loop fusion | flops 1048576 | bytes 1638400 | tf_op jit(solution)/shard_map/convert_element_type | solution.py:73
  2.9 5.2 %all-to-all-start = ((bf16[4,4,8,2048]{3,2,1,0:T(8,128)(2,1)}), bf16[4,4,8,2048]{3,2,1,0:T(8,128)(2,1)S(1)}, u32[]{:S(2)}, u32[]{:S(2)}) async-start(bf16[4,4,8,2048]{3,2,1,0:T(8,128)(2,1)} %multiply_convert_fusion), calls=%async_computation | async-start | bytes 1048576 | tf_op jit(solution)/shard_map/all_to_all | solution.py:74
  9.7 6.4 %all-to-all-done = bf16[4,4,8,2048]{3,2,1,0:T(8,128)(2,1)S(1)} async-done(((bf16[4,4,8,2048]{3,2,1,0:T(8,128)(2,1)}), bf16[4,4,8,2048]{3,2,1,0:T(8,128)(2,1)S(1)}, u32[]{:S(2)}, u32[]{:S(2)}) %all-to-all-start) | async-done | bytes 524320 | tf_op jit(solution)/shard_map/all_to_all | solution.py:74
  19.4 4.4 %fusion.5 = f32[1,16,18,2048]{3,1,2,0:T(8,128)S(1)} fusion(f32[1,16,20,2048]{3,1,2,0:T(8,128)S(1)} %broadcast_multiply_fusion, f32[18,2048]{1,0:T(8,128)S(1)} %slice_add_fusion.4, f32[18,2048]{1,0:T(8,128)S(1)} %bitcast.83), kind=kLoop, calls=%fused_computation.17 | loop fusion | flops 7667712 | bytes 12451840 | tf_op jit(solution)/shard_map/mul | solution.py:86
  23.8 5.6 %convolution_bitcast_fusion = f32[1,16,16,2048]{3,1,2,0:T(8,128)S(1)} fusion(f32[1,16,18,2048]{3,1,2,0:T(8,128)S(1)} %fusion.5, f32[16,2048]{1,0:T(8,128)S(1)} %slice_add_fusion.8, f32[16,2048]{1,0:T(8,128)S(1)} %bitcast.87, f32[16,16]{1,0:T(8,128)S(1)} %copy-done), kind=kOutput, calls=%fused_computation.3 | convolution fusion | flops 107479040 | bytes 11018240 | tf_op jit(solution)/shard_map/ts,psrc->ptrc/dot_general | solution.py:82
  30.0 7.9 %collective-permute-start.4 = (f32[1,2]{1,0:T(1,128)S(1)}, f32[1,2]{1,0:T(1,128)S(1)}, u32[]{:S(2)}, u32[]{:S(2)}) collective-permute-start(f32[1,2]{1,0:T(1,128)S(1)} %bitcast.90), channel_id=1, source_target_pairs={{0,1},{1,0},{2,3},{3,2},{4,5},{5,4},{6,7},{7,6},{8,9},{9,8},{10,11... | collective-permute-start | bytes 32 | tf_op jit(solution)/shard_map/ppermute | solution.py:40
  38.0 3.5 %fusion.33 = f32[1,16,14,2048]{3,1,2,0:T(8,128)S(1)} fusion(f32[1,16,16,2048]{3,1,2,0:T(8,128)S(1)} %convolution_bitcast_fusion, f32[14,2048]{1,0:T(8,128)S(1)} %slice_add_fusion.7, f32[14,2048]{1,0:T(8,128)S(1)} %bitcast.85), kind=kLoop, calls=%fused_computation.60 | loop fusion | flops 5963776 | bytes 9699328 | tf_op jit(solution)/shard_map/mul | solution.py:86
  41.5 1.7 %collective-permute-start.5 = (f32[1,2]{1,0:T(1,128)S(1)}, f32[1,2]{1,0:T(1,128)S(1)}, u32[]{:S(2)}, u32[]{:S(2)}) collective-permute-start(f32[1,2]{1,0:T(1,128)S(1)} %bitcast_add_fusion.2), channel_id=1, source_target_pairs={{0,2},{1,3},{2,0},{3,1},{4,6},{5,7},{6,4},{7,5},{8,10},{9,11},{10,... | collective-permute-start | bytes 32 | tf_op jit(solution)/shard_map/ppermute | solution.py:40
  43.2 4.3 %convolution_bitcast_fusion.1 = f32[1,16,12,2048]{3,1,2,0:T(8,128)S(1)} fusion(f32[1,16,14,2048]{3,1,2,0:T(8,128)S(1)} %fusion.33, f32[12,2048]{1,0:T(8,128)S(1)} %slice_add_fusion.6, f32[12,2048]{1,0:T(8,128)S(1)} %bitcast.86, f32[16,16]{1,0:T(8,128)S(1)} %copy-done), kind=kOutput, calls=%fused_computation.4 | convolution fusion | flops 80609280 | bytes 8396800 | tf_op jit(solution)/shard_map/ts,psrc->ptrc/dot_general | solution.py:82
  47.5 2.7 %collective-permute-start.6 = (f32[1,2]{1,0:T(1,128)S(1)}, f32[1,2]{1,0:T(1,128)S(1)}, u32[]{:S(2)}, u32[]{:S(2)}) collective-permute-start(f32[1,2]{1,0:T(1,128)S(1)} %add.241), channel_id=1, source_target_pairs={{0,4},{1,5},{2,6},{3,7},{4,0},{5,1},{6,2},{7,3},{8,12},{9,13},{10,... | collective-permute-start | bytes 32 | tf_op jit(solution)/shard_map/ppermute | solution.py:40
  50.2 1.9 %collective-permute-done.6 = f32[1,2]{1,0:T(1,128)S(1)} collective-permute-done((f32[1,2]{1,0:T(1,128)S(1)}, f32[1,2]{1,0:T(1,128)S(1)}, u32[]{:S(2)}, u32[]{:S(2)}) %collective-permute-start.6) | collective-permute-done | bytes 40 | tf_op jit(solution)/shard_map/ppermute | solution.py:40
  55.8 2.1 %fusion.65 = f32[1,16,10,2048]{3,1,2,0:T(8,128)S(1)} fusion(f32[1,16,12,2048]{3,1,2,0:T(8,128)S(1)} %fusion.53, f32[10,2048]{1,0:T(8,128)S(1)} %slice_add_fusion.5, f32[10,2048]{1,0:T(8,128)S(1)} %bitcast.84), kind=kLoop, calls=%fused_computation.105 | loop fusion | flops 4259840 | bytes 7077888 | tf_op jit(solution)/shard_map/mul | solution.py:86
  58.4 2.5 %convolution_bitcast_fusion.2 = f32[1,16,8,2048]{3,1,2,0:T(8,128)S(1)} fusion(f32[1,16,10,2048]{3,1,2,0:T(8,128)S(1)} %fusion.65, f32[8,2048]{1,0:T(8,128)S(1)} %broadcast_add_fusion, f32[8,2048]{1,0:T(8,128)S(1)} %bitcast.88, f32[16,16]{1,0:T(8,128)S(1)} %copy-done), kind=kOutput, calls=%fused_computation.5 | convolution fusion | flops 53739520 | bytes 5644288 | tf_op jit(solution)/shard_map/ts,psrc->ptrc/dot_general | solution.py:82
  61.5 2.6 %collective-permute-start.9 = (f32[1,3]{1,0:T(1,128)S(1)}, f32[1,3]{1,0:T(1,128)S(1)}, u32[]{:S(2)}, u32[]{:S(2)}) collective-permute-start(f32[1,3]{1,0:T(1,128)S(1)} %add.257), channel_id=1, source_target_pairs={{0,4},{1,5},{2,6},{3,7},{4,0},{5,1},{6,2},{7,3},{8,12},{9,13},{10,... | collective-permute-start | bytes 44 | tf_op jit(solution)/shard_map/ppermute | solution.py:40
  64.1 1.9 %collective-permute-done.9 = f32[1,3]{1,0:T(1,128)S(1)} collective-permute-done((f32[1,3]{1,0:T(1,128)S(1)}, f32[1,3]{1,0:T(1,128)S(1)}, u32[]{:S(2)}, u32[]{:S(2)}) %collective-permute-start.9) | collective-permute-done | bytes 44 | tf_op jit(solution)/shard_map/ppermute | solution.py:40
  70.0 1.1 %collective-permute-done.10 = f32[1,3]{1,0:T(1,128)S(1)} collective-permute-done((f32[1,3]{1,0:T(1,128)S(1)}, f32[1,3]{1,0:T(1,128)S(1)}, u32[]{:S(2)}, u32[]{:S(2)}) %collective-permute-start.10) | collective-permute-done | bytes 44 | tf_op jit(solution)/shard_map/ppermute | solution.py:40
  71.1 1.1 collective-permute-start.11
  72.2 2.5 %collective-permute-done.11 = f32[1,3]{1,0:T(1,128)S(1)} collective-permute-done((f32[1,3]{1,0:T(1,128)S(1)}, f32[1,3]{1,0:T(1,128)S(1)}, u32[]{:S(2)}, u32[]{:S(2)}) %collective-permute-start.11) | collective-permute-done | bytes 44 | tf_op jit(solution)/shard_map/ppermute | solution.py:40
  74.7 2.6 %collective-permute-start.12 = (f32[1,3]{1,0:T(1,128)S(1)}, f32[1,3]{1,0:T(1,128)S(1)}, u32[]{:S(2)}, u32[]{:S(2)}) collective-permute-start(f32[1,3]{1,0:T(1,128)S(1)} %add.267), channel_id=1, source_target_pairs={{0,4},{1,5},{2,6},{3,7},{4,0},{5,1},{6,2},{7,3},{8,12},{9,13},{10,... | collective-permute-start | bytes 44 | tf_op jit(solution)/shard_map/ppermute | solution.py:40
  77.3 1.9 %collective-permute-done.12 = f32[1,3]{1,0:T(1,128)S(1)} collective-permute-done((f32[1,3]{1,0:T(1,128)S(1)}, f32[1,3]{1,0:T(1,128)S(1)}, u32[]{:S(2)}, u32[]{:S(2)}) %collective-permute-start.12) | collective-permute-done | bytes 44 | tf_op jit(solution)/shard_map/ppermute | solution.py:40
  82.6 1.6 %copy.12 = f32[1,16,8,2048]{3,2,0,1:T(8,128)} copy(f32[1,16,8,2048]{3,1,2,0:T(8,128)S(1)} %get-tuple-element.22) | data formatting | bytes 2097152 | tf_op jit(solution)/shard_map/sub | solution.py:126
  84.2 3.5 %all-to-all-start.1 = ((f32[1,16,8,2048]{3,2,0,1:T(8,128)}), f32[1,16,8,2048]{3,2,0,1:T(8,128)S(1)}, u32[]{:S(2)}, u32[]{:S(2)}) async-start(f32[1,16,8,2048]{3,2,0,1:T(8,128)} %copy.12), calls=%async_computation.1 | async-start | bytes 2097152 | tf_op jit(solution)/shard_map/all_to_all | solution.py:144
  88.6 1.1 %collective-permute-done.13 = f32[4,7]{1,0:T(4,128)S(1)} collective-permute-done((f32[4,7]{1,0:T(4,128)S(1)}, f32[4,7]{1,0:T(4,128)S(1)}, u32[]{:S(2)}, u32[]{:S(2)}) %collective-permute-start.13) | collective-permute-done | bytes 144 | tf_op jit(solution)/shard_map/ppermute | solution.py:40
  90.4 1.1 %collective-permute-start.14 = (f32[4,7]{1,0:T(4,128)S(1)}, f32[4,7]{1,0:T(4,128)S(1)}, u32[]{:S(2)}, u32[]{:S(2)}) collective-permute-start(f32[4,7]{1,0:T(4,128)S(1)} %add.271), channel_id=1, source_target_pairs={{0,2},{1,3},{2,0},{3,1},{4,6},{5,7},{6,4},{7,5},{8,10},{9,11},{10,... | collective-permute-start | bytes 344 | tf_op jit(solution)/shard_map/ppermute | solution.py:40
  91.5 2.5 %collective-permute-done.14 = f32[4,7]{1,0:T(4,128)S(1)} collective-permute-done((f32[4,7]{1,0:T(4,128)S(1)}, f32[4,7]{1,0:T(4,128)S(1)}, u32[]{:S(2)}, u32[]{:S(2)}) %collective-permute-start.14) | collective-permute-done | bytes 144 | tf_op jit(solution)/shard_map/ppermute | solution.py:40
  94.0 2.6 %collective-permute-start.15 = (f32[4,7]{1,0:T(4,128)S(1)}, f32[4,7]{1,0:T(4,128)S(1)}, u32[]{:S(2)}, u32[]{:S(2)}) collective-permute-start(f32[4,7]{1,0:T(4,128)S(1)} %add.272), channel_id=1, source_target_pairs={{0,4},{1,5},{2,6},{3,7},{4,0},{5,1},{6,2},{7,3},{8,12},{9,13},{10,... | collective-permute-start | bytes 344 | tf_op jit(solution)/shard_map/ppermute | solution.py:40
  96.6 1.9 %collective-permute-done.15 = f32[4,7]{1,0:T(4,128)S(1)} collective-permute-done((f32[4,7]{1,0:T(4,128)S(1)}, f32[4,7]{1,0:T(4,128)S(1)}, u32[]{:S(2)}, u32[]{:S(2)}) %collective-permute-start.15) | collective-permute-done | bytes 144 | tf_op jit(solution)/shard_map/ppermute | solution.py:40
  98.5 2.0 %collective-permute-start.16 = (f32[4,7]{1,0:T(4,128)S(1)}, f32[4,7]{1,0:T(4,128)S(1)}, u32[]{:S(2)}, u32[]{:S(2)}) collective-permute-start(f32[4,7]{1,0:T(4,128)S(1)} %add.273), channel_id=1, source_target_pairs={{0,8},{8,0},{16,24},{24,16},{1,9},{9,1},{17,25},{25,17},{2,10},{10... | collective-permute-start | bytes 344 | tf_op jit(solution)/shard_map/ppermute | solution.py:40
  100.5 1.6 %collective-permute-done.16 = f32[4,7]{1,0:T(4,128)S(1)} collective-permute-done((f32[4,7]{1,0:T(4,128)S(1)}, f32[4,7]{1,0:T(4,128)S(1)}, u32[]{:S(2)}, u32[]{:S(2)}) %collective-permute-start.16) | collective-permute-done | bytes 144 | tf_op jit(solution)/shard_map/ppermute | solution.py:40
  102.1 2.0 %collective-permute-start.17 = (f32[4,7]{1,0:T(4,128)S(1)}, f32[4,7]{1,0:T(4,128)S(1)}, u32[]{:S(2)}, u32[]{:S(2)}) collective-permute-start(f32[4,7]{1,0:T(4,128)S(1)} %add.274), channel_id=1, source_target_pairs={{0,16},{8,24},{16,0},{24,8},{1,17},{9,25},{17,1},{25,9},{2,18},{10... | collective-permute-start | bytes 344 | tf_op jit(solution)/shard_map/ppermute | solution.py:40
  104.1 1.6 %collective-permute-done.17 = f32[4,7]{1,0:T(4,128)S(1)} collective-permute-done((f32[4,7]{1,0:T(4,128)S(1)}, f32[4,7]{1,0:T(4,128)S(1)}, u32[]{:S(2)}, u32[]{:S(2)}) %collective-permute-start.17) | collective-permute-done | bytes 144 | tf_op jit(solution)/shard_map/ppermute | solution.py:40
  106.7 1.2 %divide_multiply_fusion = f32[4,4,8,2048]{3,2,1,0:T(8,128)} fusion(f32[4,4,8,2048]{3,2,1,0:T(8,128)S(1)} %bitcast.81, f32[4]{0:T(128)S(1)} %get-tuple-element.20, f32[4]{0:T(128)S(1)} %get-tuple-element.19), kind=kLoop, calls=%fused_computation.142 | loop fusion | flops 524288 | bytes 2097184 | tf_op jit(solution)/shard_map/mul | solution.py:160
  (96 shorter events, 14.9 us)
Async XLA Ops:
  0.6 8.2 %copy-start = (f32[16,16]{1,0:T(8,128)S(1)}, f32[16,16]{1,0:T(8,128)}, u32[]{:S(2)}) copy-start(f32[16,16]{1,0:T(8,128)} %param.7) | copy-start | bytes 3076
  0.6 7.4 %copy-start.2 = (f32[8,2048]{1,0:T(8,128)S(1)}, f32[8,2048]{1,0:T(8,128)}, u32[]{:S(2)}) copy-start(f32[8,2048]{1,0:T(8,128)} %param.6) | copy-start | bytes 196612
  2.9 13.2 %all-to-all-start = ((bf16[4,4,8,2048]{3,2,1,0:T(8,128)(2,1)}), bf16[4,4,8,2048]{3,2,1,0:T(8,128)(2,1)S(1)}, u32[]{:S(2)}, u32[]{:S(2)}) async-start(bf16[4,4,8,2048]{3,2,1,0:T(8,128)(2,1)} %multiply_convert_fusion), calls=%async_computation | async-start | bytes 1048576 | tf_op jit(solution)/shard_map/all_to_all | solution.py:74
  8.1 1.5 %collective-permute-start.2 = (f32[6,2048]{1,0:T(8,128)S(1)}, f32[6,2048]{1,0:T(8,128)S(1)}, u32[]{:S(2)}, u32[]{:S(2)}) collective-permute-start(f32[6,2048]{1,0:T(8,128)S(1)} %get-tuple-element.42), channel_id=1, source_target_pairs={{0,1},{2,3},{4,5},{6,7},{1,0},{3,2},{5,4},{7,6},{8,9},{10,11},{12,... | collective-permute-start | bytes 147464 | tf_op jit(solution)/shard_map/ppermute | solution.py:64
  8.2 1.4 %collective-permute-start.3 = (f32[6,2048]{1,0:T(8,128)S(1)}, f32[6,2048]{1,0:T(8,128)S(1)}, u32[]{:S(2)}, u32[]{:S(2)}) collective-permute-start(f32[6,2048]{1,0:T(8,128)S(1)} %get-tuple-element.43), channel_id=1, source_target_pairs={{1,2},{3,4},{5,6},{2,1},{4,3},{6,5},{9,10},{11,12},{13,14},{10,9},... | collective-permute-start | bytes 147464 | tf_op jit(solution)/shard_map/ppermute | solution.py:63
  16.4 1.8 %collective-permute-start = (bf16[1,16,6,2048]{3,1,2,0:T(8,128)(2,1)S(1)}, bf16[1,16,6,2048]{3,1,2,0:T(8,128)(2,1)S(1)}, u32[]{:S(2)}, u32[]{:S(2)}) collective-permute-start(bf16[1,16,6,2048]{3,1,2,0:T(8,128)(2,1)S(1)} %get-tuple-element.38), channel_id=1, source_target_pairs={{0,1},{2,3},{4,5},{6,7},{1,0},{3,2},{5,4},{7,6},{8,9},{10,11},{12,... | collective-permute-start | bytes 1179656 | tf_op jit(solution)/shard_map/ppermute | solution.py:64
  16.5 1.7 %collective-permute-start.1 = (bf16[1,16,6,2048]{3,1,2,0:T(8,128)(2,1)S(1)}, bf16[1,16,6,2048]{3,1,2,0:T(8,128)(2,1)S(1)}, u32[]{:S(2)}, u32[]{:S(2)}) collective-permute-start(bf16[1,16,6,2048]{3,1,2,0:T(8,128)(2,1)S(1)} %get-tuple-element.39), channel_id=1, source_target_pairs={{1,2},{3,4},{5,6},{2,1},{4,3},{6,5},{9,10},{11,12},{13,14},{10,9},... | collective-permute-start | bytes 1179656 | tf_op jit(solution)/shard_map/ppermute | solution.py:63
  18.6 0.7 copy-start.1
  29.5 8.3 %slice-start = ((f32[1,1,20,2048]{3,1,2,0:T(1,128)}), f32[1,1,14,2048]{3,1,2,0:T(1,128)S(1)}, s32[]{:S(2)}) async-start(f32[1,1,20,2048]{3,1,2,0:T(1,128)} %copy-done.1), calls=%async_computation.2 | async-start | bytes 229376 | tf_op jit(solution)/shard_map/slice | solution.py:86
  29.6 8.3 %slice-start.1 = ((f32[1,1,20,2048]{3,1,2,0:T(1,128)}), f32[1,1,12,2048]{3,1,2,0:T(1,128)S(1)}, s32[]{:S(2)}) async-start(f32[1,1,20,2048]{3,1,2,0:T(1,128)} %copy-done.1), calls=%async_computation.3 | async-start | bytes 196608 | tf_op jit(solution)/shard_map/slice | solution.py:86
  29.6 8.4 %slice-start.2 = ((f32[1,1,20,2048]{3,1,2,0:T(1,128)}), f32[1,1,10,2048]{3,1,2,0:T(1,128)S(1)}, s32[]{:S(2)}) async-start(f32[1,1,20,2048]{3,1,2,0:T(1,128)} %copy-done.1), calls=%async_computation.4 | async-start | bytes 163840 | tf_op jit(solution)/shard_map/slice | solution.py:86
  29.6 8.4 %slice-start.3 = ((f32[1,1,20,2048]{3,1,2,0:T(1,128)}), f32[1,1,8,2048]{3,1,2,0:T(1,128)S(1)}, s32[]{:S(2)}) async-start(f32[1,1,20,2048]{3,1,2,0:T(1,128)} %copy-done.1), calls=%async_computation.5 | async-start | bytes 131072 | tf_op jit(solution)/shard_map/slice | solution.py:86
  30.0 11.6 %collective-permute-start.4 = (f32[1,2]{1,0:T(1,128)S(1)}, f32[1,2]{1,0:T(1,128)S(1)}, u32[]{:S(2)}, u32[]{:S(2)}) collective-permute-start(f32[1,2]{1,0:T(1,128)S(1)} %bitcast.90), channel_id=1, source_target_pairs={{0,1},{1,0},{2,3},{3,2},{4,5},{5,4},{6,7},{7,6},{8,9},{9,8},{10,11... | collective-permute-start | bytes 32 | tf_op jit(solution)/shard_map/ppermute | solution.py:40
  41.5 6.0 %collective-permute-start.5 = (f32[1,2]{1,0:T(1,128)S(1)}, f32[1,2]{1,0:T(1,128)S(1)}, u32[]{:S(2)}, u32[]{:S(2)}) collective-permute-start(f32[1,2]{1,0:T(1,128)S(1)} %bitcast_add_fusion.2), channel_id=1, source_target_pairs={{0,2},{1,3},{2,0},{3,1},{4,6},{5,7},{6,4},{7,5},{8,10},{9,11},{10,... | collective-permute-start | bytes 32 | tf_op jit(solution)/shard_map/ppermute | solution.py:40
  47.5 4.5 %collective-permute-start.6 = (f32[1,2]{1,0:T(1,128)S(1)}, f32[1,2]{1,0:T(1,128)S(1)}, u32[]{:S(2)}, u32[]{:S(2)}) collective-permute-start(f32[1,2]{1,0:T(1,128)S(1)} %add.241), channel_id=1, source_target_pairs={{0,4},{1,5},{2,6},{3,7},{4,0},{5,1},{6,2},{7,3},{8,12},{9,13},{10,... | collective-permute-start | bytes 32 | tf_op jit(solution)/shard_map/ppermute | solution.py:40
  55.8 2.1 %collective-permute-start.7 = (f32[1,3]{1,0:T(1,128)S(1)}, f32[1,3]{1,0:T(1,128)S(1)}, u32[]{:S(2)}, u32[]{:S(2)}) collective-permute-start(f32[1,3]{1,0:T(1,128)S(1)} %bitcast.91), channel_id=1, source_target_pairs={{0,1},{1,0},{2,3},{3,2},{4,5},{5,4},{6,7},{7,6},{8,9},{9,8},{10,11... | collective-permute-start | bytes 44 | tf_op jit(solution)/shard_map/ppermute | solution.py:40
  57.9 3.6 %collective-permute-start.8 = (f32[1,3]{1,0:T(1,128)S(1)}, f32[1,3]{1,0:T(1,128)S(1)}, u32[]{:S(2)}, u32[]{:S(2)}) collective-permute-start(f32[1,3]{1,0:T(1,128)S(1)} %bitcast_add_fusion.1), channel_id=1, source_target_pairs={{0,2},{1,3},{2,0},{3,1},{4,6},{5,7},{6,4},{7,5},{8,10},{9,11},{10,... | collective-permute-start | bytes 44 | tf_op jit(solution)/shard_map/ppermute | solution.py:40
  61.5 4.5 %collective-permute-start.9 = (f32[1,3]{1,0:T(1,128)S(1)}, f32[1,3]{1,0:T(1,128)S(1)}, u32[]{:S(2)}, u32[]{:S(2)}) collective-permute-start(f32[1,3]{1,0:T(1,128)S(1)} %add.257), channel_id=1, source_target_pairs={{0,4},{1,5},{2,6},{3,7},{4,0},{5,1},{6,2},{7,3},{8,12},{9,13},{10,... | collective-permute-start | bytes 44 | tf_op jit(solution)/shard_map/ppermute | solution.py:40
  69.9 1.2 %collective-permute-start.10 = (f32[1,3]{1,0:T(1,128)S(1)}, f32[1,3]{1,0:T(1,128)S(1)}, u32[]{:S(2)}, u32[]{:S(2)}) collective-permute-start(f32[1,3]{1,0:T(1,128)S(1)} %bitcast.92), channel_id=1, source_target_pairs={{0,1},{1,0},{2,3},{3,2},{4,5},{5,4},{6,7},{7,6},{8,9},{9,8},{10,11... | collective-permute-start | bytes 44 | tf_op jit(solution)/shard_map/ppermute | solution.py:40
  71.1 3.6 %collective-permute-start.11 = (f32[1,3]{1,0:T(1,128)S(1)}, f32[1,3]{1,0:T(1,128)S(1)}, u32[]{:S(2)}, u32[]{:S(2)}) collective-permute-start(f32[1,3]{1,0:T(1,128)S(1)} %bitcast_add_fusion), channel_id=1, source_target_pairs={{0,2},{1,3},{2,0},{3,1},{4,6},{5,7},{6,4},{7,5},{8,10},{9,11},{10,... | collective-permute-start | bytes 44 | tf_op jit(solution)/shard_map/ppermute | solution.py:40
  74.7 4.5 %collective-permute-start.12 = (f32[1,3]{1,0:T(1,128)S(1)}, f32[1,3]{1,0:T(1,128)S(1)}, u32[]{:S(2)}, u32[]{:S(2)}) collective-permute-start(f32[1,3]{1,0:T(1,128)S(1)} %add.267), channel_id=1, source_target_pairs={{0,4},{1,5},{2,6},{3,7},{4,0},{5,1},{6,2},{7,3},{8,12},{9,13},{10,... | collective-permute-start | bytes 44 | tf_op jit(solution)/shard_map/ppermute | solution.py:40
  84.2 22.5 %all-to-all-start.1 = ((f32[1,16,8,2048]{3,2,0,1:T(8,128)}), f32[1,16,8,2048]{3,2,0,1:T(8,128)S(1)}, u32[]{:S(2)}, u32[]{:S(2)}) async-start(f32[1,16,8,2048]{3,2,0,1:T(8,128)} %copy.12), calls=%async_computation.1 | async-start | bytes 2097152 | tf_op jit(solution)/shard_map/all_to_all | solution.py:144
  88.5 1.2 %collective-permute-start.13 = (f32[4,7]{1,0:T(4,128)S(1)}, f32[4,7]{1,0:T(4,128)S(1)}, u32[]{:S(2)}, u32[]{:S(2)}) collective-permute-start(f32[4,7]{1,0:T(4,128)S(1)} %dynamic_update_slice.5), channel_id=1, source_target_pairs={{0,1},{1,0},{2,3},{3,2},{4,5},{5,4},{6,7},{7,6},{8,9},{9,8},{10,11... | collective-permute-start | bytes 344 | tf_op jit(solution)/shard_map/ppermute | solution.py:40
  90.4 3.6 %collective-permute-start.14 = (f32[4,7]{1,0:T(4,128)S(1)}, f32[4,7]{1,0:T(4,128)S(1)}, u32[]{:S(2)}, u32[]{:S(2)}) collective-permute-start(f32[4,7]{1,0:T(4,128)S(1)} %add.271), channel_id=1, source_target_pairs={{0,2},{1,3},{2,0},{3,1},{4,6},{5,7},{6,4},{7,5},{8,10},{9,11},{10,... | collective-permute-start | bytes 344 | tf_op jit(solution)/shard_map/ppermute | solution.py:40
  94.0 4.5 %collective-permute-start.15 = (f32[4,7]{1,0:T(4,128)S(1)}, f32[4,7]{1,0:T(4,128)S(1)}, u32[]{:S(2)}, u32[]{:S(2)}) collective-permute-start(f32[4,7]{1,0:T(4,128)S(1)} %add.272), channel_id=1, source_target_pairs={{0,4},{1,5},{2,6},{3,7},{4,0},{5,1},{6,2},{7,3},{8,12},{9,13},{10,... | collective-permute-start | bytes 344 | tf_op jit(solution)/shard_map/ppermute | solution.py:40
  98.5 3.6 %collective-permute-start.16 = (f32[4,7]{1,0:T(4,128)S(1)}, f32[4,7]{1,0:T(4,128)S(1)}, u32[]{:S(2)}, u32[]{:S(2)}) collective-permute-start(f32[4,7]{1,0:T(4,128)S(1)} %add.273), channel_id=1, source_target_pairs={{0,8},{8,0},{16,24},{24,16},{1,9},{9,1},{17,25},{25,17},{2,10},{10... | collective-permute-start | bytes 344 | tf_op jit(solution)/shard_map/ppermute | solution.py:40
  102.1 3.6 %collective-permute-start.17 = (f32[4,7]{1,0:T(4,128)S(1)}, f32[4,7]{1,0:T(4,128)S(1)}, u32[]{:S(2)}, u32[]{:S(2)}) collective-permute-start(f32[4,7]{1,0:T(4,128)S(1)} %add.274), channel_id=1, source_target_pairs={{0,16},{8,24},{16,0},{24,8},{1,17},{9,25},{17,1},{25,9},{2,18},{10... | collective-permute-start | bytes 344 | tf_op jit(solution)/shard_map/ppermute | solution.py:40
  105.7 2.2 %copy-start.3 = (f32[4,7]{1,0:T(4,128)}, f32[4,7]{1,0:T(4,128)S(1)}, u32[]{:S(2)}) copy-start(f32[4,7]{1,0:T(4,128)S(1)} %add.275) | copy-start | bytes 340

commit v3 on v2

--- a/solution.py
+++ b/solution.py
@@ -94,6 +94,9 @@
     def own(x, off):
         return x[:, :, h - off : h - off + rows]
 
+    def lanes(v):
+        return lax.optimization_barrier(jnp.broadcast_to(v[:, :, None], v.shape + (128,)))
+
     def crop(x, k):
         return x[:, :, k : x.shape[2] - k]
 
@@ -104,8 +107,11 @@
     az = apply_a(z, 0)
     z2 = crop(z, 2)
     sums, aaz = reduce_tile([(z2, z2), (az, z2)], 2, a_stages(az, 2))
-    norm = jnp.sqrt(sums[:, 0] + epsilon)
-    alpha = sums[:, 1] / (norm * norm)
+    sv = lanes(sums)
+    norm_v = jnp.sqrt(sv[:, 0] + epsilon)
+    alpha_v = sv[:, 1] / (norm_v * norm_v)
+    norm = norm_v[:, 0]
+    alpha = alpha_v[:, 0]
     q = z2 / norm[:, None, None, None]
     aq = az / norm[:, None, None, None]
     w = aq - alpha[:, None, None, None] * q
@@ -120,8 +126,11 @@
     for step in range(1, iters):
         last_step = step == iters - 1
         sums, aaw = reduce_tile([(w, w), (aw, w), (q, w)], off, () if last_step else a_stages(aw, off))
-        beta = jnp.sqrt(sums[:, 0] + epsilon)
-        alpha = sums[:, 1] / (beta * beta) - sums[:, 2]
+        sv = lanes(sums)
+        beta_v = jnp.sqrt(sv[:, 0] + epsilon)
+        alpha_v = sv[:, 1] / (beta_v * beta_v) - sv[:, 2]
+        beta = beta_v[:, 0]
+        alpha = alpha_v[:, 0]
         q_next = w / beta[:, None, None, None]
         w_next = aw / beta[:, None, None, None] - beta[:, None, None, None] * q - alpha[:, None, None, None] * q_next
         if not last_step:
@@ -153,8 +162,7 @@
         mine,
         (lax.axis_index("trait") * probes_local, 0),
     )
-    scalars = butterfly_sum(spread, "tile")[0]
-    scalars = butterfly_sum(scalars, "trait")[0]
+    scalars = butterfly_sum(butterfly_sum(spread, "tile")[0], "trait")[0]
     beta = jnp.sqrt(scalars[:, 2 * iters - 1] + epsilon)
     norm_all = scalars[:, 2 * iters]
     last = (w_back / beta[:, None, None, None]) * norm_all[:, None, None, None]

time: 108 us -> 102 us (0.944)
  between operations: 6.37 us -> 1.19 us
  local copies, waits for them, and re-layouts: 5.29 us -> 3.76 us
    slice x3 -> x0, local copies, waits for them, and re-layouts: 1.79 us -> none  [the longest x2 1.21 us: shards(): alpha = sums[:, 1] / (beta * beta) - sums[:, 2]]
  transfers between devices with their start and end apart: 20 -> 20, of which waited for: 13 -> 13; matrix products, arithmetic and copies ran while one was open for 15% -> 16% of each run, Pallas kernels for 0% -> 0%
where the time goes in v3:
time: 102 us
  starting transfers between devices  36.9 us (36%)
  waiting for transfers between devices  26 us (25%)
  other arithmetic  21.4 us (21%)
  matrix products  12.4 us (12%)
  local copies, waits for them, and re-layouts  3.76 us (4%)
  between operations  1.19 us (1%)
    ppermute x14, starting transfers between devices, butterfly_sum(): got = lax.ppermute(v, axis, [(i, i ^ s) for i in range(n)])  26.7 us
    ppermute x14, waiting for transfers between devices, butterfly_sum(): got = lax.ppermute(v, axis, [(i, i ^ s) for i in range(n)])  18.6 us
    dot_general x3, matrix products, mix(): jnp.einsum('ts,psrc->ptrc', trait_covariance, x, precision=lax.Precision....  12.4 us
    mul x3, other arithmetic, stencil(): land_ext[off + 1:off + r - 1]  9.99 us
    all_to_all x1, waiting for transfers between devices, shards(): lax.all_to_all(signed, 'trait', split_axis=0, concat_axis=1, tiled=True)  6.36 us
    all_to_all x1, starting transfers between devices, shards(): lax.all_to_all(signed, 'trait', split_axis=0, concat_axis=1, tiled=True)  5.19 us
    all_to_all x1, starting transfers between devices, shards(): lax.all_to_all(w_own, 'trait', split_axis=1, concat_axis=0, tiled=True)  3.52 us
    convert_element_type x1, other arithmetic, shards(): (land_mask[None, None] * (2 * probe_signs - 1)).astype(jnp.bfloat16)  2.22 us
  transfers between devices with their start and end apart: 20, of which 13 were waited for; matrix products, arithmetic and copies ran while one was open for 16% of the time, Pallas kernels for 0%

profile of v3, /device:TPU:0, one launch (start us, length us, event | category | flops | bytes accessed | tf_op | source)
XLA Modules:
  0.0 101.6 jit_solution(10261278362942862919)
XLA Ops:
  0.7 2.2 %multiply_convert_fusion = bf16[4,4,8,2048]{3,2,1,0:T(8,128)(2,1)} fusion(s32[4,4,8,2048]{3,2,1,0:T(8,128)} %param.4, s32[8,2048]{1,0:T(8,128)} %param.5), kind=kLoop, calls=%fused_computation.163 | loop fusion | flops 1048576 | bytes 1638400 | tf_op jit(solution)/shard_map/convert_element_type | solution.py:73
  2.9 5.2 %all-to-all-start = ((bf16[4,4,8,2048]{3,2,1,0:T(8,128)(2,1)}), bf16[4,4,8,2048]{3,2,1,0:T(8,128)(2,1)S(1)}, u32[]{:S(2)}, u32[]{:S(2)}) async-start(bf16[4,4,8,2048]{3,2,1,0:T(8,128)(2,1)} %multiply_convert_fusion), calls=%async_computation | async-start | bytes 1048576 | tf_op jit(solution)/shard_map/all_to_all | solution.py:74
  9.7 6.4 %all-to-all-done = bf16[4,4,8,2048]{3,2,1,0:T(8,128)(2,1)S(1)} async-done(((bf16[4,4,8,2048]{3,2,1,0:T(8,128)(2,1)}), bf16[4,4,8,2048]{3,2,1,0:T(8,128)(2,1)S(1)}, u32[]{:S(2)}, u32[]{:S(2)}) %all-to-all-start) | async-done | bytes 524320 | tf_op jit(solution)/shard_map/all_to_all | solution.py:74
  19.4 4.4 %fusion.5 = f32[1,16,18,2048]{3,1,2,0:T(8,128)S(1)} fusion(f32[1,16,20,2048]{3,1,2,0:T(8,128)S(1)} %broadcast_multiply_fusion, f32[18,2048]{1,0:T(8,128)S(1)} %slice_add_fusion.4, f32[18,2048]{1,0:T(8,128)S(1)} %bitcast.121), kind=kLoop, calls=%fused_computation.17 | loop fusion | flops 7667712 | bytes 12451840 | tf_op jit(solution)/shard_map/mul | solution.py:86
  23.8 5.6 %convolution_bitcast_fusion = f32[1,16,16,2048]{3,1,2,0:T(8,128)S(1)} fusion(f32[1,16,18,2048]{3,1,2,0:T(8,128)S(1)} %fusion.5, f32[16,2048]{1,0:T(8,128)S(1)} %slice_add_fusion.8, f32[16,2048]{1,0:T(8,128)S(1)} %bitcast.125, f32[16,16]{1,0:T(8,128)S(1)} %copy-done), kind=kOutput, calls=%fused_computation.3 | convolution fusion | flops 107479040 | bytes 11018240 | tf_op jit(solution)/shard_map/ts,psrc->ptrc/dot_general | solution.py:82
  30.0 7.9 %collective-permute-start.4 = (f32[1,2]{1,0:T(1,128)S(1)}, f32[1,2]{1,0:T(1,128)S(1)}, u32[]{:S(2)}, u32[]{:S(2)}) collective-permute-start(f32[1,2]{1,0:T(1,128)S(1)} %bitcast.145), channel_id=1, source_target_pairs={{0,1},{1,0},{2,3},{3,2},{4,5},{5,4},{6,7},{7,6},{8,9},{9,8},{10,11... | collective-permute-start | bytes 32 | tf_op jit(solution)/shard_map/ppermute | solution.py:40
  38.0 3.5 %fusion.33 = f32[1,16,14,2048]{3,1,2,0:T(8,128)S(1)} fusion(f32[1,16,16,2048]{3,1,2,0:T(8,128)S(1)} %convolution_bitcast_fusion, f32[14,2048]{1,0:T(8,128)S(1)} %slice_add_fusion.7, f32[14,2048]{1,0:T(8,128)S(1)} %bitcast.123), kind=kLoop, calls=%fused_computation.60 | loop fusion | flops 5963776 | bytes 9699328 | tf_op jit(solution)/shard_map/mul | solution.py:86
  41.5 1.7 %collective-permute-start.5 = (f32[1,2]{1,0:T(1,128)S(1)}, f32[1,2]{1,0:T(1,128)S(1)}, u32[]{:S(2)}, u32[]{:S(2)}) collective-permute-start(f32[1,2]{1,0:T(1,128)S(1)} %bitcast_add_fusion.2), channel_id=1, source_target_pairs={{0,2},{1,3},{2,0},{3,1},{4,6},{5,7},{6,4},{7,5},{8,10},{9,11},{10,... | collective-permute-start | bytes 32 | tf_op jit(solution)/shard_map/ppermute | solution.py:40
  43.2 4.3 %convolution_bitcast_fusion.1 = f32[1,16,12,2048]{3,1,2,0:T(8,128)S(1)} fusion(f32[1,16,14,2048]{3,1,2,0:T(8,128)S(1)} %fusion.33, f32[12,2048]{1,0:T(8,128)S(1)} %slice_add_fusion.6, f32[12,2048]{1,0:T(8,128)S(1)} %bitcast.124, f32[16,16]{1,0:T(8,128)S(1)} %copy-done), kind=kOutput, calls=%fused_computation.4 | convolution fusion | flops 80609280 | bytes 8396800 | tf_op jit(solution)/shard_map/ts,psrc->ptrc/dot_general | solution.py:82
  47.5 2.7 %collective-permute-start.6 = (f32[1,2]{1,0:T(1,128)S(1)}, f32[1,2]{1,0:T(1,128)S(1)}, u32[]{:S(2)}, u32[]{:S(2)}) collective-permute-start(f32[1,2]{1,0:T(1,128)S(1)} %add.277), channel_id=1, source_target_pairs={{0,4},{1,5},{2,6},{3,7},{4,0},{5,1},{6,2},{7,3},{8,12},{9,13},{10,... | collective-permute-start | bytes 32 | tf_op jit(solution)/shard_map/ppermute | solution.py:40
  50.2 1.9 %collective-permute-done.6 = f32[1,2]{1,0:T(1,128)S(1)} collective-permute-done((f32[1,2]{1,0:T(1,128)S(1)}, f32[1,2]{1,0:T(1,128)S(1)}, u32[]{:S(2)}, u32[]{:S(2)}) %collective-permute-start.6) | collective-permute-done | bytes 40 | tf_op jit(solution)/shard_map/ppermute | solution.py:40
  54.0 2.1 %fusion.65 = f32[1,16,10,2048]{3,1,2,0:T(8,128)S(1)} fusion(f32[1,16,12,2048]{3,1,2,0:T(8,128)S(1)} %fusion.53, f32[10,2048]{1,0:T(8,128)S(1)} %slice_add_fusion.5, f32[10,2048]{1,0:T(8,128)S(1)} %bitcast.122), kind=kLoop, calls=%fused_computation.105 | loop fusion | flops 4259840 | bytes 7077888 | tf_op jit(solution)/shard_map/mul | solution.py:86
  56.6 2.5 %convolution_bitcast_fusion.2 = f32[1,16,8,2048]{3,1,2,0:T(8,128)S(1)} fusion(f32[1,16,10,2048]{3,1,2,0:T(8,128)S(1)} %fusion.65, f32[8,2048]{1,0:T(8,128)S(1)} %broadcast_add_fusion, f32[8,2048]{1,0:T(8,128)S(1)} %bitcast.126, f32[16,16]{1,0:T(8,128)S(1)} %copy-done), kind=kOutput, calls=%fused_computation.5 | convolution fusion | flops 53739520 | bytes 5644288 | tf_op jit(solution)/shard_map/ts,psrc->ptrc/dot_general | solution.py:82
  59.8 2.6 %collective-permute-start.9 = (f32[1,3]{1,0:T(1,128)S(1)}, f32[1,3]{1,0:T(1,128)S(1)}, u32[]{:S(2)}, u32[]{:S(2)}) collective-permute-start(f32[1,3]{1,0:T(1,128)S(1)} %add.293), channel_id=1, source_target_pairs={{0,4},{1,5},{2,6},{3,7},{4,0},{5,1},{6,2},{7,3},{8,12},{9,13},{10,... | collective-permute-start | bytes 44 | tf_op jit(solution)/shard_map/ppermute | solution.py:40
  62.4 1.9 %collective-permute-done.9 = f32[1,3]{1,0:T(1,128)S(1)} collective-permute-done((f32[1,3]{1,0:T(1,128)S(1)}, f32[1,3]{1,0:T(1,128)S(1)}, u32[]{:S(2)}, u32[]{:S(2)}) %collective-permute-start.9) | collective-permute-done | bytes 44 | tf_op jit(solution)/shard_map/ppermute | solution.py:40
  65.9 1.1 %collective-permute-done.10 = f32[1,3]{1,0:T(1,128)S(1)} collective-permute-done((f32[1,3]{1,0:T(1,128)S(1)}, f32[1,3]{1,0:T(1,128)S(1)}, u32[]{:S(2)}, u32[]{:S(2)}) %collective-permute-start.10) | collective-permute-done | bytes 44 | tf_op jit(solution)/shard_map/ppermute | solution.py:40
  67.1 1.1 %collective-permute-start.11 = (f32[1,3]{1,0:T(1,128)S(1)}, f32[1,3]{1,0:T(1,128)S(1)}, u32[]{:S(2)}, u32[]{:S(2)}) collective-permute-start(f32[1,3]{1,0:T(1,128)S(1)} %bitcast_add_fusion), channel_id=1, source_target_pairs={{0,2},{1,3},{2,0},{3,1},{4,6},{5,7},{6,4},{7,5},{8,10},{9,11},{10,... | collective-permute-start | bytes 44 | tf_op jit(solution)/shard_map/ppermute | solution.py:40
  68.1 2.5 %collective-permute-done.11 = f32[1,3]{1,0:T(1,128)S(1)} collective-permute-done((f32[1,3]{1,0:T(1,128)S(1)}, f32[1,3]{1,0:T(1,128)S(1)}, u32[]{:S(2)}, u32[]{:S(2)}) %collective-permute-start.11) | collective-permute-done | bytes 44 | tf_op jit(solution)/shard_map/ppermute | solution.py:40
  70.6 2.6 %collective-permute-start.12 = (f32[1,3]{1,0:T(1,128)S(1)}, f32[1,3]{1,0:T(1,128)S(1)}, u32[]{:S(2)}, u32[]{:S(2)}) collective-permute-start(f32[1,3]{1,0:T(1,128)S(1)} %add.303), channel_id=1, source_target_pairs={{0,4},{1,5},{2,6},{3,7},{4,0},{5,1},{6,2},{7,3},{8,12},{9,13},{10,... | collective-permute-start | bytes 44 | tf_op jit(solution)/shard_map/ppermute | solution.py:40
  73.2 1.9 %collective-permute-done.12 = f32[1,3]{1,0:T(1,128)S(1)} collective-permute-done((f32[1,3]{1,0:T(1,128)S(1)}, f32[1,3]{1,0:T(1,128)S(1)}, u32[]{:S(2)}, u32[]{:S(2)}) %collective-permute-start.12) | collective-permute-done | bytes 44 | tf_op jit(solution)/shard_map/ppermute | solution.py:40
  76.1 1.6 %copy.12 = f32[1,16,8,2048]{3,2,0,1:T(8,128)} copy(f32[1,16,8,2048]{3,1,2,0:T(8,128)S(1)} %get-tuple-element.22) | data formatting | bytes 2097152 | tf_op jit(solution)/shard_map/sub | solution.py:135
  77.7 3.5 %all-to-all-start.1 = ((f32[1,16,8,2048]{3,2,0,1:T(8,128)}), f32[1,16,8,2048]{3,2,0,1:T(8,128)S(1)}, u32[]{:S(2)}, u32[]{:S(2)}) async-start(f32[1,16,8,2048]{3,2,0,1:T(8,128)} %copy.12), calls=%async_computation.1 | async-start | bytes 2097152 | tf_op jit(solution)/shard_map/all_to_all | solution.py:153
  82.3 1.1 %collective-permute-done.13 = f32[4,7]{1,0:T(4,128)S(1)} collective-permute-done((f32[4,7]{1,0:T(4,128)S(1)}, f32[4,7]{1,0:T(4,128)S(1)}, u32[]{:S(2)}, u32[]{:S(2)}) %collective-permute-start.13) | collective-permute-done | bytes 144 | tf_op jit(solution)/shard_map/ppermute | solution.py:40
  84.2 1.1 %collective-permute-start.14 = (f32[4,7]{1,0:T(4,128)S(1)}, f32[4,7]{1,0:T(4,128)S(1)}, u32[]{:S(2)}, u32[]{:S(2)}) collective-permute-start(f32[4,7]{1,0:T(4,128)S(1)} %add.307), channel_id=1, source_target_pairs={{0,2},{1,3},{2,0},{3,1},{4,6},{5,7},{6,4},{7,5},{8,10},{9,11},{10,... | collective-permute-start | bytes 344 | tf_op jit(solution)/shard_map/ppermute | solution.py:40
  85.3 2.5 %collective-permute-done.14 = f32[4,7]{1,0:T(4,128)S(1)} collective-permute-done((f32[4,7]{1,0:T(4,128)S(1)}, f32[4,7]{1,0:T(4,128)S(1)}, u32[]{:S(2)}, u32[]{:S(2)}) %collective-permute-start.14) | collective-permute-done | bytes 144 | tf_op jit(solution)/shard_map/ppermute | solution.py:40
  87.8 2.6 %collective-permute-start.15 = (f32[4,7]{1,0:T(4,128)S(1)}, f32[4,7]{1,0:T(4,128)S(1)}, u32[]{:S(2)}, u32[]{:S(2)}) collective-permute-start(f32[4,7]{1,0:T(4,128)S(1)} %add.308), channel_id=1, source_target_pairs={{0,4},{1,5},{2,6},{3,7},{4,0},{5,1},{6,2},{7,3},{8,12},{9,13},{10,... | collective-permute-start | bytes 344 | tf_op jit(solution)/shard_map/ppermute | solution.py:40
  90.4 1.9 %collective-permute-done.15 = f32[4,7]{1,0:T(4,128)S(1)} collective-permute-done((f32[4,7]{1,0:T(4,128)S(1)}, f32[4,7]{1,0:T(4,128)S(1)}, u32[]{:S(2)}, u32[]{:S(2)}) %collective-permute-start.15) | collective-permute-done | bytes 144 | tf_op jit(solution)/shard_map/ppermute | solution.py:40
  92.3 2.0 %collective-permute-start.16 = (f32[4,7]{1,0:T(4,128)S(1)}, f32[4,7]{1,0:T(4,128)S(1)}, u32[]{:S(2)}, u32[]{:S(2)}) collective-permute-start(f32[4,7]{1,0:T(4,128)S(1)} %add.309), channel_id=1, source_target_pairs={{0,8},{8,0},{16,24},{24,16},{1,9},{9,1},{17,25},{25,17},{2,10},{10... | collective-permute-start | bytes 344 | tf_op jit(solution)/shard_map/ppermute | solution.py:40
  94.3 1.6 %collective-permute-done.16 = f32[4,7]{1,0:T(4,128)S(1)} collective-permute-done((f32[4,7]{1,0:T(4,128)S(1)}, f32[4,7]{1,0:T(4,128)S(1)}, u32[]{:S(2)}, u32[]{:S(2)}) %collective-permute-start.16) | collective-permute-done | bytes 144 | tf_op jit(solution)/shard_map/ppermute | solution.py:40
  95.9 2.0 %collective-permute-start.17 = (f32[4,7]{1,0:T(4,128)S(1)}, f32[4,7]{1,0:T(4,128)S(1)}, u32[]{:S(2)}, u32[]{:S(2)}) collective-permute-start(f32[4,7]{1,0:T(4,128)S(1)} %add.310), channel_id=1, source_target_pairs={{0,16},{8,24},{16,0},{24,8},{1,17},{9,25},{17,1},{25,9},{2,18},{10... | collective-permute-start | bytes 344 | tf_op jit(solution)/shard_map/ppermute | solution.py:40
  97.9 1.6 %collective-permute-done.17 = f32[4,7]{1,0:T(4,128)S(1)} collective-permute-done((f32[4,7]{1,0:T(4,128)S(1)}, f32[4,7]{1,0:T(4,128)S(1)}, u32[]{:S(2)}, u32[]{:S(2)}) %collective-permute-start.17) | collective-permute-done | bytes 144 | tf_op jit(solution)/shard_map/ppermute | solution.py:40
  100.4 1.2 %divide_multiply_fusion = f32[4,4,8,2048]{3,2,1,0:T(8,128)} fusion(f32[4,4,8,2048]{3,2,1,0:T(8,128)S(1)} %bitcast.119, f32[4]{0:T(128)S(1)} %get-tuple-element.20, f32[4]{0:T(128)S(1)} %get-tuple-element.19), kind=kLoop, calls=%fused_computation.142 | loop fusion | flops 524288 | bytes 2097184 | tf_op jit(solution)/shard_map/mul | solution.py:168
  (102 shorter events, 13.8 us)
Async XLA Ops:
  0.6 8.2 %copy-start = (f32[16,16]{1,0:T(8,128)S(1)}, f32[16,16]{1,0:T(8,128)}, u32[]{:S(2)}) copy-start(f32[16,16]{1,0:T(8,128)} %param.7) | copy-start | bytes 3076
  0.6 7.4 %copy-start.2 = (f32[8,2048]{1,0:T(8,128)S(1)}, f32[8,2048]{1,0:T(8,128)}, u32[]{:S(2)}) copy-start(f32[8,2048]{1,0:T(8,128)} %param.6) | copy-start | bytes 196612
  2.9 13.2 %all-to-all-start = ((bf16[4,4,8,2048]{3,2,1,0:T(8,128)(2,1)}), bf16[4,4,8,2048]{3,2,1,0:T(8,128)(2,1)S(1)}, u32[]{:S(2)}, u32[]{:S(2)}) async-start(bf16[4,4,8,2048]{3,2,1,0:T(8,128)(2,1)} %multiply_convert_fusion), calls=%async_computation | async-start | bytes 1048576 | tf_op jit(solution)/shard_map/all_to_all | solution.py:74
  8.1 1.5 %collective-permute-start.2 = (f32[6,2048]{1,0:T(8,128)S(1)}, f32[6,2048]{1,0:T(8,128)S(1)}, u32[]{:S(2)}, u32[]{:S(2)}) collective-permute-start(f32[6,2048]{1,0:T(8,128)S(1)} %get-tuple-element.42), channel_id=1, source_target_pairs={{0,1},{2,3},{4,5},{6,7},{1,0},{3,2},{5,4},{7,6},{8,9},{10,11},{12,... | collective-permute-start | bytes 147464 | tf_op jit(solution)/shard_map/ppermute | solution.py:64
  8.2 1.4 %collective-permute-start.3 = (f32[6,2048]{1,0:T(8,128)S(1)}, f32[6,2048]{1,0:T(8,128)S(1)}, u32[]{:S(2)}, u32[]{:S(2)}) collective-permute-start(f32[6,2048]{1,0:T(8,128)S(1)} %get-tuple-element.43), channel_id=1, source_target_pairs={{1,2},{3,4},{5,6},{2,1},{4,3},{6,5},{9,10},{11,12},{13,14},{10,9},... | collective-permute-start | bytes 147464 | tf_op jit(solution)/shard_map/ppermute | solution.py:63
  16.4 1.8 %collective-permute-start = (bf16[1,16,6,2048]{3,1,2,0:T(8,128)(2,1)S(1)}, bf16[1,16,6,2048]{3,1,2,0:T(8,128)(2,1)S(1)}, u32[]{:S(2)}, u32[]{:S(2)}) collective-permute-start(bf16[1,16,6,2048]{3,1,2,0:T(8,128)(2,1)S(1)} %get-tuple-element.38), channel_id=1, source_target_pairs={{0,1},{2,3},{4,5},{6,7},{1,0},{3,2},{5,4},{7,6},{8,9},{10,11},{12,... | collective-permute-start | bytes 1179656 | tf_op jit(solution)/shard_map/ppermute | solution.py:64
  16.5 1.7 %collective-permute-start.1 = (bf16[1,16,6,2048]{3,1,2,0:T(8,128)(2,1)S(1)}, bf16[1,16,6,2048]{3,1,2,0:T(8,128)(2,1)S(1)}, u32[]{:S(2)}, u32[]{:S(2)}) collective-permute-start(bf16[1,16,6,2048]{3,1,2,0:T(8,128)(2,1)S(1)} %get-tuple-element.39), channel_id=1, source_target_pairs={{1,2},{3,4},{5,6},{2,1},{4,3},{6,5},{9,10},{11,12},{13,14},{10,9},... | collective-permute-start | bytes 1179656 | tf_op jit(solution)/shard_map/ppermute | solution.py:63
  18.6 0.7 copy-start.1
  29.5 8.3 %slice-start = ((f32[1,1,20,2048]{3,1,2,0:T(1,128)}), f32[1,1,14,2048]{3,1,2,0:T(1,128)S(1)}, s32[]{:S(2)}) async-start(f32[1,1,20,2048]{3,1,2,0:T(1,128)} %copy-done.1), calls=%async_computation.2 | async-start | bytes 229376 | tf_op jit(solution)/shard_map/slice | solution.py:86
  29.6 8.3 %slice-start.1 = ((f32[1,1,20,2048]{3,1,2,0:T(1,128)}), f32[1,1,12,2048]{3,1,2,0:T(1,128)S(1)}, s32[]{:S(2)}) async-start(f32[1,1,20,2048]{3,1,2,0:T(1,128)} %copy-done.1), calls=%async_computation.3 | async-start | bytes 196608 | tf_op jit(solution)/shard_map/slice | solution.py:86
  29.6 8.4 %slice-start.2 = ((f32[1,1,20,2048]{3,1,2,0:T(1,128)}), f32[1,1,10,2048]{3,1,2,0:T(1,128)S(1)}, s32[]{:S(2)}) async-start(f32[1,1,20,2048]{3,1,2,0:T(1,128)} %copy-done.1), calls=%async_computation.4 | async-start | bytes 163840 | tf_op jit(solution)/shard_map/slice | solution.py:86
  29.6 8.4 %slice-start.3 = ((f32[1,1,20,2048]{3,1,2,0:T(1,128)}), f32[1,1,8,2048]{3,1,2,0:T(1,128)S(1)}, s32[]{:S(2)}) async-start(f32[1,1,20,2048]{3,1,2,0:T(1,128)} %copy-done.1), calls=%async_computation.5 | async-start | bytes 131072 | tf_op jit(solution)/shard_map/slice | solution.py:86
  30.0 11.6 %collective-permute-start.4 = (f32[1,2]{1,0:T(1,128)S(1)}, f32[1,2]{1,0:T(1,128)S(1)}, u32[]{:S(2)}, u32[]{:S(2)}) collective-permute-start(f32[1,2]{1,0:T(1,128)S(1)} %bitcast.145), channel_id=1, source_target_pairs={{0,1},{1,0},{2,3},{3,2},{4,5},{5,4},{6,7},{7,6},{8,9},{9,8},{10,11... | collective-permute-start | bytes 32 | tf_op jit(solution)/shard_map/ppermute | solution.py:40
  41.5 6.0 %collective-permute-start.5 = (f32[1,2]{1,0:T(1,128)S(1)}, f32[1,2]{1,0:T(1,128)S(1)}, u32[]{:S(2)}, u32[]{:S(2)}) collective-permute-start(f32[1,2]{1,0:T(1,128)S(1)} %bitcast_add_fusion.2), channel_id=1, source_target_pairs={{0,2},{1,3},{2,0},{3,1},{4,6},{5,7},{6,4},{7,5},{8,10},{9,11},{10,... | collective-permute-start | bytes 32 | tf_op jit(solution)/shard_map/ppermute | solution.py:40
  47.5 4.5 %collective-permute-start.6 = (f32[1,2]{1,0:T(1,128)S(1)}, f32[1,2]{1,0:T(1,128)S(1)}, u32[]{:S(2)}, u32[]{:S(2)}) collective-permute-start(f32[1,2]{1,0:T(1,128)S(1)} %add.277), channel_id=1, source_target_pairs={{0,4},{1,5},{2,6},{3,7},{4,0},{5,1},{6,2},{7,3},{8,12},{9,13},{10,... | collective-permute-start | bytes 32 | tf_op jit(solution)/shard_map/ppermute | solution.py:40
  54.0 2.1 %collective-permute-start.7 = (f32[1,3]{1,0:T(1,128)S(1)}, f32[1,3]{1,0:T(1,128)S(1)}, u32[]{:S(2)}, u32[]{:S(2)}) collective-permute-start(f32[1,3]{1,0:T(1,128)S(1)} %bitcast.146), channel_id=1, source_target_pairs={{0,1},{1,0},{2,3},{3,2},{4,5},{5,4},{6,7},{7,6},{8,9},{9,8},{10,11... | collective-permute-start | bytes 44 | tf_op jit(solution)/shard_map/ppermute | solution.py:40
  56.1 3.6 %collective-permute-start.8 = (f32[1,3]{1,0:T(1,128)S(1)}, f32[1,3]{1,0:T(1,128)S(1)}, u32[]{:S(2)}, u32[]{:S(2)}) collective-permute-start(f32[1,3]{1,0:T(1,128)S(1)} %bitcast_add_fusion.1), channel_id=1, source_target_pairs={{0,2},{1,3},{2,0},{3,1},{4,6},{5,7},{6,4},{7,5},{8,10},{9,11},{10,... | collective-permute-start | bytes 44 | tf_op jit(solution)/shard_map/ppermute | solution.py:40
  59.8 4.5 %collective-permute-start.9 = (f32[1,3]{1,0:T(1,128)S(1)}, f32[1,3]{1,0:T(1,128)S(1)}, u32[]{:S(2)}, u32[]{:S(2)}) collective-permute-start(f32[1,3]{1,0:T(1,128)S(1)} %add.293), channel_id=1, source_target_pairs={{0,4},{1,5},{2,6},{3,7},{4,0},{5,1},{6,2},{7,3},{8,12},{9,13},{10,... | collective-permute-start | bytes 44 | tf_op jit(solution)/shard_map/ppermute | solution.py:40
  65.9 1.2 %collective-permute-start.10 = (f32[1,3]{1,0:T(1,128)S(1)}, f32[1,3]{1,0:T(1,128)S(1)}, u32[]{:S(2)}, u32[]{:S(2)}) collective-permute-start(f32[1,3]{1,0:T(1,128)S(1)} %bitcast.147), channel_id=1, source_target_pairs={{0,1},{1,0},{2,3},{3,2},{4,5},{5,4},{6,7},{7,6},{8,9},{9,8},{10,11... | collective-permute-start | bytes 44 | tf_op jit(solution)/shard_map/ppermute | solution.py:40
  67.1 3.6 %collective-permute-start.11 = (f32[1,3]{1,0:T(1,128)S(1)}, f32[1,3]{1,0:T(1,128)S(1)}, u32[]{:S(2)}, u32[]{:S(2)}) collective-permute-start(f32[1,3]{1,0:T(1,128)S(1)} %bitcast_add_fusion), channel_id=1, source_target_pairs={{0,2},{1,3},{2,0},{3,1},{4,6},{5,7},{6,4},{7,5},{8,10},{9,11},{10,... | collective-permute-start | bytes 44 | tf_op jit(solution)/shard_map/ppermute | solution.py:40
  70.6 4.5 %collective-permute-start.12 = (f32[1,3]{1,0:T(1,128)S(1)}, f32[1,3]{1,0:T(1,128)S(1)}, u32[]{:S(2)}, u32[]{:S(2)}) collective-permute-start(f32[1,3]{1,0:T(1,128)S(1)} %add.303), channel_id=1, source_target_pairs={{0,4},{1,5},{2,6},{3,7},{4,0},{5,1},{6,2},{7,3},{8,12},{9,13},{10,... | collective-permute-start | bytes 44 | tf_op jit(solution)/shard_map/ppermute | solution.py:40
  77.7 22.7 %all-to-all-start.1 = ((f32[1,16,8,2048]{3,2,0,1:T(8,128)}), f32[1,16,8,2048]{3,2,0,1:T(8,128)S(1)}, u32[]{:S(2)}, u32[]{:S(2)}) async-start(f32[1,16,8,2048]{3,2,0,1:T(8,128)} %copy.12), calls=%async_computation.1 | async-start | bytes 2097152 | tf_op jit(solution)/shard_map/all_to_all | solution.py:153
  82.2 1.2 %collective-permute-start.13 = (f32[4,7]{1,0:T(4,128)S(1)}, f32[4,7]{1,0:T(4,128)S(1)}, u32[]{:S(2)}, u32[]{:S(2)}) collective-permute-start(f32[4,7]{1,0:T(4,128)S(1)} %dynamic_update_slice.5), channel_id=1, source_target_pairs={{0,1},{1,0},{2,3},{3,2},{4,5},{5,4},{6,7},{7,6},{8,9},{9,8},{10,11... | collective-permute-start | bytes 344 | tf_op jit(solution)/shard_map/ppermute | solution.py:40
  84.2 3.6 %collective-permute-start.14 = (f32[4,7]{1,0:T(4,128)S(1)}, f32[4,7]{1,0:T(4,128)S(1)}, u32[]{:S(2)}, u32[]{:S(2)}) collective-permute-start(f32[4,7]{1,0:T(4,128)S(1)} %add.307), channel_id=1, source_target_pairs={{0,2},{1,3},{2,0},{3,1},{4,6},{5,7},{6,4},{7,5},{8,10},{9,11},{10,... | collective-permute-start | bytes 344 | tf_op jit(solution)/shard_map/ppermute | solution.py:40
  87.8 4.5 %collective-permute-start.15 = (f32[4,7]{1,0:T(4,128)S(1)}, f32[4,7]{1,0:T(4,128)S(1)}, u32[]{:S(2)}, u32[]{:S(2)}) collective-permute-start(f32[4,7]{1,0:T(4,128)S(1)} %add.308), channel_id=1, source_target_pairs={{0,4},{1,5},{2,6},{3,7},{4,0},{5,1},{6,2},{7,3},{8,12},{9,13},{10,... | collective-permute-start | bytes 344 | tf_op jit(solution)/shard_map/ppermute | solution.py:40
  92.3 3.6 %collective-permute-start.16 = (f32[4,7]{1,0:T(4,128)S(1)}, f32[4,7]{1,0:T(4,128)S(1)}, u32[]{:S(2)}, u32[]{:S(2)}) collective-permute-start(f32[4,7]{1,0:T(4,128)S(1)} %add.309), channel_id=1, source_target_pairs={{0,8},{8,0},{16,24},{24,16},{1,9},{9,1},{17,25},{25,17},{2,10},{10... | collective-permute-start | bytes 344 | tf_op jit(solution)/shard_map/ppermute | solution.py:40
  95.9 3.6 %collective-permute-start.17 = (f32[4,7]{1,0:T(4,128)S(1)}, f32[4,7]{1,0:T(4,128)S(1)}, u32[]{:S(2)}, u32[]{:S(2)}) collective-permute-start(f32[4,7]{1,0:T(4,128)S(1)} %add.310), channel_id=1, source_target_pairs={{0,16},{8,24},{16,0},{24,8},{1,17},{9,25},{17,1},{25,9},{2,18},{10... | collective-permute-start | bytes 344 | tf_op jit(solution)/shard_map/ppermute | solution.py:40
  99.5 2.2 %copy-start.3 = (f32[4,7]{1,0:T(4,128)}, f32[4,7]{1,0:T(4,128)S(1)}, u32[]{:S(2)}) copy-start(f32[4,7]{1,0:T(4,128)S(1)} %add.311) | copy-start | bytes 340

commit v4 on v3

--- a/solution.py
+++ b/solution.py
@@ -162,7 +162,11 @@
         mine,
         (lax.axis_index("trait") * probes_local, 0),
     )
-    scalars = butterfly_sum(butterfly_sum(spread, "tile")[0], "trait")[0]
+    scalars = butterfly_sum(spread, "tile")[0]
+    n_t = lax.axis_size("trait")
+    shifted = [lax.ppermute(scalars, "trait", [(i, (i + d) % n_t) for i in range(n_t)]) for d in range(1, n_t)]
+    for got in shifted:
+        scalars = scalars + got
     beta = jnp.sqrt(scalars[:, 2 * iters - 1] + epsilon)
     norm_all = scalars[:, 2 * iters]
     last = (w_back / beta[:, None, None, None]) * norm_all[:, None, None, None]

time: 102 us -> 105 us (1.029)
  other arithmetic: 21.4 us -> 23.5 us
    ppermute x14 -> x12, starting transfers between devices: 26.7 us -> 22.7 us  [butterfly_sum(): got = lax.ppermute(v, axis, [(i, i ^ s) for i in range(n)])]
    ppermute x0 -> x3, starting transfers between devices: none -> 4 us  [shards(): lax.ppermute(scalars, 'trait', [(i, (i + d) % n_t) for i in range(n_t)])]
    ppermute x0 -> x3, waiting for transfers between devices: none -> 3.92 us  [shards(): lax.ppermute(scalars, 'trait', [(i, (i + d) % n_t) for i in range(n_t)])]
    ppermute x14 -> x12, waiting for transfers between devices: 18.6 us -> 15.5 us  [butterfly_sum(): got = lax.ppermute(v, axis, [(i, i ^ s) for i in range(n)])]
    reduce_sum x1, other arithmetic: 0.93 us -> 2.14 us  [shards(): partial = jnp.sum(w_own * w_own, axis=(1, 2, 3))[:, None]]
  transfers between devices with their start and end apart: 20 -> 21, of which waited for: 13 -> 14; matrix products, arithmetic and copies ran while one was open for 16% -> 15% of each run, Pallas kernels for 0% -> 0%
where the time goes in v4:
time: 105 us
  starting transfers between devices  36.9 us (35%)
  waiting for transfers between devices  26.7 us (25%)
  other arithmetic  23.5 us (22%)
  matrix products  12.3 us (12%)
  local copies, waits for them, and re-layouts  3.77 us (4%)
  between operations  1.2 us (1%)
    ppermute x12, starting transfers between devices, butterfly_sum(): got = lax.ppermute(v, axis, [(i, i ^ s) for i in range(n)])  22.7 us
    ppermute x12, waiting for transfers between devices, butterfly_sum(): got = lax.ppermute(v, axis, [(i, i ^ s) for i in range(n)])  15.5 us
    dot_general x3, matrix products, mix(): jnp.einsum('ts,psrc->ptrc', trait_covariance, x, precision=lax.Precision....  12.3 us
    mul x3, other arithmetic, stencil(): land_ext[off + 1:off + r - 1]  9.94 us
    all_to_all x1, waiting for transfers between devices, shards(): lax.all_to_all(signed, 'trait', split_axis=0, concat_axis=1, tiled=True)  6.35 us
    all_to_all x1, starting transfers between devices, shards(): lax.all_to_all(signed, 'trait', split_axis=0, concat_axis=1, tiled=True)  5.19 us
    ppermute x3, starting transfers between devices, shards(): lax.ppermute(scalars, 'trait', [(i, (i + d) % n_t) for i in range(n_t)])  4 us
    ppermute x3, waiting for transfers between devices, shards(): lax.ppermute(scalars, 'trait', [(i, (i + d) % n_t) for i in range(n_t)])  3.92 us
  transfers between devices with their start and end apart: 21, of which 14 were waited for; matrix products, arithmetic and copies ran while one was open for 15% of the time, Pallas kernels for 0%

profile of v4, /device:TPU:0, one launch (start us, length us, event | category | flops | bytes accessed | tf_op | source)
XLA Modules:
  0.0 104.5 jit_solution(7398598607968214989)
XLA Ops:
  0.7 2.2 %multiply_convert_fusion = bf16[4,4,8,2048]{3,2,1,0:T(8,128)(2,1)} fusion(s32[4,4,8,2048]{3,2,1,0:T(8,128)} %param.4, s32[8,2048]{1,0:T(8,128)} %param.5), kind=kLoop, calls=%fused_computation.163 | loop fusion | flops 1048576 | bytes 1638400 | tf_op jit(solution)/shard_map/convert_element_type | solution.py:73
  2.9 5.2 %all-to-all-start = ((bf16[4,4,8,2048]{3,2,1,0:T(8,128)(2,1)}), bf16[4,4,8,2048]{3,2,1,0:T(8,128)(2,1)S(1)}, u32[]{:S(2)}, u32[]{:S(2)}) async-start(bf16[4,4,8,2048]{3,2,1,0:T(8,128)(2,1)} %multiply_convert_fusion), calls=%async_computation | async-start | bytes 1048576 | tf_op jit(solution)/shard_map/all_to_all | solution.py:74
  9.7 6.3 %all-to-all-done = bf16[4,4,8,2048]{3,2,1,0:T(8,128)(2,1)S(1)} async-done(((bf16[4,4,8,2048]{3,2,1,0:T(8,128)(2,1)}), bf16[4,4,8,2048]{3,2,1,0:T(8,128)(2,1)S(1)}, u32[]{:S(2)}, u32[]{:S(2)}) %all-to-all-start) | async-done | bytes 524320 | tf_op jit(solution)/shard_map/all_to_all | solution.py:74
  19.4 4.4 %fusion.5 = f32[1,16,18,2048]{3,1,2,0:T(8,128)S(1)} fusion(f32[1,16,20,2048]{3,1,2,0:T(8,128)S(1)} %broadcast_multiply_fusion, f32[18,2048]{1,0:T(8,128)S(1)} %slice_add_fusion.4, f32[18,2048]{1,0:T(8,128)S(1)} %bitcast.121), kind=kLoop, calls=%fused_computation.17 | loop fusion | flops 7667712 | bytes 12451840 | tf_op jit(solution)/shard_map/mul | solution.py:86
  23.7 5.5 %convolution_bitcast_fusion = f32[1,16,16,2048]{3,1,2,0:T(8,128)S(1)} fusion(f32[1,16,18,2048]{3,1,2,0:T(8,128)S(1)} %fusion.5, f32[16,2048]{1,0:T(8,128)S(1)} %slice_add_fusion.8, f32[16,2048]{1,0:T(8,128)S(1)} %bitcast.125, f32[16,16]{1,0:T(8,128)S(1)} %copy-done), kind=kOutput, calls=%fused_computation.3 | convolution fusion | flops 107479040 | bytes 11018240 | tf_op jit(solution)/shard_map/ts,psrc->ptrc/dot_general | solution.py:82
  29.9 7.9 %collective-permute-start.4 = (f32[1,2]{1,0:T(1,128)S(1)}, f32[1,2]{1,0:T(1,128)S(1)}, u32[]{:S(2)}, u32[]{:S(2)}) collective-permute-start(f32[1,2]{1,0:T(1,128)S(1)} %bitcast.145), channel_id=1, source_target_pairs={{0,1},{1,0},{2,3},{3,2},{4,5},{5,4},{6,7},{7,6},{8,9},{9,8},{10,11... | collective-permute-start | bytes 32 | tf_op jit(solution)/shard_map/ppermute | solution.py:40
  38.0 3.5 %fusion.33 = f32[1,16,14,2048]{3,1,2,0:T(8,128)S(1)} fusion(f32[1,16,16,2048]{3,1,2,0:T(8,128)S(1)} %convolution_bitcast_fusion, f32[14,2048]{1,0:T(8,128)S(1)} %slice_add_fusion.7, f32[14,2048]{1,0:T(8,128)S(1)} %bitcast.123), kind=kLoop, calls=%fused_computation.60 | loop fusion | flops 5963776 | bytes 9699328 | tf_op jit(solution)/shard_map/mul | solution.py:86
  41.5 1.7 %collective-permute-start.5 = (f32[1,2]{1,0:T(1,128)S(1)}, f32[1,2]{1,0:T(1,128)S(1)}, u32[]{:S(2)}, u32[]{:S(2)}) collective-permute-start(f32[1,2]{1,0:T(1,128)S(1)} %bitcast_add_fusion.2), channel_id=1, source_target_pairs={{0,2},{1,3},{2,0},{3,1},{4,6},{5,7},{6,4},{7,5},{8,10},{9,11},{10,... | collective-permute-start | bytes 32 | tf_op jit(solution)/shard_map/ppermute | solution.py:40
  43.2 4.3 %convolution_bitcast_fusion.1 = f32[1,16,12,2048]{3,1,2,0:T(8,128)S(1)} fusion(f32[1,16,14,2048]{3,1,2,0:T(8,128)S(1)} %fusion.33, f32[12,2048]{1,0:T(8,128)S(1)} %slice_add_fusion.6, f32[12,2048]{1,0:T(8,128)S(1)} %bitcast.124, f32[16,16]{1,0:T(8,128)S(1)} %copy-done), kind=kOutput, calls=%fused_computation.4 | convolution fusion | flops 80609280 | bytes 8396800 | tf_op jit(solution)/shard_map/ts,psrc->ptrc/dot_general | solution.py:82
  47.5 2.7 %collective-permute-start.6 = (f32[1,2]{1,0:T(1,128)S(1)}, f32[1,2]{1,0:T(1,128)S(1)}, u32[]{:S(2)}, u32[]{:S(2)}) collective-permute-start(f32[1,2]{1,0:T(1,128)S(1)} %add.280), channel_id=1, source_target_pairs={{0,4},{1,5},{2,6},{3,7},{4,0},{5,1},{6,2},{7,3},{8,12},{9,13},{10,... | collective-permute-start | bytes 32 | tf_op jit(solution)/shard_map/ppermute | solution.py:40
  50.1 1.9 %collective-permute-done.6 = f32[1,2]{1,0:T(1,128)S(1)} collective-permute-done((f32[1,2]{1,0:T(1,128)S(1)}, f32[1,2]{1,0:T(1,128)S(1)}, u32[]{:S(2)}, u32[]{:S(2)}) %collective-permute-start.6) | collective-permute-done | bytes 40 | tf_op jit(solution)/shard_map/ppermute | solution.py:40
  54.1 2.1 %fusion.65 = f32[1,16,10,2048]{3,1,2,0:T(8,128)S(1)} fusion(f32[1,16,12,2048]{3,1,2,0:T(8,128)S(1)} %fusion.53, f32[10,2048]{1,0:T(8,128)S(1)} %slice_add_fusion.5, f32[10,2048]{1,0:T(8,128)S(1)} %bitcast.122), kind=kLoop, calls=%fused_computation.105 | loop fusion | flops 4259840 | bytes 7077888 | tf_op jit(solution)/shard_map/mul | solution.py:86
  56.7 2.5 %convolution_bitcast_fusion.2 = f32[1,16,8,2048]{3,1,2,0:T(8,128)S(1)} fusion(f32[1,16,10,2048]{3,1,2,0:T(8,128)S(1)} %fusion.65, f32[8,2048]{1,0:T(8,128)S(1)} %broadcast_add_fusion, f32[8,2048]{1,0:T(8,128)S(1)} %bitcast.126, f32[16,16]{1,0:T(8,128)S(1)} %copy-done), kind=kOutput, calls=%fused_computation.5 | convolution fusion | flops 53739520 | bytes 5644288 | tf_op jit(solution)/shard_map/ts,psrc->ptrc/dot_general | solution.py:82
  59.9 2.6 %collective-permute-start.9 = (f32[1,3]{1,0:T(1,128)S(1)}, f32[1,3]{1,0:T(1,128)S(1)}, u32[]{:S(2)}, u32[]{:S(2)}) collective-permute-start(f32[1,3]{1,0:T(1,128)S(1)} %add.296), channel_id=1, source_target_pairs={{0,4},{1,5},{2,6},{3,7},{4,0},{5,1},{6,2},{7,3},{8,12},{9,13},{10,... | collective-permute-start | bytes 44 | tf_op jit(solution)/shard_map/ppermute | solution.py:40
  62.5 1.9 %collective-permute-done.9 = f32[1,3]{1,0:T(1,128)S(1)} collective-permute-done((f32[1,3]{1,0:T(1,128)S(1)}, f32[1,3]{1,0:T(1,128)S(1)}, u32[]{:S(2)}, u32[]{:S(2)}) %collective-permute-start.9) | collective-permute-done | bytes 44 | tf_op jit(solution)/shard_map/ppermute | solution.py:40
  65.0 1.5 %multiply_bitcast_fusion.1 = (f32[1,16,8,2048,1]{3,1,2,4,0:T(8,128)S(1)}, f32[1,16,8,2048]{3,1,2,0:T(8,128)}, f32[1,16,8,2048,1]{3,1,2,4,0:T(8,128)S(1)}) fusion(f32[1,16,8,2048]{3,1,2,0:T(8,128)S(1)} %get-tuple-element.24, f32[1,16,12,2048]{3,1,2,0:T(8,128)S(1)} %fusion.53, f32[]{:T(128)S(1)} %bitcast.129, f32[1,16,16,2048]{3,1,2,0:T(8,128)S(1)} %get-tuple-element.28, ...), kind=kLoop, calls=%fused_computation.146 | loop fusion | flops 2097152 | bytes 8388616 | tf_op jit(solution)/shard_map/stack | solution.py:104
  66.9 1.1 %collective-permute-done.10 = f32[1,3]{1,0:T(1,128)S(1)} collective-permute-done((f32[1,3]{1,0:T(1,128)S(1)}, f32[1,3]{1,0:T(1,128)S(1)}, u32[]{:S(2)}, u32[]{:S(2)}) %collective-permute-start.10) | collective-permute-done | bytes 44 | tf_op jit(solution)/shard_map/ppermute | solution.py:40
  69.1 2.5 %collective-permute-done.11 = f32[1,3]{1,0:T(1,128)S(1)} collective-permute-done((f32[1,3]{1,0:T(1,128)S(1)}, f32[1,3]{1,0:T(1,128)S(1)}, u32[]{:S(2)}, u32[]{:S(2)}) %collective-permute-start.11) | collective-permute-done | bytes 44 | tf_op jit(solution)/shard_map/ppermute | solution.py:40
  71.6 2.6 %collective-permute-start.12 = (f32[1,3]{1,0:T(1,128)S(1)}, f32[1,3]{1,0:T(1,128)S(1)}, u32[]{:S(2)}, u32[]{:S(2)}) collective-permute-start(f32[1,3]{1,0:T(1,128)S(1)} %add.306), channel_id=1, source_target_pairs={{0,4},{1,5},{2,6},{3,7},{4,0},{5,1},{6,2},{7,3},{8,12},{9,13},{10,... | collective-permute-start | bytes 44 | tf_op jit(solution)/shard_map/ppermute | solution.py:40
  74.2 1.9 %collective-permute-done.12 = f32[1,3]{1,0:T(1,128)S(1)} collective-permute-done((f32[1,3]{1,0:T(1,128)S(1)}, f32[1,3]{1,0:T(1,128)S(1)}, u32[]{:S(2)}, u32[]{:S(2)}) %collective-permute-start.12) | collective-permute-done | bytes 44 | tf_op jit(solution)/shard_map/ppermute | solution.py:40
  76.3 2.1 %multiply_reduce_fusion = (f32[]{:T(128)}, f32[1,16,8,2048]{3,1,2,0:T(8,128)S(1)}) fusion(f32[1,16,8,2048]{3,1,2,0:T(8,128)S(1)} %get-tuple-element.24, f32[]{:T(128)S(1)} %bitcast.139, f32[1,16,12,2048]{3,1,2,0:T(8,128)S(1)} %slice_divide_fusion.1, f32[1,16,8,2048]{3,1,2,0:T(8,128)} %get-tuple-element.26, f32[]{:T(128)S(1)} %bitcast.144), kind=kLoop, calls=%fused_computation.143 | loop fusion | flops 2097151 | bytes 4194316 | tf_op jit(solution)/shard_map/reduce_sum | solution.py:154
  78.5 1.6 %copy.12 = f32[1,16,8,2048]{3,2,0,1:T(8,128)} copy(f32[1,16,8,2048]{3,1,2,0:T(8,128)S(1)} %get-tuple-element.22) | data formatting | bytes 2097152 | tf_op jit(solution)/shard_map/sub | solution.py:135
  80.1 3.5 %all-to-all-start.1 = ((f32[1,16,8,2048]{3,2,0,1:T(8,128)}), f32[1,16,8,2048]{3,2,0,1:T(8,128)S(1)}, u32[]{:S(2)}, u32[]{:S(2)}) async-start(f32[1,16,8,2048]{3,2,0,1:T(8,128)} %copy.12), calls=%async_computation.1 | async-start | bytes 2097152 | tf_op jit(solution)/shard_map/all_to_all | solution.py:153
  84.4 1.1 %collective-permute-done.13 = f32[4,7]{1,0:T(4,128)S(1)} collective-permute-done((f32[4,7]{1,0:T(4,128)S(1)}, f32[4,7]{1,0:T(4,128)S(1)}, u32[]{:S(2)}, u32[]{:S(2)}) %collective-permute-start.13) | collective-permute-done | bytes 144 | tf_op jit(solution)/shard_map/ppermute | solution.py:40
  86.3 1.1 %collective-permute-start.14 = (f32[4,7]{1,0:T(4,128)S(1)}, f32[4,7]{1,0:T(4,128)S(1)}, u32[]{:S(2)}, u32[]{:S(2)}) collective-permute-start(f32[4,7]{1,0:T(4,128)S(1)} %add.310), channel_id=1, source_target_pairs={{0,2},{1,3},{2,0},{3,1},{4,6},{5,7},{6,4},{7,5},{8,10},{9,11},{10,... | collective-permute-start | bytes 344 | tf_op jit(solution)/shard_map/ppermute | solution.py:40
  87.5 2.5 %collective-permute-done.14 = f32[4,7]{1,0:T(4,128)S(1)} collective-permute-done((f32[4,7]{1,0:T(4,128)S(1)}, f32[4,7]{1,0:T(4,128)S(1)}, u32[]{:S(2)}, u32[]{:S(2)}) %collective-permute-start.14) | collective-permute-done | bytes 144 | tf_op jit(solution)/shard_map/ppermute | solution.py:40
  90.0 2.6 %collective-permute-start.15 = (f32[4,7]{1,0:T(4,128)S(1)}, f32[4,7]{1,0:T(4,128)S(1)}, u32[]{:S(2)}, u32[]{:S(2)}) collective-permute-start(f32[4,7]{1,0:T(4,128)S(1)} %add.311), channel_id=1, source_target_pairs={{0,4},{1,5},{2,6},{3,7},{4,0},{5,1},{6,2},{7,3},{8,12},{9,13},{10,... | collective-permute-start | bytes 344 | tf_op jit(solution)/shard_map/ppermute | solution.py:40
  92.6 1.9 %collective-permute-done.15 = f32[4,7]{1,0:T(4,128)S(1)} collective-permute-done((f32[4,7]{1,0:T(4,128)S(1)}, f32[4,7]{1,0:T(4,128)S(1)}, u32[]{:S(2)}, u32[]{:S(2)}) %collective-permute-start.15) | collective-permute-done | bytes 144 | tf_op jit(solution)/shard_map/ppermute | solution.py:40
  94.5 2.9 %collective-permute-start.18 = (f32[4,7]{1,0:T(4,128)S(1)}, f32[4,7]{1,0:T(4,128)S(1)}, u32[]{:S(2)}, u32[]{:S(2)}) collective-permute-start(f32[4,7]{1,0:T(4,128)S(1)} %add.312), channel_id=1, source_target_pairs={{0,24},{8,0},{16,8},{24,16},{1,25},{9,1},{17,9},{25,17},{2,26},{10... | collective-permute-start | bytes 344 | tf_op jit(solution)/shard_map/ppermute | solution.py:167
  98.7 2.3 %collective-permute-done.17 = f32[4,7]{1,0:T(4,128)S(1)} collective-permute-done((f32[4,7]{1,0:T(4,128)S(1)}, f32[4,7]{1,0:T(4,128)S(1)}, u32[]{:S(2)}, u32[]{:S(2)}) %collective-permute-start.17) | collective-permute-done | bytes 144 | tf_op jit(solution)/shard_map/ppermute | solution.py:167
  100.9 1.5 %collective-permute-done.16 = f32[4,7]{1,0:T(4,128)S(1)} collective-permute-done((f32[4,7]{1,0:T(4,128)S(1)}, f32[4,7]{1,0:T(4,128)S(1)}, u32[]{:S(2)}, u32[]{:S(2)}) %collective-permute-start.16) | collective-permute-done | bytes 144 | tf_op jit(solution)/shard_map/ppermute | solution.py:167
  103.4 1.2 %divide_multiply_fusion = f32[4,4,8,2048]{3,2,1,0:T(8,128)} fusion(f32[4,4,8,2048]{3,2,1,0:T(8,128)S(1)} %bitcast.119, f32[4]{0:T(128)S(1)} %get-tuple-element.20, f32[4]{0:T(128)S(1)} %get-tuple-element.19), kind=kLoop, calls=%fused_computation.142 | loop fusion | flops 524288 | bytes 2097184 | tf_op jit(solution)/shard_map/mul | solution.py:172
  (103 shorter events, 14.8 us)
Async XLA Ops:
  0.6 8.2 %copy-start = (f32[16,16]{1,0:T(8,128)S(1)}, f32[16,16]{1,0:T(8,128)}, u32[]{:S(2)}) copy-start(f32[16,16]{1,0:T(8,128)} %param.7) | copy-start | bytes 3076
  0.6 7.4 %copy-start.2 = (f32[8,2048]{1,0:T(8,128)S(1)}, f32[8,2048]{1,0:T(8,128)}, u32[]{:S(2)}) copy-start(f32[8,2048]{1,0:T(8,128)} %param.6) | copy-start | bytes 196612
  2.9 13.2 %all-to-all-start = ((bf16[4,4,8,2048]{3,2,1,0:T(8,128)(2,1)}), bf16[4,4,8,2048]{3,2,1,0:T(8,128)(2,1)S(1)}, u32[]{:S(2)}, u32[]{:S(2)}) async-start(bf16[4,4,8,2048]{3,2,1,0:T(8,128)(2,1)} %multiply_convert_fusion), calls=%async_computation | async-start | bytes 1048576 | tf_op jit(solution)/shard_map/all_to_all | solution.py:74
  8.1 1.5 %collective-permute-start.2 = (f32[6,2048]{1,0:T(8,128)S(1)}, f32[6,2048]{1,0:T(8,128)S(1)}, u32[]{:S(2)}, u32[]{:S(2)}) collective-permute-start(f32[6,2048]{1,0:T(8,128)S(1)} %get-tuple-element.42), channel_id=1, source_target_pairs={{0,1},{2,3},{4,5},{6,7},{1,0},{3,2},{5,4},{7,6},{8,9},{10,11},{12,... | collective-permute-start | bytes 147464 | tf_op jit(solution)/shard_map/ppermute | solution.py:64
  8.2 1.4 %collective-permute-start.3 = (f32[6,2048]{1,0:T(8,128)S(1)}, f32[6,2048]{1,0:T(8,128)S(1)}, u32[]{:S(2)}, u32[]{:S(2)}) collective-permute-start(f32[6,2048]{1,0:T(8,128)S(1)} %get-tuple-element.43), channel_id=1, source_target_pairs={{1,2},{3,4},{5,6},{2,1},{4,3},{6,5},{9,10},{11,12},{13,14},{10,9},... | collective-permute-start | bytes 147464 | tf_op jit(solution)/shard_map/ppermute | solution.py:63
  16.4 1.8 %collective-permute-start = (bf16[1,16,6,2048]{3,1,2,0:T(8,128)(2,1)S(1)}, bf16[1,16,6,2048]{3,1,2,0:T(8,128)(2,1)S(1)}, u32[]{:S(2)}, u32[]{:S(2)}) collective-permute-start(bf16[1,16,6,2048]{3,1,2,0:T(8,128)(2,1)S(1)} %get-tuple-element.38), channel_id=1, source_target_pairs={{0,1},{2,3},{4,5},{6,7},{1,0},{3,2},{5,4},{7,6},{8,9},{10,11},{12,... | collective-permute-start | bytes 1179656 | tf_op jit(solution)/shard_map/ppermute | solution.py:64
  16.5 1.7 %collective-permute-start.1 = (bf16[1,16,6,2048]{3,1,2,0:T(8,128)(2,1)S(1)}, bf16[1,16,6,2048]{3,1,2,0:T(8,128)(2,1)S(1)}, u32[]{:S(2)}, u32[]{:S(2)}) collective-permute-start(bf16[1,16,6,2048]{3,1,2,0:T(8,128)(2,1)S(1)} %get-tuple-element.39), channel_id=1, source_target_pairs={{1,2},{3,4},{5,6},{2,1},{4,3},{6,5},{9,10},{11,12},{13,14},{10,9},... | collective-permute-start | bytes 1179656 | tf_op jit(solution)/shard_map/ppermute | solution.py:63
  18.6 0.7 copy-start.1
  29.5 8.3 %slice-start = ((f32[1,1,20,2048]{3,1,2,0:T(1,128)}), f32[1,1,14,2048]{3,1,2,0:T(1,128)S(1)}, s32[]{:S(2)}) async-start(f32[1,1,20,2048]{3,1,2,0:T(1,128)} %copy-done.1), calls=%async_computation.2 | async-start | bytes 229376 | tf_op jit(solution)/shard_map/slice | solution.py:86
  29.5 8.3 %slice-start.1 = ((f32[1,1,20,2048]{3,1,2,0:T(1,128)}), f32[1,1,12,2048]{3,1,2,0:T(1,128)S(1)}, s32[]{:S(2)}) async-start(f32[1,1,20,2048]{3,1,2,0:T(1,128)} %copy-done.1), calls=%async_computation.3 | async-start | bytes 196608 | tf_op jit(solution)/shard_map/slice | solution.py:86
  29.5 8.4 %slice-start.2 = ((f32[1,1,20,2048]{3,1,2,0:T(1,128)}), f32[1,1,10,2048]{3,1,2,0:T(1,128)S(1)}, s32[]{:S(2)}) async-start(f32[1,1,20,2048]{3,1,2,0:T(1,128)} %copy-done.1), calls=%async_computation.4 | async-start | bytes 163840 | tf_op jit(solution)/shard_map/slice | solution.py:86
  29.5 8.4 %slice-start.3 = ((f32[1,1,20,2048]{3,1,2,0:T(1,128)}), f32[1,1,8,2048]{3,1,2,0:T(1,128)S(1)}, s32[]{:S(2)}) async-start(f32[1,1,20,2048]{3,1,2,0:T(1,128)} %copy-done.1), calls=%async_computation.5 | async-start | bytes 131072 | tf_op jit(solution)/shard_map/slice | solution.py:86
  29.9 11.5 %collective-permute-start.4 = (f32[1,2]{1,0:T(1,128)S(1)}, f32[1,2]{1,0:T(1,128)S(1)}, u32[]{:S(2)}, u32[]{:S(2)}) collective-permute-start(f32[1,2]{1,0:T(1,128)S(1)} %bitcast.145), channel_id=1, source_target_pairs={{0,1},{1,0},{2,3},{3,2},{4,5},{5,4},{6,7},{7,6},{8,9},{9,8},{10,11... | collective-permute-start | bytes 32 | tf_op jit(solution)/shard_map/ppermute | solution.py:40
  41.5 6.0 %collective-permute-start.5 = (f32[1,2]{1,0:T(1,128)S(1)}, f32[1,2]{1,0:T(1,128)S(1)}, u32[]{:S(2)}, u32[]{:S(2)}) collective-permute-start(f32[1,2]{1,0:T(1,128)S(1)} %bitcast_add_fusion.2), channel_id=1, source_target_pairs={{0,2},{1,3},{2,0},{3,1},{4,6},{5,7},{6,4},{7,5},{8,10},{9,11},{10,... | collective-permute-start | bytes 32 | tf_op jit(solution)/shard_map/ppermute | solution.py:40
  47.5 4.5 %collective-permute-start.6 = (f32[1,2]{1,0:T(1,128)S(1)}, f32[1,2]{1,0:T(1,128)S(1)}, u32[]{:S(2)}, u32[]{:S(2)}) collective-permute-start(f32[1,2]{1,0:T(1,128)S(1)} %add.280), channel_id=1, source_target_pairs={{0,4},{1,5},{2,6},{3,7},{4,0},{5,1},{6,2},{7,3},{8,12},{9,13},{10,... | collective-permute-start | bytes 32 | tf_op jit(solution)/shard_map/ppermute | solution.py:40
  54.1 2.1 %collective-permute-start.7 = (f32[1,3]{1,0:T(1,128)S(1)}, f32[1,3]{1,0:T(1,128)S(1)}, u32[]{:S(2)}, u32[]{:S(2)}) collective-permute-start(f32[1,3]{1,0:T(1,128)S(1)} %bitcast.146), channel_id=1, source_target_pairs={{0,1},{1,0},{2,3},{3,2},{4,5},{5,4},{6,7},{7,6},{8,9},{9,8},{10,11... | collective-permute-start | bytes 44 | tf_op jit(solution)/shard_map/ppermute | solution.py:40
  56.2 3.6 %collective-permute-start.8 = (f32[1,3]{1,0:T(1,128)S(1)}, f32[1,3]{1,0:T(1,128)S(1)}, u32[]{:S(2)}, u32[]{:S(2)}) collective-permute-start(f32[1,3]{1,0:T(1,128)S(1)} %bitcast_add_fusion.1), channel_id=1, source_target_pairs={{0,2},{1,3},{2,0},{3,1},{4,6},{5,7},{6,4},{7,5},{8,10},{9,11},{10,... | collective-permute-start | bytes 44 | tf_op jit(solution)/shard_map/ppermute | solution.py:40
  59.9 4.5 %collective-permute-start.9 = (f32[1,3]{1,0:T(1,128)S(1)}, f32[1,3]{1,0:T(1,128)S(1)}, u32[]{:S(2)}, u32[]{:S(2)}) collective-permute-start(f32[1,3]{1,0:T(1,128)S(1)} %add.296), channel_id=1, source_target_pairs={{0,4},{1,5},{2,6},{3,7},{4,0},{5,1},{6,2},{7,3},{8,12},{9,13},{10,... | collective-permute-start | bytes 44 | tf_op jit(solution)/shard_map/ppermute | solution.py:40
  66.9 1.2 %collective-permute-start.10 = (f32[1,3]{1,0:T(1,128)S(1)}, f32[1,3]{1,0:T(1,128)S(1)}, u32[]{:S(2)}, u32[]{:S(2)}) collective-permute-start(f32[1,3]{1,0:T(1,128)S(1)} %bitcast.147), channel_id=1, source_target_pairs={{0,1},{1,0},{2,3},{3,2},{4,5},{5,4},{6,7},{7,6},{8,9},{9,8},{10,11... | collective-permute-start | bytes 44 | tf_op jit(solution)/shard_map/ppermute | solution.py:40
  68.1 3.6 %collective-permute-start.11 = (f32[1,3]{1,0:T(1,128)S(1)}, f32[1,3]{1,0:T(1,128)S(1)}, u32[]{:S(2)}, u32[]{:S(2)}) collective-permute-start(f32[1,3]{1,0:T(1,128)S(1)} %bitcast_add_fusion), channel_id=1, source_target_pairs={{0,2},{1,3},{2,0},{3,1},{4,6},{5,7},{6,4},{7,5},{8,10},{9,11},{10,... | collective-permute-start | bytes 44 | tf_op jit(solution)/shard_map/ppermute | solution.py:40
  71.6 4.5 %collective-permute-start.12 = (f32[1,3]{1,0:T(1,128)S(1)}, f32[1,3]{1,0:T(1,128)S(1)}, u32[]{:S(2)}, u32[]{:S(2)}) collective-permute-start(f32[1,3]{1,0:T(1,128)S(1)} %add.306), channel_id=1, source_target_pairs={{0,4},{1,5},{2,6},{3,7},{4,0},{5,1},{6,2},{7,3},{8,12},{9,13},{10,... | collective-permute-start | bytes 44 | tf_op jit(solution)/shard_map/ppermute | solution.py:40
  80.1 23.3 %all-to-all-start.1 = ((f32[1,16,8,2048]{3,2,0,1:T(8,128)}), f32[1,16,8,2048]{3,2,0,1:T(8,128)S(1)}, u32[]{:S(2)}, u32[]{:S(2)}) async-start(f32[1,16,8,2048]{3,2,0,1:T(8,128)} %copy.12), calls=%async_computation.1 | async-start | bytes 2097152 | tf_op jit(solution)/shard_map/all_to_all | solution.py:153
  84.4 1.2 %collective-permute-start.13 = (f32[4,7]{1,0:T(4,128)S(1)}, f32[4,7]{1,0:T(4,128)S(1)}, u32[]{:S(2)}, u32[]{:S(2)}) collective-permute-start(f32[4,7]{1,0:T(4,128)S(1)} %dynamic_update_slice.5), channel_id=1, source_target_pairs={{0,1},{1,0},{2,3},{3,2},{4,5},{5,4},{6,7},{7,6},{8,9},{9,8},{10,11... | collective-permute-start | bytes 344 | tf_op jit(solution)/shard_map/ppermute | solution.py:40
  86.3 3.6 %collective-permute-start.14 = (f32[4,7]{1,0:T(4,128)S(1)}, f32[4,7]{1,0:T(4,128)S(1)}, u32[]{:S(2)}, u32[]{:S(2)}) collective-permute-start(f32[4,7]{1,0:T(4,128)S(1)} %add.310), channel_id=1, source_target_pairs={{0,2},{1,3},{2,0},{3,1},{4,6},{5,7},{6,4},{7,5},{8,10},{9,11},{10,... | collective-permute-start | bytes 344 | tf_op jit(solution)/shard_map/ppermute | solution.py:40
  90.0 4.5 %collective-permute-start.15 = (f32[4,7]{1,0:T(4,128)S(1)}, f32[4,7]{1,0:T(4,128)S(1)}, u32[]{:S(2)}, u32[]{:S(2)}) collective-permute-start(f32[4,7]{1,0:T(4,128)S(1)} %add.311), channel_id=1, source_target_pairs={{0,4},{1,5},{2,6},{3,7},{4,0},{5,1},{6,2},{7,3},{8,12},{9,13},{10,... | collective-permute-start | bytes 344 | tf_op jit(solution)/shard_map/ppermute | solution.py:40
  94.5 4.2 %collective-permute-start.18 = (f32[4,7]{1,0:T(4,128)S(1)}, f32[4,7]{1,0:T(4,128)S(1)}, u32[]{:S(2)}, u32[]{:S(2)}) collective-permute-start(f32[4,7]{1,0:T(4,128)S(1)} %add.312), channel_id=1, source_target_pairs={{0,24},{8,0},{16,8},{24,16},{1,25},{9,1},{17,9},{25,17},{2,26},{10... | collective-permute-start | bytes 344 | tf_op jit(solution)/shard_map/ppermute | solution.py:167
  97.3 3.6 %collective-permute-start.17 = (f32[4,7]{1,0:T(4,128)S(1)}, f32[4,7]{1,0:T(4,128)S(1)}, u32[]{:S(2)}, u32[]{:S(2)}) collective-permute-start(f32[4,7]{1,0:T(4,128)S(1)} %add.312), channel_id=1, source_target_pairs={{0,16},{8,24},{16,0},{24,8},{1,17},{9,25},{17,1},{25,9},{2,18},{10... | collective-permute-start | bytes 344 | tf_op jit(solution)/shard_map/ppermute | solution.py:167
  97.9 4.5 %collective-permute-start.16 = (f32[4,7]{1,0:T(4,128)S(1)}, f32[4,7]{1,0:T(4,128)S(1)}, u32[]{:S(2)}, u32[]{:S(2)}) collective-permute-start(f32[4,7]{1,0:T(4,128)S(1)} %add.312), channel_id=1, source_target_pairs={{0,8},{8,16},{16,24},{24,0},{1,9},{9,17},{17,25},{25,1},{2,10},{10... | collective-permute-start | bytes 344 | tf_op jit(solution)/shard_map/ppermute | solution.py:167
  102.4 2.1 %copy-start.3 = (f32[4,7]{1,0:T(4,128)}, f32[4,7]{1,0:T(4,128)S(1)}, u32[]{:S(2)}) copy-start(f32[4,7]{1,0:T(4,128)S(1)} %add_add_fusion) | copy-start | bytes 340

commit v5 on v3

--- a/solution.py
+++ b/solution.py
@@ -88,7 +88,9 @@
     def apply_a(x, off):
         return mix(stencil(stencil(x, off), off + 1))
 
-    def a_stages(x, off):
+    def a_stages(x, off, split_mix=False):
+        if split_mix:
+            return (lambda _: stencil(x, off), lambda first: stencil(first, off + 1), mix)
         return (lambda _: stencil(x, off), lambda first: mix(stencil(first, off + 1)))
 
     def own(x, off):
@@ -106,7 +108,7 @@
 
     az = apply_a(z, 0)
     z2 = crop(z, 2)
-    sums, aaz = reduce_tile([(z2, z2), (az, z2)], 2, a_stages(az, 2))
+    sums, aaz = reduce_tile([(z2, z2), (az, z2)], 2, a_stages(az, 2, split_mix=True))
     sv = lanes(sums)
     norm_v = jnp.sqrt(sv[:, 0] + epsilon)
     alpha_v = sv[:, 1] / (norm_v * norm_v)
@@ -125,7 +127,7 @@
     iters = 3
     for step in range(1, iters):
         last_step = step == iters - 1
-        sums, aaw = reduce_tile([(w, w), (aw, w), (q, w)], off, () if last_step else a_stages(aw, off))
+        sums, aaw = reduce_tile([(w, w), (aw, w), (q, w)], off, () if last_step else a_stages(aw, off, split_mix=True))
         sv = lanes(sums)
         beta_v = jnp.sqrt(sv[:, 0] + epsilon)
         alpha_v = sv[:, 1] / (beta_v * beta_v) - sv[:, 2]

time: 102 us -> 101 us (level)
  other arithmetic: 21.4 us -> 25.9 us
  matrix products: 12.4 us -> 8.13 us
  waiting for transfers between devices: 26 us -> 23.9 us
    dot_general x3, matrix products: 12.4 us -> 8.13 us  [mix(): jnp.einsum('ts,psrc->ptrc', trait_covariance, x, precision=lax.Precision....]
    mul x3 -> x5, other arithmetic: 9.99 us -> 14.2 us  [stencil(): land_ext[off + 1:off + r - 1]]
    ppermute x14, waiting for transfers between devices: 18.6 us -> 16.6 us  [butterfly_sum(): got = lax.ppermute(v, axis, [(i, i ^ s) for i in range(n)])]
where the time goes in v5:
time: 101 us; the launch traced here: 100 us
  starting transfers between devices  37.3 us (37%)
  other arithmetic  25.9 us (26%)
  waiting for transfers between devices  23.9 us (24%)
  matrix products  8.13 us (8%)
  local copies, waits for them, and re-layouts  3.76 us (4%)
  between operations  1.2 us (1%)
    ppermute x14, starting transfers between devices, butterfly_sum(): got = lax.ppermute(v, axis, [(i, i ^ s) for i in range(n)])  27.1 us
    ppermute x14, waiting for transfers between devices, butterfly_sum(): got = lax.ppermute(v, axis, [(i, i ^ s) for i in range(n)])  16.6 us
    mul x5, other arithmetic, stencil(): land_ext[off + 1:off + r - 1]  14.2 us
    dot_general x3, matrix products, mix(): jnp.einsum('ts,psrc->ptrc', trait_covariance, x, precision=lax.Precision....  8.13 us
    all_to_all x1, waiting for transfers between devices, shards(): lax.all_to_all(signed, 'trait', split_axis=0, concat_axis=1, tiled=True)  6.36 us
    all_to_all x1, starting transfers between devices, shards(): lax.all_to_all(signed, 'trait', split_axis=0, concat_axis=1, tiled=True)  5.19 us
    all_to_all x1, starting transfers between devices, shards(): lax.all_to_all(w_own, 'trait', split_axis=1, concat_axis=0, tiled=True)  3.52 us
    convert_element_type x1, other arithmetic, shards(): (land_mask[None, None] * (2 * probe_signs - 1)).astype(jnp.bfloat16)  2.22 us
  transfers between devices with their start and end apart: 20, of which 13 were waited for; matrix products, arithmetic and copies ran while one was open for 16% of the time, Pallas kernels for 0%

profile of v5, /device:TPU:0, one launch (start us, length us, event | category | flops | bytes accessed | tf_op | source)
XLA Modules:
  0.0 100.2 jit_solution(111373596148544819)
XLA Ops:
  0.7 2.2 %multiply_convert_fusion = bf16[4,4,8,2048]{3,2,1,0:T(8,128)(2,1)} fusion(s32[4,4,8,2048]{3,2,1,0:T(8,128)} %param.4, s32[8,2048]{1,0:T(8,128)} %param.5), kind=kLoop, calls=%fused_computation.151 | loop fusion | flops 1048576 | bytes 1638400 | tf_op jit(solution)/shard_map/convert_element_type | solution.py:73
  2.9 5.2 %all-to-all-start = ((bf16[4,4,8,2048]{3,2,1,0:T(8,128)(2,1)}), bf16[4,4,8,2048]{3,2,1,0:T(8,128)(2,1)S(1)}, u32[]{:S(2)}, u32[]{:S(2)}) async-start(bf16[4,4,8,2048]{3,2,1,0:T(8,128)(2,1)} %multiply_convert_fusion), calls=%async_computation | async-start | bytes 1048576 | tf_op jit(solution)/shard_map/all_to_all | solution.py:74
  9.7 6.4 %all-to-all-done = bf16[4,4,8,2048]{3,2,1,0:T(8,128)(2,1)S(1)} async-done(((bf16[4,4,8,2048]{3,2,1,0:T(8,128)(2,1)}), bf16[4,4,8,2048]{3,2,1,0:T(8,128)(2,1)S(1)}, u32[]{:S(2)}, u32[]{:S(2)}) %all-to-all-start) | async-done | bytes 524320 | tf_op jit(solution)/shard_map/all_to_all | solution.py:74
  19.4 4.3 %fusion.5 = f32[1,16,18,2048]{3,1,2,0:T(8,128)S(1)} fusion(f32[1,16,20,2048]{3,1,2,0:T(8,128)S(1)} %broadcast_multiply_fusion, f32[18,2048]{1,0:T(8,128)S(1)} %slice_add_fusion.4, f32[18,2048]{1,0:T(8,128)S(1)} %bitcast.119), kind=kLoop, calls=%fused_computation.17 | loop fusion | flops 7667712 | bytes 12451840 | tf_op jit(solution)/shard_map/mul | solution.py:86
  23.7 5.6 %convolution_bitcast_fusion = f32[1,16,16,2048]{3,1,2,0:T(8,128)S(1)} fusion(f32[1,16,18,2048]{3,1,2,0:T(8,128)S(1)} %fusion.5, f32[16,2048]{1,0:T(8,128)S(1)} %slice_add_fusion.8, f32[16,2048]{1,0:T(8,128)S(1)} %bitcast.124, f32[16,16]{1,0:T(8,128)S(1)} %copy-done), kind=kOutput, calls=%fused_computation.3 | convolution fusion | flops 107479040 | bytes 11018240 | tf_op jit(solution)/shard_map/ts,psrc->ptrc/dot_general | solution.py:82
  30.0 7.9 %collective-permute-start.4 = (f32[1,2]{1,0:T(1,128)S(1)}, f32[1,2]{1,0:T(1,128)S(1)}, u32[]{:S(2)}, u32[]{:S(2)}) collective-permute-start(f32[1,2]{1,0:T(1,128)S(1)} %bitcast.143), channel_id=1, source_target_pairs={{0,1},{1,0},{2,3},{3,2},{4,5},{5,4},{6,7},{7,6},{8,9},{9,8},{10,11... | collective-permute-start | bytes 32 | tf_op jit(solution)/shard_map/ppermute | solution.py:40
  38.0 3.6 %fusion.33 = f32[1,16,14,2048]{3,1,2,0:T(8,128)S(1)} fusion(f32[1,16,16,2048]{3,1,2,0:T(8,128)S(1)} %convolution_bitcast_fusion, f32[14,2048]{1,0:T(8,128)S(1)} %slice_add_fusion.7, f32[14,2048]{1,0:T(8,128)S(1)} %bitcast.122), kind=kLoop, calls=%fused_computation.60 | loop fusion | flops 5963776 | bytes 9699328 | tf_op jit(solution)/shard_map/mul | solution.py:86
  41.7 1.7 %collective-permute-start.5 = (f32[1,2]{1,0:T(1,128)S(1)}, f32[1,2]{1,0:T(1,128)S(1)}, u32[]{:S(2)}, u32[]{:S(2)}) collective-permute-start(f32[1,2]{1,0:T(1,128)S(1)} %bitcast_add_fusion.2), channel_id=1, source_target_pairs={{0,2},{1,3},{2,0},{3,1},{4,6},{5,7},{6,4},{7,5},{8,10},{9,11},{10,... | collective-permute-start | bytes 32 | tf_op jit(solution)/shard_map/ppermute | solution.py:40
  43.3 2.5 %fusion.44 = f32[1,16,12,2048]{3,1,2,0:T(8,128)S(1)} fusion(f32[1,16,14,2048]{3,1,2,0:T(8,128)S(1)} %fusion.33, f32[12,2048]{1,0:T(8,128)S(1)} %slice_add_fusion.6, f32[12,2048]{1,0:T(8,128)S(1)} %bitcast.120), kind=kLoop, calls=%fused_computation.79 | loop fusion | flops 5111808 | bytes 8388608 | tf_op jit(solution)/shard_map/mul | solution.py:86
  45.9 2.6 %collective-permute-start.6 = (f32[1,2]{1,0:T(1,128)S(1)}, f32[1,2]{1,0:T(1,128)S(1)}, u32[]{:S(2)}, u32[]{:S(2)}) collective-permute-start(f32[1,2]{1,0:T(1,128)S(1)} %add.277), channel_id=1, source_target_pairs={{0,4},{1,5},{2,6},{3,7},{4,0},{5,1},{6,2},{7,3},{8,12},{9,13},{10,... | collective-permute-start | bytes 32 | tf_op jit(solution)/shard_map/ppermute | solution.py:40
  48.5 1.5 %convolution_bitcast_fusion.1 = f32[1,16,12,2048]{3,1,2,0:T(8,128)S(1)} fusion(f32[1,16,12,2048]{3,1,2,0:T(8,128)S(1)} %fusion.44, f32[16,16]{1,0:T(8,128)S(1)} %copy-done), kind=kOutput, calls=%fused_computation.4 | convolution fusion | flops 75497472 | bytes 3146752 | tf_op jit(solution)/shard_map/ts,psrc->ptrc/dot_general | solution.py:82
  52.5 2.1 %fusion.56 = f32[1,16,10,2048]{3,1,2,0:T(8,128)S(1)} fusion(f32[1,16,12,2048]{3,1,2,0:T(8,128)S(1)} %fusion.49, f32[10,2048]{1,0:T(8,128)S(1)} %slice_add_fusion.5, f32[10,2048]{1,0:T(8,128)S(1)} %bitcast.121), kind=kLoop, calls=%fused_computation.99 | loop fusion | flops 4259840 | bytes 7077888 | tf_op jit(solution)/shard_map/mul | solution.py:86
  54.6 1.0 %collective-permute-start.8 = (f32[1,3]{1,0:T(1,128)S(1)}, f32[1,3]{1,0:T(1,128)S(1)}, u32[]{:S(2)}, u32[]{:S(2)}) collective-permute-start(f32[1,3]{1,0:T(1,128)S(1)} %bitcast_add_fusion.1), channel_id=1, source_target_pairs={{0,2},{1,3},{2,0},{3,1},{4,6},{5,7},{6,4},{7,5},{8,10},{9,11},{10,... | collective-permute-start | bytes 44 | tf_op jit(solution)/shard_map/ppermute | solution.py:40
  55.7 1.7 %fusion.67 = f32[1,16,8,2048]{3,1,2,0:T(8,128)S(1)} fusion(f32[1,16,10,2048]{3,1,2,0:T(8,128)S(1)} %fusion.56, f32[8,2048]{1,0:T(8,128)S(1)} %broadcast_add_fusion, f32[8,2048]{1,0:T(8,128)S(1)} %bitcast.123), kind=kLoop, calls=%fused_computation.120 | loop fusion | flops 3407872 | bytes 5636096 | tf_op jit(solution)/shard_map/mul | solution.py:86
  58.3 2.6 %collective-permute-start.9 = (f32[1,3]{1,0:T(1,128)S(1)}, f32[1,3]{1,0:T(1,128)S(1)}, u32[]{:S(2)}, u32[]{:S(2)}) collective-permute-start(f32[1,3]{1,0:T(1,128)S(1)} %add.293), channel_id=1, source_target_pairs={{0,4},{1,5},{2,6},{3,7},{4,0},{5,1},{6,2},{7,3},{8,12},{9,13},{10,... | collective-permute-start | bytes 44 | tf_op jit(solution)/shard_map/ppermute | solution.py:40
  60.9 1.0 %convolution_bitcast_fusion.2 = f32[1,16,8,2048]{3,1,2,0:T(8,128)S(1)} fusion(f32[1,16,8,2048]{3,1,2,0:T(8,128)S(1)} %fusion.67, f32[16,16]{1,0:T(8,128)S(1)} %copy-done), kind=kOutput, calls=%fused_computation.5 | convolution fusion | flops 50331648 | bytes 2098176 | tf_op jit(solution)/shard_map/ts,psrc->ptrc/dot_general | solution.py:82
  64.5 1.1 %collective-permute-done.10 = f32[1,3]{1,0:T(1,128)S(1)} collective-permute-done((f32[1,3]{1,0:T(1,128)S(1)}, f32[1,3]{1,0:T(1,128)S(1)}, u32[]{:S(2)}, u32[]{:S(2)}) %collective-permute-start.10) | collective-permute-done | bytes 44 | tf_op jit(solution)/shard_map/ppermute | solution.py:40
  66.6 2.6 %collective-permute-done.11 = f32[1,3]{1,0:T(1,128)S(1)} collective-permute-done((f32[1,3]{1,0:T(1,128)S(1)}, f32[1,3]{1,0:T(1,128)S(1)}, u32[]{:S(2)}, u32[]{:S(2)}) %collective-permute-start.11) | collective-permute-done | bytes 44 | tf_op jit(solution)/shard_map/ppermute | solution.py:40
  69.2 2.6 %collective-permute-start.12 = (f32[1,3]{1,0:T(1,128)S(1)}, f32[1,3]{1,0:T(1,128)S(1)}, u32[]{:S(2)}, u32[]{:S(2)}) collective-permute-start(f32[1,3]{1,0:T(1,128)S(1)} %add.303), channel_id=1, source_target_pairs={{0,4},{1,5},{2,6},{3,7},{4,0},{5,1},{6,2},{7,3},{8,12},{9,13},{10,... | collective-permute-start | bytes 44 | tf_op jit(solution)/shard_map/ppermute | solution.py:40
  71.8 1.9 %collective-permute-done.12 = f32[1,3]{1,0:T(1,128)S(1)} collective-permute-done((f32[1,3]{1,0:T(1,128)S(1)}, f32[1,3]{1,0:T(1,128)S(1)}, u32[]{:S(2)}, u32[]{:S(2)}) %collective-permute-start.12) | collective-permute-done | bytes 44 | tf_op jit(solution)/shard_map/ppermute | solution.py:40
  74.7 1.6 %copy.12 = f32[1,16,8,2048]{3,2,0,1:T(8,128)} copy(f32[1,16,8,2048]{3,1,2,0:T(8,128)S(1)} %get-tuple-element.30) | data formatting | bytes 2097152 | tf_op jit(solution)/shard_map/sub | solution.py:137
  76.3 3.5 %all-to-all-start.1 = ((f32[1,16,8,2048]{3,2,0,1:T(8,128)}), f32[1,16,8,2048]{3,2,0,1:T(8,128)S(1)}, u32[]{:S(2)}, u32[]{:S(2)}) async-start(f32[1,16,8,2048]{3,2,0,1:T(8,128)} %copy.12), calls=%async_computation.1 | async-start | bytes 2097152 | tf_op jit(solution)/shard_map/all_to_all | solution.py:155
  80.8 1.1 %collective-permute-done.13 = f32[4,7]{1,0:T(4,128)S(1)} collective-permute-done((f32[4,7]{1,0:T(4,128)S(1)}, f32[4,7]{1,0:T(4,128)S(1)}, u32[]{:S(2)}, u32[]{:S(2)}) %collective-permute-start.13) | collective-permute-done | bytes 144 | tf_op jit(solution)/shard_map/ppermute | solution.py:40
  82.7 1.0 %collective-permute-start.14 = (f32[4,7]{1,0:T(4,128)S(1)}, f32[4,7]{1,0:T(4,128)S(1)}, u32[]{:S(2)}, u32[]{:S(2)}) collective-permute-start(f32[4,7]{1,0:T(4,128)S(1)} %add.307), channel_id=1, source_target_pairs={{0,2},{1,3},{2,0},{3,1},{4,6},{5,7},{6,4},{7,5},{8,10},{9,11},{10,... | collective-permute-start | bytes 344 | tf_op jit(solution)/shard_map/ppermute | solution.py:40
  83.8 2.6 %collective-permute-done.14 = f32[4,7]{1,0:T(4,128)S(1)} collective-permute-done((f32[4,7]{1,0:T(4,128)S(1)}, f32[4,7]{1,0:T(4,128)S(1)}, u32[]{:S(2)}, u32[]{:S(2)}) %collective-permute-start.14) | collective-permute-done | bytes 144 | tf_op jit(solution)/shard_map/ppermute | solution.py:40
  86.4 2.6 %collective-permute-start.15 = (f32[4,7]{1,0:T(4,128)S(1)}, f32[4,7]{1,0:T(4,128)S(1)}, u32[]{:S(2)}, u32[]{:S(2)}) collective-permute-start(f32[4,7]{1,0:T(4,128)S(1)} %add.308), channel_id=1, source_target_pairs={{0,4},{1,5},{2,6},{3,7},{4,0},{5,1},{6,2},{7,3},{8,12},{9,13},{10,... | collective-permute-start | bytes 344 | tf_op jit(solution)/shard_map/ppermute | solution.py:40
  89.0 1.9 %collective-permute-done.15 = f32[4,7]{1,0:T(4,128)S(1)} collective-permute-done((f32[4,7]{1,0:T(4,128)S(1)}, f32[4,7]{1,0:T(4,128)S(1)}, u32[]{:S(2)}, u32[]{:S(2)}) %collective-permute-start.15) | collective-permute-done | bytes 144 | tf_op jit(solution)/shard_map/ppermute | solution.py:40
  90.9 2.0 %collective-permute-start.16 = (f32[4,7]{1,0:T(4,128)S(1)}, f32[4,7]{1,0:T(4,128)S(1)}, u32[]{:S(2)}, u32[]{:S(2)}) collective-permute-start(f32[4,7]{1,0:T(4,128)S(1)} %add.309), channel_id=1, source_target_pairs={{0,8},{8,0},{16,24},{24,16},{1,9},{9,1},{17,25},{25,17},{2,10},{10... | collective-permute-start | bytes 344 | tf_op jit(solution)/shard_map/ppermute | solution.py:40
  92.9 1.6 %collective-permute-done.16 = f32[4,7]{1,0:T(4,128)S(1)} collective-permute-done((f32[4,7]{1,0:T(4,128)S(1)}, f32[4,7]{1,0:T(4,128)S(1)}, u32[]{:S(2)}, u32[]{:S(2)}) %collective-permute-start.16) | collective-permute-done | bytes 144 | tf_op jit(solution)/shard_map/ppermute | solution.py:40
  94.5 2.0 %collective-permute-start.17 = (f32[4,7]{1,0:T(4,128)S(1)}, f32[4,7]{1,0:T(4,128)S(1)}, u32[]{:S(2)}, u32[]{:S(2)}) collective-permute-start(f32[4,7]{1,0:T(4,128)S(1)} %add.310), channel_id=1, source_target_pairs={{0,16},{8,24},{16,0},{24,8},{1,17},{9,25},{17,1},{25,9},{2,18},{10... | collective-permute-start | bytes 344 | tf_op jit(solution)/shard_map/ppermute | solution.py:40
  96.4 1.6 %collective-permute-done.17 = f32[4,7]{1,0:T(4,128)S(1)} collective-permute-done((f32[4,7]{1,0:T(4,128)S(1)}, f32[4,7]{1,0:T(4,128)S(1)}, u32[]{:S(2)}, u32[]{:S(2)}) %collective-permute-start.17) | collective-permute-done | bytes 144 | tf_op jit(solution)/shard_map/ppermute | solution.py:40
  99.0 1.2 %divide_multiply_fusion = f32[4,4,8,2048]{3,2,1,0:T(8,128)} fusion(f32[4,4,8,2048]{3,2,1,0:T(8,128)S(1)} %bitcast.117, f32[4]{0:T(128)S(1)} %get-tuple-element.28, f32[4]{0:T(128)S(1)} %get-tuple-element.27), kind=kLoop, calls=%fused_computation.136 | loop fusion | flops 524288 | bytes 2097184 | tf_op jit(solution)/shard_map/mul | solution.py:170
  (104 shorter events, 16.1 us)
Async XLA Ops:
  0.6 8.2 %copy-start = (f32[16,16]{1,0:T(8,128)S(1)}, f32[16,16]{1,0:T(8,128)}, u32[]{:S(2)}) copy-start(f32[16,16]{1,0:T(8,128)} %param.7) | copy-start | bytes 3076
  0.6 7.4 %copy-start.2 = (f32[8,2048]{1,0:T(8,128)S(1)}, f32[8,2048]{1,0:T(8,128)}, u32[]{:S(2)}) copy-start(f32[8,2048]{1,0:T(8,128)} %param.6) | copy-start | bytes 196612
  2.9 13.2 %all-to-all-start = ((bf16[4,4,8,2048]{3,2,1,0:T(8,128)(2,1)}), bf16[4,4,8,2048]{3,2,1,0:T(8,128)(2,1)S(1)}, u32[]{:S(2)}, u32[]{:S(2)}) async-start(bf16[4,4,8,2048]{3,2,1,0:T(8,128)(2,1)} %multiply_convert_fusion), calls=%async_computation | async-start | bytes 1048576 | tf_op jit(solution)/shard_map/all_to_all | solution.py:74
  8.1 1.5 %collective-permute-start.2 = (f32[6,2048]{1,0:T(8,128)S(1)}, f32[6,2048]{1,0:T(8,128)S(1)}, u32[]{:S(2)}, u32[]{:S(2)}) collective-permute-start(f32[6,2048]{1,0:T(8,128)S(1)} %get-tuple-element.50), channel_id=1, source_target_pairs={{0,1},{2,3},{4,5},{6,7},{1,0},{3,2},{5,4},{7,6},{8,9},{10,11},{12,... | collective-permute-start | bytes 147464 | tf_op jit(solution)/shard_map/ppermute | solution.py:64
  8.2 1.4 %collective-permute-start.3 = (f32[6,2048]{1,0:T(8,128)S(1)}, f32[6,2048]{1,0:T(8,128)S(1)}, u32[]{:S(2)}, u32[]{:S(2)}) collective-permute-start(f32[6,2048]{1,0:T(8,128)S(1)} %get-tuple-element.51), channel_id=1, source_target_pairs={{1,2},{3,4},{5,6},{2,1},{4,3},{6,5},{9,10},{11,12},{13,14},{10,9},... | collective-permute-start | bytes 147464 | tf_op jit(solution)/shard_map/ppermute | solution.py:63
  16.4 1.8 %collective-permute-start = (bf16[1,16,6,2048]{3,1,2,0:T(8,128)(2,1)S(1)}, bf16[1,16,6,2048]{3,1,2,0:T(8,128)(2,1)S(1)}, u32[]{:S(2)}, u32[]{:S(2)}) collective-permute-start(bf16[1,16,6,2048]{3,1,2,0:T(8,128)(2,1)S(1)} %get-tuple-element.46), channel_id=1, source_target_pairs={{0,1},{2,3},{4,5},{6,7},{1,0},{3,2},{5,4},{7,6},{8,9},{10,11},{12,... | collective-permute-start | bytes 1179656 | tf_op jit(solution)/shard_map/ppermute | solution.py:64
  16.5 1.7 %collective-permute-start.1 = (bf16[1,16,6,2048]{3,1,2,0:T(8,128)(2,1)S(1)}, bf16[1,16,6,2048]{3,1,2,0:T(8,128)(2,1)S(1)}, u32[]{:S(2)}, u32[]{:S(2)}) collective-permute-start(bf16[1,16,6,2048]{3,1,2,0:T(8,128)(2,1)S(1)} %get-tuple-element.47), channel_id=1, source_target_pairs={{1,2},{3,4},{5,6},{2,1},{4,3},{6,5},{9,10},{11,12},{13,14},{10,9},... | collective-permute-start | bytes 1179656 | tf_op jit(solution)/shard_map/ppermute | solution.py:63
  18.6 0.7 copy-start.1
  29.5 8.3 %slice-start = ((f32[1,1,20,2048]{3,1,2,0:T(1,128)}), f32[1,1,14,2048]{3,1,2,0:T(1,128)S(1)}, s32[]{:S(2)}) async-start(f32[1,1,20,2048]{3,1,2,0:T(1,128)} %copy-done.1), calls=%async_computation.2 | async-start | bytes 229376 | tf_op jit(solution)/shard_map/slice | solution.py:86
  29.6 8.3 %slice-start.1 = ((f32[1,1,20,2048]{3,1,2,0:T(1,128)}), f32[1,1,12,2048]{3,1,2,0:T(1,128)S(1)}, s32[]{:S(2)}) async-start(f32[1,1,20,2048]{3,1,2,0:T(1,128)} %copy-done.1), calls=%async_computation.3 | async-start | bytes 196608 | tf_op jit(solution)/shard_map/slice | solution.py:86
  29.6 8.4 %slice-start.2 = ((f32[1,1,20,2048]{3,1,2,0:T(1,128)}), f32[1,1,10,2048]{3,1,2,0:T(1,128)S(1)}, s32[]{:S(2)}) async-start(f32[1,1,20,2048]{3,1,2,0:T(1,128)} %copy-done.1), calls=%async_computation.4 | async-start | bytes 163840 | tf_op jit(solution)/shard_map/slice | solution.py:86
  29.6 8.4 %slice-start.3 = ((f32[1,1,20,2048]{3,1,2,0:T(1,128)}), f32[1,1,8,2048]{3,1,2,0:T(1,128)S(1)}, s32[]{:S(2)}) async-start(f32[1,1,20,2048]{3,1,2,0:T(1,128)} %copy-done.1), calls=%async_computation.5 | async-start | bytes 131072 | tf_op jit(solution)/shard_map/slice | solution.py:86
  30.0 11.7 %collective-permute-start.4 = (f32[1,2]{1,0:T(1,128)S(1)}, f32[1,2]{1,0:T(1,128)S(1)}, u32[]{:S(2)}, u32[]{:S(2)}) collective-permute-start(f32[1,2]{1,0:T(1,128)S(1)} %bitcast.143), channel_id=1, source_target_pairs={{0,1},{1,0},{2,3},{3,2},{4,5},{5,4},{6,7},{7,6},{8,9},{9,8},{10,11... | collective-permute-start | bytes 32 | tf_op jit(solution)/shard_map/ppermute | solution.py:40
  41.7 4.2 %collective-permute-start.5 = (f32[1,2]{1,0:T(1,128)S(1)}, f32[1,2]{1,0:T(1,128)S(1)}, u32[]{:S(2)}, u32[]{:S(2)}) collective-permute-start(f32[1,2]{1,0:T(1,128)S(1)} %bitcast_add_fusion.2), channel_id=1, source_target_pairs={{0,2},{1,3},{2,0},{3,1},{4,6},{5,7},{6,4},{7,5},{8,10},{9,11},{10,... | collective-permute-start | bytes 32 | tf_op jit(solution)/shard_map/ppermute | solution.py:40
  45.9 4.5 %collective-permute-start.6 = (f32[1,2]{1,0:T(1,128)S(1)}, f32[1,2]{1,0:T(1,128)S(1)}, u32[]{:S(2)}, u32[]{:S(2)}) collective-permute-start(f32[1,2]{1,0:T(1,128)S(1)} %add.277), channel_id=1, source_target_pairs={{0,4},{1,5},{2,6},{3,7},{4,0},{5,1},{6,2},{7,3},{8,12},{9,13},{10,... | collective-permute-start | bytes 32 | tf_op jit(solution)/shard_map/ppermute | solution.py:40
  52.5 2.1 %collective-permute-start.7 = (f32[1,3]{1,0:T(1,128)S(1)}, f32[1,3]{1,0:T(1,128)S(1)}, u32[]{:S(2)}, u32[]{:S(2)}) collective-permute-start(f32[1,3]{1,0:T(1,128)S(1)} %bitcast.145), channel_id=1, source_target_pairs={{0,1},{1,0},{2,3},{3,2},{4,5},{5,4},{6,7},{7,6},{8,9},{9,8},{10,11... | collective-permute-start | bytes 44 | tf_op jit(solution)/shard_map/ppermute | solution.py:40
  54.6 3.6 %collective-permute-start.8 = (f32[1,3]{1,0:T(1,128)S(1)}, f32[1,3]{1,0:T(1,128)S(1)}, u32[]{:S(2)}, u32[]{:S(2)}) collective-permute-start(f32[1,3]{1,0:T(1,128)S(1)} %bitcast_add_fusion.1), channel_id=1, source_target_pairs={{0,2},{1,3},{2,0},{3,1},{4,6},{5,7},{6,4},{7,5},{8,10},{9,11},{10,... | collective-permute-start | bytes 44 | tf_op jit(solution)/shard_map/ppermute | solution.py:40
  58.3 4.5 %collective-permute-start.9 = (f32[1,3]{1,0:T(1,128)S(1)}, f32[1,3]{1,0:T(1,128)S(1)}, u32[]{:S(2)}, u32[]{:S(2)}) collective-permute-start(f32[1,3]{1,0:T(1,128)S(1)} %add.293), channel_id=1, source_target_pairs={{0,4},{1,5},{2,6},{3,7},{4,0},{5,1},{6,2},{7,3},{8,12},{9,13},{10,... | collective-permute-start | bytes 44 | tf_op jit(solution)/shard_map/ppermute | solution.py:40
  64.5 1.2 %collective-permute-start.10 = (f32[1,3]{1,0:T(1,128)S(1)}, f32[1,3]{1,0:T(1,128)S(1)}, u32[]{:S(2)}, u32[]{:S(2)}) collective-permute-start(f32[1,3]{1,0:T(1,128)S(1)} %bitcast.146), channel_id=1, source_target_pairs={{0,1},{1,0},{2,3},{3,2},{4,5},{5,4},{6,7},{7,6},{8,9},{9,8},{10,11... | collective-permute-start | bytes 44 | tf_op jit(solution)/shard_map/ppermute | solution.py:40
  65.6 3.6 %collective-permute-start.11 = (f32[1,3]{1,0:T(1,128)S(1)}, f32[1,3]{1,0:T(1,128)S(1)}, u32[]{:S(2)}, u32[]{:S(2)}) collective-permute-start(f32[1,3]{1,0:T(1,128)S(1)} %bitcast_add_fusion), channel_id=1, source_target_pairs={{0,2},{1,3},{2,0},{3,1},{4,6},{5,7},{6,4},{7,5},{8,10},{9,11},{10,... | collective-permute-start | bytes 44 | tf_op jit(solution)/shard_map/ppermute | solution.py:40
  69.2 4.5 %collective-permute-start.12 = (f32[1,3]{1,0:T(1,128)S(1)}, f32[1,3]{1,0:T(1,128)S(1)}, u32[]{:S(2)}, u32[]{:S(2)}) collective-permute-start(f32[1,3]{1,0:T(1,128)S(1)} %add.303), channel_id=1, source_target_pairs={{0,4},{1,5},{2,6},{3,7},{4,0},{5,1},{6,2},{7,3},{8,12},{9,13},{10,... | collective-permute-start | bytes 44 | tf_op jit(solution)/shard_map/ppermute | solution.py:40
  76.3 22.7 %all-to-all-start.1 = ((f32[1,16,8,2048]{3,2,0,1:T(8,128)}), f32[1,16,8,2048]{3,2,0,1:T(8,128)S(1)}, u32[]{:S(2)}, u32[]{:S(2)}) async-start(f32[1,16,8,2048]{3,2,0,1:T(8,128)} %copy.12), calls=%async_computation.1 | async-start | bytes 2097152 | tf_op jit(solution)/shard_map/all_to_all | solution.py:155
  80.8 1.2 %collective-permute-start.13 = (f32[4,7]{1,0:T(4,128)S(1)}, f32[4,7]{1,0:T(4,128)S(1)}, u32[]{:S(2)}, u32[]{:S(2)}) collective-permute-start(f32[4,7]{1,0:T(4,128)S(1)} %dynamic_update_slice.5), channel_id=1, source_target_pairs={{0,1},{1,0},{2,3},{3,2},{4,5},{5,4},{6,7},{7,6},{8,9},{9,8},{10,11... | collective-permute-start | bytes 344 | tf_op jit(solution)/shard_map/ppermute | solution.py:40
  82.7 3.6 %collective-permute-start.14 = (f32[4,7]{1,0:T(4,128)S(1)}, f32[4,7]{1,0:T(4,128)S(1)}, u32[]{:S(2)}, u32[]{:S(2)}) collective-permute-start(f32[4,7]{1,0:T(4,128)S(1)} %add.307), channel_id=1, source_target_pairs={{0,2},{1,3},{2,0},{3,1},{4,6},{5,7},{6,4},{7,5},{8,10},{9,11},{10,... | collective-permute-start | bytes 344 | tf_op jit(solution)/shard_map/ppermute | solution.py:40
  86.4 4.5 %collective-permute-start.15 = (f32[4,7]{1,0:T(4,128)S(1)}, f32[4,7]{1,0:T(4,128)S(1)}, u32[]{:S(2)}, u32[]{:S(2)}) collective-permute-start(f32[4,7]{1,0:T(4,128)S(1)} %add.308), channel_id=1, source_target_pairs={{0,4},{1,5},{2,6},{3,7},{4,0},{5,1},{6,2},{7,3},{8,12},{9,13},{10,... | collective-permute-start | bytes 344 | tf_op jit(solution)/shard_map/ppermute | solution.py:40
  90.9 3.6 %collective-permute-start.16 = (f32[4,7]{1,0:T(4,128)S(1)}, f32[4,7]{1,0:T(4,128)S(1)}, u32[]{:S(2)}, u32[]{:S(2)}) collective-permute-start(f32[4,7]{1,0:T(4,128)S(1)} %add.309), channel_id=1, source_target_pairs={{0,8},{8,0},{16,24},{24,16},{1,9},{9,1},{17,25},{25,17},{2,10},{10... | collective-permute-start | bytes 344 | tf_op jit(solution)/shard_map/ppermute | solution.py:40
  94.5 3.6 %collective-permute-start.17 = (f32[4,7]{1,0:T(4,128)S(1)}, f32[4,7]{1,0:T(4,128)S(1)}, u32[]{:S(2)}, u32[]{:S(2)}) collective-permute-start(f32[4,7]{1,0:T(4,128)S(1)} %add.310), channel_id=1, source_target_pairs={{0,16},{8,24},{16,0},{24,8},{1,17},{9,25},{17,1},{25,9},{2,18},{10... | collective-permute-start | bytes 344 | tf_op jit(solution)/shard_map/ppermute | solution.py:40
  98.0 2.2 %copy-start.3 = (f32[4,7]{1,0:T(4,128)}, f32[4,7]{1,0:T(4,128)S(1)}, u32[]{:S(2)}) copy-start(f32[4,7]{1,0:T(4,128)S(1)} %add.311) | copy-start | bytes 340

commit v6 on v5

--- a/solution.py
+++ b/solution.py
@@ -127,7 +127,7 @@
     iters = 3
     for step in range(1, iters):
         last_step = step == iters - 1
-        sums, aaw = reduce_tile([(w, w), (aw, w), (q, w)], off, () if last_step else a_stages(aw, off, split_mix=True))
+        sums, aaw = reduce_tile([(w, w), (aw, w), (q, w)], off, () if last_step else a_stages(aw, off))
         sv = lanes(sums)
         beta_v = jnp.sqrt(sv[:, 0] + epsilon)
         alpha_v = sv[:, 1] / (beta_v * beta_v) - sv[:, 2]
@@ -159,16 +159,15 @@
     mine = jnp.concatenate([known * first, partial, norm[:, None] * first], axis=1)
     probes_local = mine.shape[0]
     n_trait = lax.axis_size("trait")
-    spread = lax.dynamic_update_slice(
-        jnp.zeros((probes_local * n_trait, mine.shape[1]), jnp.float32),
-        mine,
-        (lax.axis_index("trait") * probes_local, 0),
-    )
+    owner = lax.broadcasted_iota(jnp.int32, (probes_local * n_trait, 1), 0) // probes_local
+    spread = jnp.where(owner == lax.axis_index("trait"), jnp.tile(mine, (n_trait, 1)), 0.0)
     scalars = butterfly_sum(butterfly_sum(spread, "tile")[0], "trait")[0]
-    beta = jnp.sqrt(scalars[:, 2 * iters - 1] + epsilon)
+    tail = scalars[:, iters : 2 * iters]
+    last_col = lax.broadcasted_iota(jnp.int32, tail.shape, 1) == iters - 1
+    betas_all = jnp.where(last_col, jnp.sqrt(tail + epsilon), tail)
+    beta = betas_all[:, iters - 1]
     norm_all = scalars[:, 2 * iters]
     last = (w_back / beta[:, None, None, None]) * norm_all[:, None, None, None]
-    betas_all = jnp.concatenate([scalars[:, iters : 2 * iters - 1], beta[:, None]], axis=1)
     return scalars[:, :iters], betas_all, last
 
 

time: 101 us -> 103 us (1.020)
  waiting for transfers between devices: 23.9 us -> 26.1 us
  matrix products: 8.13 us -> 9.52 us
    ppermute x14, waiting for transfers between devices: 16.6 us -> 18.8 us  [butterfly_sum(): got = lax.ppermute(v, axis, [(i, i ^ s) for i in range(n)])]
    mul x5 -> x4, other arithmetic: 14.2 us -> 12.6 us  [stencil(): land_ext[off + 1:off + r - 1]]
    dot_general x3, matrix products: 8.13 us -> 9.52 us  [mix(): jnp.einsum('ts,psrc->ptrc', trait_covariance, x, precision=lax.Precision....]
    concatenate x2 -> x0, other arithmetic: 1.38 us -> none  [the longest x1 0.72 us: shards(): jnp.concatenate([known * first, partial, norm[:, None] * first], axis=1)]
    reduce_sum x1, other arithmetic: 0.93 us -> 2.14 us  [shards(): partial = jnp.sum(w_own * w_own, axis=(1, 2, 3))[:, None]]
  transfers between devices with their start and end apart: 20 -> 20, of which waited for: 13 -> 12; matrix products, arithmetic and copies ran while one was open for 16% -> 15% of each run, Pallas kernels for 0% -> 0%
where the time goes in v6:
time: 103 us
  starting transfers between devices  36.8 us (36%)
  waiting for transfers between devices  26.1 us (25%)
  other arithmetic  25.5 us (25%)
  matrix products  9.52 us (9%)
  local copies, waits for them, and re-layouts  3.84 us (4%)
  between operations  1.21 us (1%)
    ppermute x14, starting transfers between devices, butterfly_sum(): got = lax.ppermute(v, axis, [(i, i ^ s) for i in range(n)])  26.6 us
    ppermute x14, waiting for transfers between devices, butterfly_sum(): got = lax.ppermute(v, axis, [(i, i ^ s) for i in range(n)])  18.8 us
    mul x4, other arithmetic, stencil(): land_ext[off + 1:off + r - 1]  12.6 us
    dot_general x3, matrix products, mix(): jnp.einsum('ts,psrc->ptrc', trait_covariance, x, precision=lax.Precision....  9.52 us
    all_to_all x1, waiting for transfers between devices, shards(): lax.all_to_all(signed, 'trait', split_axis=0, concat_axis=1, tiled=True)  6.33 us
    all_to_all x1, starting transfers between devices, shards(): lax.all_to_all(signed, 'trait', split_axis=0, concat_axis=1, tiled=True)  5.19 us
    all_to_all x1, starting transfers between devices, shards(): lax.all_to_all(w_own, 'trait', split_axis=1, concat_axis=0, tiled=True)  3.52 us
    another operation x4, other arithmetic, reduce_tile(): prods = jnp.stack([own(a, off) * own(b, off) for a, b in pairs], axis=-1)  2.36 us
  transfers between devices with their start and end apart: 20, of which 12 were waited for; matrix products, arithmetic and copies ran while one was open for 15% of the time, Pallas kernels for 0%

profile of v6, /device:TPU:0, one launch (start us, length us, event | category | flops | bytes accessed | tf_op | source)
XLA Modules:
  0.0 103.0 jit_solution(12609016592419564484)
XLA Ops:
  0.7 2.2 %multiply_convert_fusion = bf16[4,4,8,2048]{3,2,1,0:T(8,128)(2,1)} fusion(s32[4,4,8,2048]{3,2,1,0:T(8,128)} %param.4, s32[8,2048]{1,0:T(8,128)} %param.5), kind=kLoop, calls=%fused_computation.157 | loop fusion | flops 1048576 | bytes 1638400 | tf_op jit(solution)/shard_map/convert_element_type | solution.py:73
  2.9 5.2 %all-to-all-start = ((bf16[4,4,8,2048]{3,2,1,0:T(8,128)(2,1)}), bf16[4,4,8,2048]{3,2,1,0:T(8,128)(2,1)S(1)}, u32[]{:S(2)}, u32[]{:S(2)}) async-start(bf16[4,4,8,2048]{3,2,1,0:T(8,128)(2,1)} %multiply_convert_fusion), calls=%async_computation | async-start | bytes 1048576 | tf_op jit(solution)/shard_map/all_to_all | solution.py:74
  9.8 6.3 %all-to-all-done = bf16[4,4,8,2048]{3,2,1,0:T(8,128)(2,1)S(1)} async-done(((bf16[4,4,8,2048]{3,2,1,0:T(8,128)(2,1)}), bf16[4,4,8,2048]{3,2,1,0:T(8,128)(2,1)S(1)}, u32[]{:S(2)}, u32[]{:S(2)}) %all-to-all-start) | async-done | bytes 524320 | tf_op jit(solution)/shard_map/all_to_all | solution.py:74
  19.4 4.4 %fusion.5 = f32[1,16,18,2048]{3,1,2,0:T(8,128)S(1)} fusion(f32[1,16,20,2048]{3,1,2,0:T(8,128)S(1)} %broadcast_multiply_fusion, f32[18,2048]{1,0:T(8,128)S(1)} %slice_add_fusion.4, f32[18,2048]{1,0:T(8,128)S(1)} %bitcast.121), kind=kLoop, calls=%fused_computation.17 | loop fusion | flops 7667712 | bytes 12451840 | tf_op jit(solution)/shard_map/mul | solution.py:86
  23.7 5.5 %convolution_bitcast_fusion = f32[1,16,16,2048]{3,1,2,0:T(8,128)S(1)} fusion(f32[1,16,18,2048]{3,1,2,0:T(8,128)S(1)} %fusion.5, f32[16,2048]{1,0:T(8,128)S(1)} %slice_add_fusion.8, f32[16,2048]{1,0:T(8,128)S(1)} %bitcast.125, f32[16,16]{1,0:T(8,128)S(1)} %copy-done), kind=kOutput, calls=%fused_computation.3 | convolution fusion | flops 107479040 | bytes 11018240 | tf_op jit(solution)/shard_map/ts,psrc->ptrc/dot_general | solution.py:82
  29.9 7.9 %collective-permute-start.4 = (f32[1,2]{1,0:T(1,128)S(1)}, f32[1,2]{1,0:T(1,128)S(1)}, u32[]{:S(2)}, u32[]{:S(2)}) collective-permute-start(f32[1,2]{1,0:T(1,128)S(1)} %bitcast.144), channel_id=1, source_target_pairs={{0,1},{1,0},{2,3},{3,2},{4,5},{5,4},{6,7},{7,6},{8,9},{9,8},{10,11... | collective-permute-start | bytes 32 | tf_op jit(solution)/shard_map/ppermute | solution.py:40
  37.9 3.7 %fusion.33 = f32[1,16,14,2048]{3,1,2,0:T(8,128)S(1)} fusion(f32[1,16,16,2048]{3,1,2,0:T(8,128)S(1)} %convolution_bitcast_fusion, f32[14,2048]{1,0:T(8,128)S(1)} %slice_add_fusion.7, f32[14,2048]{1,0:T(8,128)S(1)} %bitcast.124), kind=kLoop, calls=%fused_computation.60 | loop fusion | flops 5963776 | bytes 9699328 | tf_op jit(solution)/shard_map/mul | solution.py:86
  41.6 1.7 %collective-permute-start.5 = (f32[1,2]{1,0:T(1,128)S(1)}, f32[1,2]{1,0:T(1,128)S(1)}, u32[]{:S(2)}, u32[]{:S(2)}) collective-permute-start(f32[1,2]{1,0:T(1,128)S(1)} %bitcast_add_fusion.2), channel_id=1, source_target_pairs={{0,2},{1,3},{2,0},{3,1},{4,6},{5,7},{6,4},{7,5},{8,10},{9,11},{10,... | collective-permute-start | bytes 32 | tf_op jit(solution)/shard_map/ppermute | solution.py:40
  43.3 2.5 %fusion.44 = f32[1,16,12,2048]{3,1,2,0:T(8,128)S(1)} fusion(f32[1,16,14,2048]{3,1,2,0:T(8,128)S(1)} %fusion.33, f32[12,2048]{1,0:T(8,128)S(1)} %slice_add_fusion.6, f32[12,2048]{1,0:T(8,128)S(1)} %bitcast.122), kind=kLoop, calls=%fused_computation.79 | loop fusion | flops 5111808 | bytes 8388608 | tf_op jit(solution)/shard_map/mul | solution.py:86
  45.9 2.7 %collective-permute-start.6 = (f32[1,2]{1,0:T(1,128)S(1)}, f32[1,2]{1,0:T(1,128)S(1)}, u32[]{:S(2)}, u32[]{:S(2)}) collective-permute-start(f32[1,2]{1,0:T(1,128)S(1)} %add.270), channel_id=1, source_target_pairs={{0,4},{1,5},{2,6},{3,7},{4,0},{5,1},{6,2},{7,3},{8,12},{9,13},{10,... | collective-permute-start | bytes 32 | tf_op jit(solution)/shard_map/ppermute | solution.py:40
  48.5 1.5 %convolution_bitcast_fusion.1 = f32[1,16,12,2048]{3,1,2,0:T(8,128)S(1)} fusion(f32[1,16,12,2048]{3,1,2,0:T(8,128)S(1)} %fusion.44, f32[16,16]{1,0:T(8,128)S(1)} %copy-done), kind=kOutput, calls=%fused_computation.4 | convolution fusion | flops 75497472 | bytes 3146752 | tf_op jit(solution)/shard_map/ts,psrc->ptrc/dot_general | solution.py:82
  52.5 2.1 %fusion.56 = f32[1,16,10,2048]{3,1,2,0:T(8,128)S(1)} fusion(f32[1,16,12,2048]{3,1,2,0:T(8,128)S(1)} %fusion.49, f32[10,2048]{1,0:T(8,128)S(1)} %slice_add_fusion.5, f32[10,2048]{1,0:T(8,128)S(1)} %bitcast.123), kind=kLoop, calls=%fused_computation.99 | loop fusion | flops 4259840 | bytes 7077888 | tf_op jit(solution)/shard_map/mul | solution.py:86
  55.6 2.5 %convolution_bitcast_fusion.2 = f32[1,16,8,2048]{3,1,2,0:T(8,128)S(1)} fusion(f32[1,16,10,2048]{3,1,2,0:T(8,128)S(1)} %fusion.56, f32[8,2048]{1,0:T(8,128)S(1)} %broadcast_add_fusion, f32[8,2048]{1,0:T(8,128)S(1)} %bitcast.126, f32[16,16]{1,0:T(8,128)S(1)} %copy-done), kind=kOutput, calls=%fused_computation.5 | convolution fusion | flops 53739520 | bytes 5644288 | tf_op jit(solution)/shard_map/ts,psrc->ptrc/dot_general | solution.py:82
  58.2 2.6 %collective-permute-start.9 = (f32[1,3]{1,0:T(1,128)S(1)}, f32[1,3]{1,0:T(1,128)S(1)}, u32[]{:S(2)}, u32[]{:S(2)}) collective-permute-start(f32[1,3]{1,0:T(1,128)S(1)} %add.286), channel_id=1, source_target_pairs={{0,4},{1,5},{2,6},{3,7},{4,0},{5,1},{6,2},{7,3},{8,12},{9,13},{10,... | collective-permute-start | bytes 44 | tf_op jit(solution)/shard_map/ppermute | solution.py:40
  60.8 1.9 %collective-permute-done.9 = f32[1,3]{1,0:T(1,128)S(1)} collective-permute-done((f32[1,3]{1,0:T(1,128)S(1)}, f32[1,3]{1,0:T(1,128)S(1)}, u32[]{:S(2)}, u32[]{:S(2)}) %collective-permute-start.9) | collective-permute-done | bytes 44 | tf_op jit(solution)/shard_map/ppermute | solution.py:40
  63.4 1.5 %multiply_bitcast_fusion.1 = (f32[1,16,8,2048,1]{3,1,2,4,0:T(8,128)S(1)}, f32[1,16,8,2048]{3,1,2,0:T(8,128)}, f32[1,16,8,2048,1]{3,1,2,4,0:T(8,128)S(1)}) fusion(f32[1,16,8,2048]{3,1,2,0:T(8,128)S(1)} %get-tuple-element.26, f32[1,16,12,2048]{3,1,2,0:T(8,128)S(1)} %fusion.49, f32[]{:T(128)S(1)} %bitcast.128, f32[1,16,16,2048]{3,1,2,0:T(8,128)S(1)} %get-tuple-element.30, ...), kind=kLoop, calls=%fused_computation.140 | loop fusion | flops 2097152 | bytes 8388616 | tf_op jit(solution)/shard_map/stack | solution.py:106
  65.4 1.1 %collective-permute-done.10 = f32[1,3]{1,0:T(1,128)S(1)} collective-permute-done((f32[1,3]{1,0:T(1,128)S(1)}, f32[1,3]{1,0:T(1,128)S(1)}, u32[]{:S(2)}, u32[]{:S(2)}) %collective-permute-start.10) | collective-permute-done | bytes 44 | tf_op jit(solution)/shard_map/ppermute | solution.py:40
  67.6 2.5 %collective-permute-done.11 = f32[1,3]{1,0:T(1,128)S(1)} collective-permute-done((f32[1,3]{1,0:T(1,128)S(1)}, f32[1,3]{1,0:T(1,128)S(1)}, u32[]{:S(2)}, u32[]{:S(2)}) %collective-permute-start.11) | collective-permute-done | bytes 44 | tf_op jit(solution)/shard_map/ppermute | solution.py:40
  70.1 2.6 %collective-permute-start.12 = (f32[1,3]{1,0:T(1,128)S(1)}, f32[1,3]{1,0:T(1,128)S(1)}, u32[]{:S(2)}, u32[]{:S(2)}) collective-permute-start(f32[1,3]{1,0:T(1,128)S(1)} %add.296), channel_id=1, source_target_pairs={{0,4},{1,5},{2,6},{3,7},{4,0},{5,1},{6,2},{7,3},{8,12},{9,13},{10,... | collective-permute-start | bytes 44 | tf_op jit(solution)/shard_map/ppermute | solution.py:40
  72.7 1.9 %collective-permute-done.12 = f32[1,3]{1,0:T(1,128)S(1)} collective-permute-done((f32[1,3]{1,0:T(1,128)S(1)}, f32[1,3]{1,0:T(1,128)S(1)}, u32[]{:S(2)}, u32[]{:S(2)}) %collective-permute-start.12) | collective-permute-done | bytes 44 | tf_op jit(solution)/shard_map/ppermute | solution.py:40
  74.8 2.1 %multiply_reduce_fusion = (f32[]{:T(128)}, f32[1,16,8,2048]{3,1,2,0:T(8,128)S(1)}) fusion(f32[1,16,8,2048]{3,1,2,0:T(8,128)S(1)} %get-tuple-element.26, f32[]{:T(128)S(1)} %bitcast.138, f32[1,16,12,2048]{3,1,2,0:T(8,128)S(1)} %slice_divide_fusion.1, f32[1,16,8,2048]{3,1,2,0:T(8,128)} %get-tuple-element.28, f32[]{:T(128)S(1)} %bitcast.143), kind=kLoop, calls=%fused_computation.137 | loop fusion | flops 2097151 | bytes 4194316 | tf_op jit(solution)/shard_map/reduce_sum | solution.py:156
  77.7 1.6 %copy.12 = f32[1,16,8,2048]{3,2,0,1:T(8,128)} copy(f32[1,16,8,2048]{3,1,2,0:T(8,128)S(1)} %get-tuple-element.24) | data formatting | bytes 2097152 | tf_op jit(solution)/shard_map/sub | solution.py:137
  79.3 3.5 %all-to-all-start.1 = ((f32[1,16,8,2048]{3,2,0,1:T(8,128)}), f32[1,16,8,2048]{3,2,0,1:T(8,128)S(1)}, u32[]{:S(2)}, u32[]{:S(2)}) async-start(f32[1,16,8,2048]{3,2,0,1:T(8,128)} %copy.12), calls=%async_computation.1 | async-start | bytes 2097152 | tf_op jit(solution)/shard_map/all_to_all | solution.py:155
  82.9 1.1 %collective-permute-start.14 = (f32[4,7]{1,0:T(4,128)S(1)}, f32[4,7]{1,0:T(4,128)S(1)}, u32[]{:S(2)}, u32[]{:S(2)}) collective-permute-start(f32[4,7]{1,0:T(4,128)S(1)} %fusion.109), channel_id=1, source_target_pairs={{0,2},{1,3},{2,0},{3,1},{4,6},{5,7},{6,4},{7,5},{8,10},{9,11},{10,... | collective-permute-start | bytes 344 | tf_op jit(solution)/shard_map/ppermute | solution.py:40
  84.0 2.5 %collective-permute-done.14 = f32[4,7]{1,0:T(4,128)S(1)} collective-permute-done((f32[4,7]{1,0:T(4,128)S(1)}, f32[4,7]{1,0:T(4,128)S(1)}, u32[]{:S(2)}, u32[]{:S(2)}) %collective-permute-start.14) | collective-permute-done | bytes 144 | tf_op jit(solution)/shard_map/ppermute | solution.py:40
  86.6 2.6 %collective-permute-start.15 = (f32[4,7]{1,0:T(4,128)S(1)}, f32[4,7]{1,0:T(4,128)S(1)}, u32[]{:S(2)}, u32[]{:S(2)}) collective-permute-start(f32[4,7]{1,0:T(4,128)S(1)} %fusion.112), channel_id=1, source_target_pairs={{0,4},{1,5},{2,6},{3,7},{4,0},{5,1},{6,2},{7,3},{8,12},{9,13},{10,... | collective-permute-start | bytes 344 | tf_op jit(solution)/shard_map/ppermute | solution.py:40
  89.2 1.9 %collective-permute-done.15 = f32[4,7]{1,0:T(4,128)S(1)} collective-permute-done((f32[4,7]{1,0:T(4,128)S(1)}, f32[4,7]{1,0:T(4,128)S(1)}, u32[]{:S(2)}, u32[]{:S(2)}) %collective-permute-start.15) | collective-permute-done | bytes 144 | tf_op jit(solution)/shard_map/ppermute | solution.py:40
  91.1 2.0 %collective-permute-start.16 = (f32[4,7]{1,0:T(4,128)S(1)}, f32[4,7]{1,0:T(4,128)S(1)}, u32[]{:S(2)}, u32[]{:S(2)}) collective-permute-start(f32[4,7]{1,0:T(4,128)S(1)} %add.301), channel_id=1, source_target_pairs={{0,8},{8,0},{16,24},{24,16},{1,9},{9,1},{17,25},{25,17},{2,10},{10... | collective-permute-start | bytes 344 | tf_op jit(solution)/shard_map/ppermute | solution.py:40
  93.1 4.4 %collective-permute-done.16 = f32[4,7]{1,0:T(4,128)S(1)} collective-permute-done((f32[4,7]{1,0:T(4,128)S(1)}, f32[4,7]{1,0:T(4,128)S(1)}, u32[]{:S(2)}, u32[]{:S(2)}) %collective-permute-start.16) | collective-permute-done | bytes 144 | tf_op jit(solution)/shard_map/ppermute | solution.py:40
  97.5 1.5 %collective-permute-start.17 = (f32[4,7]{1,0:T(4,128)S(1)}, f32[4,7]{1,0:T(4,128)S(1)}, u32[]{:S(2)}, u32[]{:S(2)}) collective-permute-start(f32[4,7]{1,0:T(4,128)S(1)} %add.302), channel_id=1, source_target_pairs={{0,16},{8,24},{16,0},{24,8},{1,17},{9,25},{17,1},{25,9},{2,18},{10... | collective-permute-start | bytes 344 | tf_op jit(solution)/shard_map/ppermute | solution.py:40
  98.9 2.1 %collective-permute-done.17 = f32[4,7]{1,0:T(4,128)S(1)} collective-permute-done((f32[4,7]{1,0:T(4,128)S(1)}, f32[4,7]{1,0:T(4,128)S(1)}, u32[]{:S(2)}, u32[]{:S(2)}) %collective-permute-start.17) | collective-permute-done | bytes 144 | tf_op jit(solution)/shard_map/ppermute | solution.py:40
  101.8 1.2 %divide_multiply_fusion = f32[4,4,8,2048]{3,2,1,0:T(8,128)} fusion(f32[4,4,8,2048]{3,2,1,0:T(8,128)S(1)} %bitcast.119, f32[4]{0:T(128)S(1)} %get-tuple-element.48, f32[4]{0:T(128)S(1)} %get-tuple-element.49), kind=kLoop, calls=%fused_computation.136 | loop fusion | flops 524288 | bytes 2097184 | tf_op jit(solution)/shard_map/mul | solution.py:170
  (102 shorter events, 13.1 us)
Async XLA Ops:
  0.6 8.3 %copy-start = (f32[16,16]{1,0:T(8,128)S(1)}, f32[16,16]{1,0:T(8,128)}, u32[]{:S(2)}) copy-start(f32[16,16]{1,0:T(8,128)} %param.7) | copy-start | bytes 3076
  0.6 7.4 %copy-start.2 = (f32[8,2048]{1,0:T(8,128)S(1)}, f32[8,2048]{1,0:T(8,128)}, u32[]{:S(2)}) copy-start(f32[8,2048]{1,0:T(8,128)} %param.6) | copy-start | bytes 196612
  2.9 13.2 %all-to-all-start = ((bf16[4,4,8,2048]{3,2,1,0:T(8,128)(2,1)}), bf16[4,4,8,2048]{3,2,1,0:T(8,128)(2,1)S(1)}, u32[]{:S(2)}, u32[]{:S(2)}) async-start(bf16[4,4,8,2048]{3,2,1,0:T(8,128)(2,1)} %multiply_convert_fusion), calls=%async_computation | async-start | bytes 1048576 | tf_op jit(solution)/shard_map/all_to_all | solution.py:74
  8.1 1.5 %collective-permute-start.2 = (f32[6,2048]{1,0:T(8,128)S(1)}, f32[6,2048]{1,0:T(8,128)S(1)}, u32[]{:S(2)}, u32[]{:S(2)}) collective-permute-start(f32[6,2048]{1,0:T(8,128)S(1)} %get-tuple-element.44), channel_id=1, source_target_pairs={{0,1},{2,3},{4,5},{6,7},{1,0},{3,2},{5,4},{7,6},{8,9},{10,11},{12,... | collective-permute-start | bytes 147464 | tf_op jit(solution)/shard_map/ppermute | solution.py:64
  8.2 1.4 %collective-permute-start.3 = (f32[6,2048]{1,0:T(8,128)S(1)}, f32[6,2048]{1,0:T(8,128)S(1)}, u32[]{:S(2)}, u32[]{:S(2)}) collective-permute-start(f32[6,2048]{1,0:T(8,128)S(1)} %get-tuple-element.45), channel_id=1, source_target_pairs={{1,2},{3,4},{5,6},{2,1},{4,3},{6,5},{9,10},{11,12},{13,14},{10,9},... | collective-permute-start | bytes 147464 | tf_op jit(solution)/shard_map/ppermute | solution.py:63
  16.4 1.8 %collective-permute-start = (bf16[1,16,6,2048]{3,1,2,0:T(8,128)(2,1)S(1)}, bf16[1,16,6,2048]{3,1,2,0:T(8,128)(2,1)S(1)}, u32[]{:S(2)}, u32[]{:S(2)}) collective-permute-start(bf16[1,16,6,2048]{3,1,2,0:T(8,128)(2,1)S(1)} %get-tuple-element.40), channel_id=1, source_target_pairs={{0,1},{2,3},{4,5},{6,7},{1,0},{3,2},{5,4},{7,6},{8,9},{10,11},{12,... | collective-permute-start | bytes 1179656 | tf_op jit(solution)/shard_map/ppermute | solution.py:64
  16.5 1.7 %collective-permute-start.1 = (bf16[1,16,6,2048]{3,1,2,0:T(8,128)(2,1)S(1)}, bf16[1,16,6,2048]{3,1,2,0:T(8,128)(2,1)S(1)}, u32[]{:S(2)}, u32[]{:S(2)}) collective-permute-start(bf16[1,16,6,2048]{3,1,2,0:T(8,128)(2,1)S(1)} %get-tuple-element.41), channel_id=1, source_target_pairs={{1,2},{3,4},{5,6},{2,1},{4,3},{6,5},{9,10},{11,12},{13,14},{10,9},... | collective-permute-start | bytes 1179656 | tf_op jit(solution)/shard_map/ppermute | solution.py:63
  18.6 0.7 copy-start.1
  29.5 8.3 %slice-start = ((f32[1,1,20,2048]{3,1,2,0:T(1,128)}), f32[1,1,14,2048]{3,1,2,0:T(1,128)S(1)}, s32[]{:S(2)}) async-start(f32[1,1,20,2048]{3,1,2,0:T(1,128)} %copy-done.1), calls=%async_computation.2 | async-start | bytes 229376 | tf_op jit(solution)/shard_map/slice | solution.py:86
  29.5 8.3 %slice-start.1 = ((f32[1,1,20,2048]{3,1,2,0:T(1,128)}), f32[1,1,12,2048]{3,1,2,0:T(1,128)S(1)}, s32[]{:S(2)}) async-start(f32[1,1,20,2048]{3,1,2,0:T(1,128)} %copy-done.1), calls=%async_computation.3 | async-start | bytes 196608 | tf_op jit(solution)/shard_map/slice | solution.py:86
  29.5 8.4 %slice-start.2 = ((f32[1,1,20,2048]{3,1,2,0:T(1,128)}), f32[1,1,10,2048]{3,1,2,0:T(1,128)S(1)}, s32[]{:S(2)}) async-start(f32[1,1,20,2048]{3,1,2,0:T(1,128)} %copy-done.1), calls=%async_computation.4 | async-start | bytes 163840 | tf_op jit(solution)/shard_map/slice | solution.py:86
  29.5 8.4 %slice-start.3 = ((f32[1,1,20,2048]{3,1,2,0:T(1,128)}), f32[1,1,8,2048]{3,1,2,0:T(1,128)S(1)}, s32[]{:S(2)}) async-start(f32[1,1,20,2048]{3,1,2,0:T(1,128)} %copy-done.1), calls=%async_computation.5 | async-start | bytes 131072 | tf_op jit(solution)/shard_map/slice | solution.py:86
  29.9 11.7 %collective-permute-start.4 = (f32[1,2]{1,0:T(1,128)S(1)}, f32[1,2]{1,0:T(1,128)S(1)}, u32[]{:S(2)}, u32[]{:S(2)}) collective-permute-start(f32[1,2]{1,0:T(1,128)S(1)} %bitcast.144), channel_id=1, source_target_pairs={{0,1},{1,0},{2,3},{3,2},{4,5},{5,4},{6,7},{7,6},{8,9},{9,8},{10,11... | collective-permute-start | bytes 32 | tf_op jit(solution)/shard_map/ppermute | solution.py:40
  41.6 4.2 %collective-permute-start.5 = (f32[1,2]{1,0:T(1,128)S(1)}, f32[1,2]{1,0:T(1,128)S(1)}, u32[]{:S(2)}, u32[]{:S(2)}) collective-permute-start(f32[1,2]{1,0:T(1,128)S(1)} %bitcast_add_fusion.2), channel_id=1, source_target_pairs={{0,2},{1,3},{2,0},{3,1},{4,6},{5,7},{6,4},{7,5},{8,10},{9,11},{10,... | collective-permute-start | bytes 32 | tf_op jit(solution)/shard_map/ppermute | solution.py:40
  45.9 4.5 %collective-permute-start.6 = (f32[1,2]{1,0:T(1,128)S(1)}, f32[1,2]{1,0:T(1,128)S(1)}, u32[]{:S(2)}, u32[]{:S(2)}) collective-permute-start(f32[1,2]{1,0:T(1,128)S(1)} %add.270), channel_id=1, source_target_pairs={{0,4},{1,5},{2,6},{3,7},{4,0},{5,1},{6,2},{7,3},{8,12},{9,13},{10,... | collective-permute-start | bytes 32 | tf_op jit(solution)/shard_map/ppermute | solution.py:40
  52.5 2.1 %collective-permute-start.7 = (f32[1,3]{1,0:T(1,128)S(1)}, f32[1,3]{1,0:T(1,128)S(1)}, u32[]{:S(2)}, u32[]{:S(2)}) collective-permute-start(f32[1,3]{1,0:T(1,128)S(1)} %bitcast.145), channel_id=1, source_target_pairs={{0,1},{1,0},{2,3},{3,2},{4,5},{5,4},{6,7},{7,6},{8,9},{9,8},{10,11... | collective-permute-start | bytes 44 | tf_op jit(solution)/shard_map/ppermute | solution.py:40
  54.6 3.6 %collective-permute-start.8 = (f32[1,3]{1,0:T(1,128)S(1)}, f32[1,3]{1,0:T(1,128)S(1)}, u32[]{:S(2)}, u32[]{:S(2)}) collective-permute-start(f32[1,3]{1,0:T(1,128)S(1)} %bitcast_add_fusion.1), channel_id=1, source_target_pairs={{0,2},{1,3},{2,0},{3,1},{4,6},{5,7},{6,4},{7,5},{8,10},{9,11},{10,... | collective-permute-start | bytes 44 | tf_op jit(solution)/shard_map/ppermute | solution.py:40
  58.2 4.5 %collective-permute-start.9 = (f32[1,3]{1,0:T(1,128)S(1)}, f32[1,3]{1,0:T(1,128)S(1)}, u32[]{:S(2)}, u32[]{:S(2)}) collective-permute-start(f32[1,3]{1,0:T(1,128)S(1)} %add.286), channel_id=1, source_target_pairs={{0,4},{1,5},{2,6},{3,7},{4,0},{5,1},{6,2},{7,3},{8,12},{9,13},{10,... | collective-permute-start | bytes 44 | tf_op jit(solution)/shard_map/ppermute | solution.py:40
  65.3 1.2 %collective-permute-start.10 = (f32[1,3]{1,0:T(1,128)S(1)}, f32[1,3]{1,0:T(1,128)S(1)}, u32[]{:S(2)}, u32[]{:S(2)}) collective-permute-start(f32[1,3]{1,0:T(1,128)S(1)} %bitcast.146), channel_id=1, source_target_pairs={{0,1},{1,0},{2,3},{3,2},{4,5},{5,4},{6,7},{7,6},{8,9},{9,8},{10,11... | collective-permute-start | bytes 44 | tf_op jit(solution)/shard_map/ppermute | solution.py:40
  66.5 3.6 %collective-permute-start.11 = (f32[1,3]{1,0:T(1,128)S(1)}, f32[1,3]{1,0:T(1,128)S(1)}, u32[]{:S(2)}, u32[]{:S(2)}) collective-permute-start(f32[1,3]{1,0:T(1,128)S(1)} %bitcast_add_fusion), channel_id=1, source_target_pairs={{0,2},{1,3},{2,0},{3,1},{4,6},{5,7},{6,4},{7,5},{8,10},{9,11},{10,... | collective-permute-start | bytes 44 | tf_op jit(solution)/shard_map/ppermute | solution.py:40
  70.1 4.5 %collective-permute-start.12 = (f32[1,3]{1,0:T(1,128)S(1)}, f32[1,3]{1,0:T(1,128)S(1)}, u32[]{:S(2)}, u32[]{:S(2)}) collective-permute-start(f32[1,3]{1,0:T(1,128)S(1)} %add.296), channel_id=1, source_target_pairs={{0,4},{1,5},{2,6},{3,7},{4,0},{5,1},{6,2},{7,3},{8,12},{9,13},{10,... | collective-permute-start | bytes 44 | tf_op jit(solution)/shard_map/ppermute | solution.py:40
  77.7 5.1 %collective-permute-start.13 = (f32[4,7]{1,0:T(4,128)S(1)}, f32[4,7]{1,0:T(4,128)S(1)}, u32[]{:S(2)}, u32[]{:S(2)}) collective-permute-start(f32[4,7]{1,0:T(4,128)S(1)} %broadcast_select_fusion.6), channel_id=1, source_target_pairs={{0,1},{1,0},{2,3},{3,2},{4,5},{5,4},{6,7},{7,6},{8,9},{9,8},{10,11... | collective-permute-start | bytes 344 | tf_op jit(solution)/shard_map/ppermute | solution.py:40
  79.3 22.5 %all-to-all-start.1 = ((f32[1,16,8,2048]{3,2,0,1:T(8,128)}), f32[1,16,8,2048]{3,2,0,1:T(8,128)S(1)}, u32[]{:S(2)}, u32[]{:S(2)}) async-start(f32[1,16,8,2048]{3,2,0,1:T(8,128)} %copy.12), calls=%async_computation.1 | async-start | bytes 2097152 | tf_op jit(solution)/shard_map/all_to_all | solution.py:155
  82.9 3.6 %collective-permute-start.14 = (f32[4,7]{1,0:T(4,128)S(1)}, f32[4,7]{1,0:T(4,128)S(1)}, u32[]{:S(2)}, u32[]{:S(2)}) collective-permute-start(f32[4,7]{1,0:T(4,128)S(1)} %fusion.109), channel_id=1, source_target_pairs={{0,2},{1,3},{2,0},{3,1},{4,6},{5,7},{6,4},{7,5},{8,10},{9,11},{10,... | collective-permute-start | bytes 344 | tf_op jit(solution)/shard_map/ppermute | solution.py:40
  86.6 4.5 %collective-permute-start.15 = (f32[4,7]{1,0:T(4,128)S(1)}, f32[4,7]{1,0:T(4,128)S(1)}, u32[]{:S(2)}, u32[]{:S(2)}) collective-permute-start(f32[4,7]{1,0:T(4,128)S(1)} %fusion.112), channel_id=1, source_target_pairs={{0,4},{1,5},{2,6},{3,7},{4,0},{5,1},{6,2},{7,3},{8,12},{9,13},{10,... | collective-permute-start | bytes 344 | tf_op jit(solution)/shard_map/ppermute | solution.py:40
  91.1 6.4 %collective-permute-start.16 = (f32[4,7]{1,0:T(4,128)S(1)}, f32[4,7]{1,0:T(4,128)S(1)}, u32[]{:S(2)}, u32[]{:S(2)}) collective-permute-start(f32[4,7]{1,0:T(4,128)S(1)} %add.301), channel_id=1, source_target_pairs={{0,8},{8,0},{16,24},{24,16},{1,9},{9,1},{17,25},{25,17},{2,10},{10... | collective-permute-start | bytes 344 | tf_op jit(solution)/shard_map/ppermute | solution.py:40
  97.5 3.6 %collective-permute-start.17 = (f32[4,7]{1,0:T(4,128)S(1)}, f32[4,7]{1,0:T(4,128)S(1)}, u32[]{:S(2)}, u32[]{:S(2)}) collective-permute-start(f32[4,7]{1,0:T(4,128)S(1)} %add.302), channel_id=1, source_target_pairs={{0,16},{8,24},{16,0},{24,8},{1,17},{9,25},{17,1},{25,9},{2,18},{10... | collective-permute-start | bytes 344 | tf_op jit(solution)/shard_map/ppermute | solution.py:40
  101.6 1.4 %copy-start.3 = (f32[4,3]{1,0:T(4,128)}, f32[4,3]{1,0:T(4,128)S(1)}, u32[]{:S(2)}) copy-start(f32[4,3]{1,0:T(4,128)S(1)} %get-tuple-element.46) | copy-start | bytes 148

commit v7 on v6

--- a/solution.py
+++ b/solution.py
@@ -159,8 +159,11 @@
     mine = jnp.concatenate([known * first, partial, norm[:, None] * first], axis=1)
     probes_local = mine.shape[0]
     n_trait = lax.axis_size("trait")
-    owner = lax.broadcasted_iota(jnp.int32, (probes_local * n_trait, 1), 0) // probes_local
-    spread = jnp.where(owner == lax.axis_index("trait"), jnp.tile(mine, (n_trait, 1)), 0.0)
+    spread = lax.dynamic_update_slice(
+        jnp.zeros((probes_local * n_trait, mine.shape[1]), jnp.float32),
+        mine,
+        (lax.axis_index("trait") * probes_local, 0),
+    )
     scalars = butterfly_sum(butterfly_sum(spread, "tile")[0], "trait")[0]
     tail = scalars[:, iters : 2 * iters]
     last_col = lax.broadcasted_iota(jnp.int32, tail.shape, 1) == iters - 1

time: 103 us -> 102 us (level)
  waiting for transfers between devices: 26.1 us -> 24 us
    ppermute x14, waiting for transfers between devices: 18.8 us -> 16.7 us  [butterfly_sum(): got = lax.ppermute(v, axis, [(i, i ^ s) for i in range(n)])]
  transfers between devices with their start and end apart: 20 -> 20, of which waited for: 12 -> 13; matrix products, arithmetic and copies ran while one was open for 15% -> 15% of each run, Pallas kernels for 0% -> 0%
where the time goes in v7:
time: 102 us
  starting transfers between devices  37.4 us (37%)
  other arithmetic  26 us (25%)
  waiting for transfers between devices  24 us (24%)
  matrix products  9.52 us (9%)
  local copies, waits for them, and re-layouts  3.91 us (4%)
  between operations  1.21 us (1%)
    ppermute x14, starting transfers between devices, butterfly_sum(): got = lax.ppermute(v, axis, [(i, i ^ s) for i in range(n)])  27.2 us
    ppermute x14, waiting for transfers between devices, butterfly_sum(): got = lax.ppermute(v, axis, [(i, i ^ s) for i in range(n)])  16.7 us
    mul x4, other arithmetic, stencil(): land_ext[off + 1:off + r - 1]  12.6 us
    dot_general x3, matrix products, mix(): jnp.einsum('ts,psrc->ptrc', trait_covariance, x, precision=lax.Precision....  9.52 us
    all_to_all x1, waiting for transfers between devices, shards(): lax.all_to_all(signed, 'trait', split_axis=0, concat_axis=1, tiled=True)  6.35 us
    all_to_all x1, starting transfers between devices, shards(): lax.all_to_all(signed, 'trait', split_axis=0, concat_axis=1, tiled=True)  5.19 us
    all_to_all x1, starting transfers between devices, shards(): lax.all_to_all(w_own, 'trait', split_axis=1, concat_axis=0, tiled=True)  3.52 us
    another operation x4, other arithmetic, reduce_tile(): prods = jnp.stack([own(a, off) * own(b, off) for a, b in pairs], axis=-1)  2.36 us
  transfers between devices with their start and end apart: 20, of which 13 were waited for; matrix products, arithmetic and copies ran while one was open for 15% of the time, Pallas kernels for 0%

profile of v7, /device:TPU:0, one launch (start us, length us, event | category | flops | bytes accessed | tf_op | source)
XLA Modules:
  0.0 102.1 jit_solution(8816758804492666072)
XLA Ops:
  0.7 2.2 %multiply_convert_fusion = bf16[4,4,8,2048]{3,2,1,0:T(8,128)(2,1)} fusion(s32[4,4,8,2048]{3,2,1,0:T(8,128)} %param.4, s32[8,2048]{1,0:T(8,128)} %param.5), kind=kLoop, calls=%fused_computation.157 | loop fusion | flops 1048576 | bytes 1638400 | tf_op jit(solution)/shard_map/convert_element_type | solution.py:73
  2.9 5.2 %all-to-all-start = ((bf16[4,4,8,2048]{3,2,1,0:T(8,128)(2,1)}), bf16[4,4,8,2048]{3,2,1,0:T(8,128)(2,1)S(1)}, u32[]{:S(2)}, u32[]{:S(2)}) async-start(bf16[4,4,8,2048]{3,2,1,0:T(8,128)(2,1)} %multiply_convert_fusion), calls=%async_computation | async-start | bytes 1048576 | tf_op jit(solution)/shard_map/all_to_all | solution.py:74
  9.7 6.3 %all-to-all-done = bf16[4,4,8,2048]{3,2,1,0:T(8,128)(2,1)S(1)} async-done(((bf16[4,4,8,2048]{3,2,1,0:T(8,128)(2,1)}), bf16[4,4,8,2048]{3,2,1,0:T(8,128)(2,1)S(1)}, u32[]{:S(2)}, u32[]{:S(2)}) %all-to-all-start) | async-done | bytes 524320 | tf_op jit(solution)/shard_map/all_to_all | solution.py:74
  19.4 4.4 %fusion.5 = f32[1,16,18,2048]{3,1,2,0:T(8,128)S(1)} fusion(f32[1,16,20,2048]{3,1,2,0:T(8,128)S(1)} %broadcast_multiply_fusion, f32[18,2048]{1,0:T(8,128)S(1)} %slice_add_fusion.4, f32[18,2048]{1,0:T(8,128)S(1)} %bitcast.119), kind=kLoop, calls=%fused_computation.17 | loop fusion | flops 7667712 | bytes 12451840 | tf_op jit(solution)/shard_map/mul | solution.py:86
  23.7 5.5 %convolution_bitcast_fusion = f32[1,16,16,2048]{3,1,2,0:T(8,128)S(1)} fusion(f32[1,16,18,2048]{3,1,2,0:T(8,128)S(1)} %fusion.5, f32[16,2048]{1,0:T(8,128)S(1)} %slice_add_fusion.8, f32[16,2048]{1,0:T(8,128)S(1)} %bitcast.123, f32[16,16]{1,0:T(8,128)S(1)} %copy-done), kind=kOutput, calls=%fused_computation.3 | convolution fusion | flops 107479040 | bytes 11018240 | tf_op jit(solution)/shard_map/ts,psrc->ptrc/dot_general | solution.py:82
  29.9 7.9 %collective-permute-start.4 = (f32[1,2]{1,0:T(1,128)S(1)}, f32[1,2]{1,0:T(1,128)S(1)}, u32[]{:S(2)}, u32[]{:S(2)}) collective-permute-start(f32[1,2]{1,0:T(1,128)S(1)} %bitcast.142), channel_id=1, source_target_pairs={{0,1},{1,0},{2,3},{3,2},{4,5},{5,4},{6,7},{7,6},{8,9},{9,8},{10,11... | collective-permute-start | bytes 32 | tf_op jit(solution)/shard_map/ppermute | solution.py:40
  37.9 3.7 %fusion.33 = f32[1,16,14,2048]{3,1,2,0:T(8,128)S(1)} fusion(f32[1,16,16,2048]{3,1,2,0:T(8,128)S(1)} %convolution_bitcast_fusion, f32[14,2048]{1,0:T(8,128)S(1)} %slice_add_fusion.7, f32[14,2048]{1,0:T(8,128)S(1)} %bitcast.122), kind=kLoop, calls=%fused_computation.60 | loop fusion | flops 5963776 | bytes 9699328 | tf_op jit(solution)/shard_map/mul | solution.py:86
  41.6 1.7 %collective-permute-start.5 = (f32[1,2]{1,0:T(1,128)S(1)}, f32[1,2]{1,0:T(1,128)S(1)}, u32[]{:S(2)}, u32[]{:S(2)}) collective-permute-start(f32[1,2]{1,0:T(1,128)S(1)} %bitcast_add_fusion.2), channel_id=1, source_target_pairs={{0,2},{1,3},{2,0},{3,1},{4,6},{5,7},{6,4},{7,5},{8,10},{9,11},{10,... | collective-permute-start | bytes 32 | tf_op jit(solution)/shard_map/ppermute | solution.py:40
  43.3 2.5 %fusion.44 = f32[1,16,12,2048]{3,1,2,0:T(8,128)S(1)} fusion(f32[1,16,14,2048]{3,1,2,0:T(8,128)S(1)} %fusion.33, f32[12,2048]{1,0:T(8,128)S(1)} %slice_add_fusion.6, f32[12,2048]{1,0:T(8,128)S(1)} %bitcast.120), kind=kLoop, calls=%fused_computation.79 | loop fusion | flops 5111808 | bytes 8388608 | tf_op jit(solution)/shard_map/mul | solution.py:86
  45.9 2.7 %collective-permute-start.6 = (f32[1,2]{1,0:T(1,128)S(1)}, f32[1,2]{1,0:T(1,128)S(1)}, u32[]{:S(2)}, u32[]{:S(2)}) collective-permute-start(f32[1,2]{1,0:T(1,128)S(1)} %add.271), channel_id=1, source_target_pairs={{0,4},{1,5},{2,6},{3,7},{4,0},{5,1},{6,2},{7,3},{8,12},{9,13},{10,... | collective-permute-start | bytes 32 | tf_op jit(solution)/shard_map/ppermute | solution.py:40
  48.5 1.5 %convolution_bitcast_fusion.1 = f32[1,16,12,2048]{3,1,2,0:T(8,128)S(1)} fusion(f32[1,16,12,2048]{3,1,2,0:T(8,128)S(1)} %fusion.44, f32[16,16]{1,0:T(8,128)S(1)} %copy-done), kind=kOutput, calls=%fused_computation.4 | convolution fusion | flops 75497472 | bytes 3146752 | tf_op jit(solution)/shard_map/ts,psrc->ptrc/dot_general | solution.py:82
  52.5 2.1 %fusion.56 = f32[1,16,10,2048]{3,1,2,0:T(8,128)S(1)} fusion(f32[1,16,12,2048]{3,1,2,0:T(8,128)S(1)} %fusion.49, f32[10,2048]{1,0:T(8,128)S(1)} %slice_add_fusion.5, f32[10,2048]{1,0:T(8,128)S(1)} %bitcast.121), kind=kLoop, calls=%fused_computation.99 | loop fusion | flops 4259840 | bytes 7077888 | tf_op jit(solution)/shard_map/mul | solution.py:86
  55.6 2.5 %convolution_bitcast_fusion.2 = f32[1,16,8,2048]{3,1,2,0:T(8,128)S(1)} fusion(f32[1,16,10,2048]{3,1,2,0:T(8,128)S(1)} %fusion.56, f32[8,2048]{1,0:T(8,128)S(1)} %broadcast_add_fusion, f32[8,2048]{1,0:T(8,128)S(1)} %bitcast.124, f32[16,16]{1,0:T(8,128)S(1)} %copy-done), kind=kOutput, calls=%fused_computation.5 | convolution fusion | flops 53739520 | bytes 5644288 | tf_op jit(solution)/shard_map/ts,psrc->ptrc/dot_general | solution.py:82
  58.2 2.6 %collective-permute-start.9 = (f32[1,3]{1,0:T(1,128)S(1)}, f32[1,3]{1,0:T(1,128)S(1)}, u32[]{:S(2)}, u32[]{:S(2)}) collective-permute-start(f32[1,3]{1,0:T(1,128)S(1)} %add.287), channel_id=1, source_target_pairs={{0,4},{1,5},{2,6},{3,7},{4,0},{5,1},{6,2},{7,3},{8,12},{9,13},{10,... | collective-permute-start | bytes 44 | tf_op jit(solution)/shard_map/ppermute | solution.py:40
  60.8 1.9 %collective-permute-done.9 = f32[1,3]{1,0:T(1,128)S(1)} collective-permute-done((f32[1,3]{1,0:T(1,128)S(1)}, f32[1,3]{1,0:T(1,128)S(1)}, u32[]{:S(2)}, u32[]{:S(2)}) %collective-permute-start.9) | collective-permute-done | bytes 44 | tf_op jit(solution)/shard_map/ppermute | solution.py:40
  63.4 1.5 %multiply_bitcast_fusion.1 = (f32[1,16,8,2048,1]{3,1,2,4,0:T(8,128)S(1)}, f32[1,16,8,2048]{3,1,2,0:T(8,128)}, f32[1,16,8,2048,1]{3,1,2,4,0:T(8,128)S(1)}) fusion(f32[1,16,8,2048]{3,1,2,0:T(8,128)S(1)} %get-tuple-element.26, f32[1,16,12,2048]{3,1,2,0:T(8,128)S(1)} %fusion.49, f32[]{:T(128)S(1)} %bitcast.126, f32[1,16,16,2048]{3,1,2,0:T(8,128)S(1)} %get-tuple-element.30, ...), kind=kLoop, calls=%fused_computation.140 | loop fusion | flops 2097152 | bytes 8388616 | tf_op jit(solution)/shard_map/stack | solution.py:106
  65.4 1.1 %collective-permute-done.10 = f32[1,3]{1,0:T(1,128)S(1)} collective-permute-done((f32[1,3]{1,0:T(1,128)S(1)}, f32[1,3]{1,0:T(1,128)S(1)}, u32[]{:S(2)}, u32[]{:S(2)}) %collective-permute-start.10) | collective-permute-done | bytes 44 | tf_op jit(solution)/shard_map/ppermute | solution.py:40
  67.6 2.5 %collective-permute-done.11 = f32[1,3]{1,0:T(1,128)S(1)} collective-permute-done((f32[1,3]{1,0:T(1,128)S(1)}, f32[1,3]{1,0:T(1,128)S(1)}, u32[]{:S(2)}, u32[]{:S(2)}) %collective-permute-start.11) | collective-permute-done | bytes 44 | tf_op jit(solution)/shard_map/ppermute | solution.py:40
  70.1 2.6 %collective-permute-start.12 = (f32[1,3]{1,0:T(1,128)S(1)}, f32[1,3]{1,0:T(1,128)S(1)}, u32[]{:S(2)}, u32[]{:S(2)}) collective-permute-start(f32[1,3]{1,0:T(1,128)S(1)} %add.297), channel_id=1, source_target_pairs={{0,4},{1,5},{2,6},{3,7},{4,0},{5,1},{6,2},{7,3},{8,12},{9,13},{10,... | collective-permute-start | bytes 44 | tf_op jit(solution)/shard_map/ppermute | solution.py:40
  72.7 1.9 %collective-permute-done.12 = f32[1,3]{1,0:T(1,128)S(1)} collective-permute-done((f32[1,3]{1,0:T(1,128)S(1)}, f32[1,3]{1,0:T(1,128)S(1)}, u32[]{:S(2)}, u32[]{:S(2)}) %collective-permute-start.12) | collective-permute-done | bytes 44 | tf_op jit(solution)/shard_map/ppermute | solution.py:40
  74.8 2.1 %multiply_reduce_fusion = (f32[]{:T(128)}, f32[1,16,8,2048]{3,1,2,0:T(8,128)S(1)}) fusion(f32[1,16,8,2048]{3,1,2,0:T(8,128)S(1)} %get-tuple-element.26, f32[]{:T(128)S(1)} %bitcast.136, f32[1,16,12,2048]{3,1,2,0:T(8,128)S(1)} %slice_divide_fusion.1, f32[1,16,8,2048]{3,1,2,0:T(8,128)} %get-tuple-element.28, f32[]{:T(128)S(1)} %bitcast.141), kind=kLoop, calls=%fused_computation.137 | loop fusion | flops 2097151 | bytes 4194316 | tf_op jit(solution)/shard_map/reduce_sum | solution.py:156
  76.9 1.6 %copy.12 = f32[1,16,8,2048]{3,2,0,1:T(8,128)} copy(f32[1,16,8,2048]{3,1,2,0:T(8,128)S(1)} %get-tuple-element.24) | data formatting | bytes 2097152 | tf_op jit(solution)/shard_map/sub | solution.py:137
  78.5 3.5 %all-to-all-start.1 = ((f32[1,16,8,2048]{3,2,0,1:T(8,128)}), f32[1,16,8,2048]{3,2,0,1:T(8,128)S(1)}, u32[]{:S(2)}, u32[]{:S(2)}) async-start(f32[1,16,8,2048]{3,2,0,1:T(8,128)} %copy.12), calls=%async_computation.1 | async-start | bytes 2097152 | tf_op jit(solution)/shard_map/all_to_all | solution.py:155
  82.9 1.1 %collective-permute-done.13 = f32[4,7]{1,0:T(4,128)S(1)} collective-permute-done((f32[4,7]{1,0:T(4,128)S(1)}, f32[4,7]{1,0:T(4,128)S(1)}, u32[]{:S(2)}, u32[]{:S(2)}) %collective-permute-start.13) | collective-permute-done | bytes 144 | tf_op jit(solution)/shard_map/ppermute | solution.py:40
  85.9 2.5 %collective-permute-done.14 = f32[4,7]{1,0:T(4,128)S(1)} collective-permute-done((f32[4,7]{1,0:T(4,128)S(1)}, f32[4,7]{1,0:T(4,128)S(1)}, u32[]{:S(2)}, u32[]{:S(2)}) %collective-permute-start.14) | collective-permute-done | bytes 144 | tf_op jit(solution)/shard_map/ppermute | solution.py:40
  88.4 2.6 %collective-permute-start.15 = (f32[4,7]{1,0:T(4,128)S(1)}, f32[4,7]{1,0:T(4,128)S(1)}, u32[]{:S(2)}, u32[]{:S(2)}) collective-permute-start(f32[4,7]{1,0:T(4,128)S(1)} %add.302), channel_id=1, source_target_pairs={{0,4},{1,5},{2,6},{3,7},{4,0},{5,1},{6,2},{7,3},{8,12},{9,13},{10,... | collective-permute-start | bytes 344 | tf_op jit(solution)/shard_map/ppermute | solution.py:40
  91.0 1.9 %collective-permute-done.15 = f32[4,7]{1,0:T(4,128)S(1)} collective-permute-done((f32[4,7]{1,0:T(4,128)S(1)}, f32[4,7]{1,0:T(4,128)S(1)}, u32[]{:S(2)}, u32[]{:S(2)}) %collective-permute-start.15) | collective-permute-done | bytes 144 | tf_op jit(solution)/shard_map/ppermute | solution.py:40
  92.9 2.0 %collective-permute-start.16 = (f32[4,7]{1,0:T(4,128)S(1)}, f32[4,7]{1,0:T(4,128)S(1)}, u32[]{:S(2)}, u32[]{:S(2)}) collective-permute-start(f32[4,7]{1,0:T(4,128)S(1)} %add.303), channel_id=1, source_target_pairs={{0,8},{8,0},{16,24},{24,16},{1,9},{9,1},{17,25},{25,17},{2,10},{10... | collective-permute-start | bytes 344 | tf_op jit(solution)/shard_map/ppermute | solution.py:40
  94.9 1.6 %collective-permute-done.16 = f32[4,7]{1,0:T(4,128)S(1)} collective-permute-done((f32[4,7]{1,0:T(4,128)S(1)}, f32[4,7]{1,0:T(4,128)S(1)}, u32[]{:S(2)}, u32[]{:S(2)}) %collective-permute-start.16) | collective-permute-done | bytes 144 | tf_op jit(solution)/shard_map/ppermute | solution.py:40
  96.5 2.0 %collective-permute-start.17 = (f32[4,7]{1,0:T(4,128)S(1)}, f32[4,7]{1,0:T(4,128)S(1)}, u32[]{:S(2)}, u32[]{:S(2)}) collective-permute-start(f32[4,7]{1,0:T(4,128)S(1)} %add.304), channel_id=1, source_target_pairs={{0,16},{8,24},{16,0},{24,8},{1,17},{9,25},{17,1},{25,9},{2,18},{10... | collective-permute-start | bytes 344 | tf_op jit(solution)/shard_map/ppermute | solution.py:40
  98.5 1.6 %collective-permute-done.17 = f32[4,7]{1,0:T(4,128)S(1)} collective-permute-done((f32[4,7]{1,0:T(4,128)S(1)}, f32[4,7]{1,0:T(4,128)S(1)}, u32[]{:S(2)}, u32[]{:S(2)}) %collective-permute-start.17) | collective-permute-done | bytes 144 | tf_op jit(solution)/shard_map/ppermute | solution.py:40
  100.9 1.2 %divide_multiply_fusion = f32[4,4,8,2048]{3,2,1,0:T(8,128)} fusion(f32[4,4,8,2048]{3,2,1,0:T(8,128)S(1)} %bitcast.117, f32[4]{0:T(128)S(1)} %get-tuple-element.48, f32[4]{0:T(128)S(1)} %get-tuple-element.49), kind=kLoop, calls=%fused_computation.136 | loop fusion | flops 524288 | bytes 2097184 | tf_op jit(solution)/shard_map/mul | solution.py:173
  (103 shorter events, 14.9 us)
Async XLA Ops:
  0.6 8.2 %copy-start = (f32[16,16]{1,0:T(8,128)S(1)}, f32[16,16]{1,0:T(8,128)}, u32[]{:S(2)}) copy-start(f32[16,16]{1,0:T(8,128)} %param.7) | copy-start | bytes 3076
  0.6 7.4 %copy-start.2 = (f32[8,2048]{1,0:T(8,128)S(1)}, f32[8,2048]{1,0:T(8,128)}, u32[]{:S(2)}) copy-start(f32[8,2048]{1,0:T(8,128)} %param.6) | copy-start | bytes 196612
  2.9 13.2 %all-to-all-start = ((bf16[4,4,8,2048]{3,2,1,0:T(8,128)(2,1)}), bf16[4,4,8,2048]{3,2,1,0:T(8,128)(2,1)S(1)}, u32[]{:S(2)}, u32[]{:S(2)}) async-start(bf16[4,4,8,2048]{3,2,1,0:T(8,128)(2,1)} %multiply_convert_fusion), calls=%async_computation | async-start | bytes 1048576 | tf_op jit(solution)/shard_map/all_to_all | solution.py:74
  8.1 1.5 %collective-permute-start.2 = (f32[6,2048]{1,0:T(8,128)S(1)}, f32[6,2048]{1,0:T(8,128)S(1)}, u32[]{:S(2)}, u32[]{:S(2)}) collective-permute-start(f32[6,2048]{1,0:T(8,128)S(1)} %get-tuple-element.44), channel_id=1, source_target_pairs={{0,1},{2,3},{4,5},{6,7},{1,0},{3,2},{5,4},{7,6},{8,9},{10,11},{12,... | collective-permute-start | bytes 147464 | tf_op jit(solution)/shard_map/ppermute | solution.py:64
  8.2 1.4 %collective-permute-start.3 = (f32[6,2048]{1,0:T(8,128)S(1)}, f32[6,2048]{1,0:T(8,128)S(1)}, u32[]{:S(2)}, u32[]{:S(2)}) collective-permute-start(f32[6,2048]{1,0:T(8,128)S(1)} %get-tuple-element.45), channel_id=1, source_target_pairs={{1,2},{3,4},{5,6},{2,1},{4,3},{6,5},{9,10},{11,12},{13,14},{10,9},... | collective-permute-start | bytes 147464 | tf_op jit(solution)/shard_map/ppermute | solution.py:63
  16.4 1.8 %collective-permute-start = (bf16[1,16,6,2048]{3,1,2,0:T(8,128)(2,1)S(1)}, bf16[1,16,6,2048]{3,1,2,0:T(8,128)(2,1)S(1)}, u32[]{:S(2)}, u32[]{:S(2)}) collective-permute-start(bf16[1,16,6,2048]{3,1,2,0:T(8,128)(2,1)S(1)} %get-tuple-element.40), channel_id=1, source_target_pairs={{0,1},{2,3},{4,5},{6,7},{1,0},{3,2},{5,4},{7,6},{8,9},{10,11},{12,... | collective-permute-start | bytes 1179656 | tf_op jit(solution)/shard_map/ppermute | solution.py:64
  16.5 1.7 %collective-permute-start.1 = (bf16[1,16,6,2048]{3,1,2,0:T(8,128)(2,1)S(1)}, bf16[1,16,6,2048]{3,1,2,0:T(8,128)(2,1)S(1)}, u32[]{:S(2)}, u32[]{:S(2)}) collective-permute-start(bf16[1,16,6,2048]{3,1,2,0:T(8,128)(2,1)S(1)} %get-tuple-element.41), channel_id=1, source_target_pairs={{1,2},{3,4},{5,6},{2,1},{4,3},{6,5},{9,10},{11,12},{13,14},{10,9},... | collective-permute-start | bytes 1179656 | tf_op jit(solution)/shard_map/ppermute | solution.py:63
  18.6 0.7 copy-start.1
  29.5 8.3 %slice-start = ((f32[1,1,20,2048]{3,1,2,0:T(1,128)}), f32[1,1,14,2048]{3,1,2,0:T(1,128)S(1)}, s32[]{:S(2)}) async-start(f32[1,1,20,2048]{3,1,2,0:T(1,128)} %copy-done.1), calls=%async_computation.2 | async-start | bytes 229376 | tf_op jit(solution)/shard_map/slice | solution.py:86
  29.5 8.3 %slice-start.1 = ((f32[1,1,20,2048]{3,1,2,0:T(1,128)}), f32[1,1,12,2048]{3,1,2,0:T(1,128)S(1)}, s32[]{:S(2)}) async-start(f32[1,1,20,2048]{3,1,2,0:T(1,128)} %copy-done.1), calls=%async_computation.3 | async-start | bytes 196608 | tf_op jit(solution)/shard_map/slice | solution.py:86
  29.5 8.4 %slice-start.2 = ((f32[1,1,20,2048]{3,1,2,0:T(1,128)}), f32[1,1,10,2048]{3,1,2,0:T(1,128)S(1)}, s32[]{:S(2)}) async-start(f32[1,1,20,2048]{3,1,2,0:T(1,128)} %copy-done.1), calls=%async_computation.4 | async-start | bytes 163840 | tf_op jit(solution)/shard_map/slice | solution.py:86
  29.5 8.4 %slice-start.3 = ((f32[1,1,20,2048]{3,1,2,0:T(1,128)}), f32[1,1,8,2048]{3,1,2,0:T(1,128)S(1)}, s32[]{:S(2)}) async-start(f32[1,1,20,2048]{3,1,2,0:T(1,128)} %copy-done.1), calls=%async_computation.5 | async-start | bytes 131072 | tf_op jit(solution)/shard_map/slice | solution.py:86
  29.9 11.7 %collective-permute-start.4 = (f32[1,2]{1,0:T(1,128)S(1)}, f32[1,2]{1,0:T(1,128)S(1)}, u32[]{:S(2)}, u32[]{:S(2)}) collective-permute-start(f32[1,2]{1,0:T(1,128)S(1)} %bitcast.142), channel_id=1, source_target_pairs={{0,1},{1,0},{2,3},{3,2},{4,5},{5,4},{6,7},{7,6},{8,9},{9,8},{10,11... | collective-permute-start | bytes 32 | tf_op jit(solution)/shard_map/ppermute | solution.py:40
  41.6 4.2 %collective-permute-start.5 = (f32[1,2]{1,0:T(1,128)S(1)}, f32[1,2]{1,0:T(1,128)S(1)}, u32[]{:S(2)}, u32[]{:S(2)}) collective-permute-start(f32[1,2]{1,0:T(1,128)S(1)} %bitcast_add_fusion.2), channel_id=1, source_target_pairs={{0,2},{1,3},{2,0},{3,1},{4,6},{5,7},{6,4},{7,5},{8,10},{9,11},{10,... | collective-permute-start | bytes 32 | tf_op jit(solution)/shard_map/ppermute | solution.py:40
  45.9 4.5 %collective-permute-start.6 = (f32[1,2]{1,0:T(1,128)S(1)}, f32[1,2]{1,0:T(1,128)S(1)}, u32[]{:S(2)}, u32[]{:S(2)}) collective-permute-start(f32[1,2]{1,0:T(1,128)S(1)} %add.271), channel_id=1, source_target_pairs={{0,4},{1,5},{2,6},{3,7},{4,0},{5,1},{6,2},{7,3},{8,12},{9,13},{10,... | collective-permute-start | bytes 32 | tf_op jit(solution)/shard_map/ppermute | solution.py:40
  52.5 2.1 %collective-permute-start.7 = (f32[1,3]{1,0:T(1,128)S(1)}, f32[1,3]{1,0:T(1,128)S(1)}, u32[]{:S(2)}, u32[]{:S(2)}) collective-permute-start(f32[1,3]{1,0:T(1,128)S(1)} %bitcast.143), channel_id=1, source_target_pairs={{0,1},{1,0},{2,3},{3,2},{4,5},{5,4},{6,7},{7,6},{8,9},{9,8},{10,11... | collective-permute-start | bytes 44 | tf_op jit(solution)/shard_map/ppermute | solution.py:40
  54.6 3.6 %collective-permute-start.8 = (f32[1,3]{1,0:T(1,128)S(1)}, f32[1,3]{1,0:T(1,128)S(1)}, u32[]{:S(2)}, u32[]{:S(2)}) collective-permute-start(f32[1,3]{1,0:T(1,128)S(1)} %bitcast_add_fusion.1), channel_id=1, source_target_pairs={{0,2},{1,3},{2,0},{3,1},{4,6},{5,7},{6,4},{7,5},{8,10},{9,11},{10,... | collective-permute-start | bytes 44 | tf_op jit(solution)/shard_map/ppermute | solution.py:40
  58.2 4.5 %collective-permute-start.9 = (f32[1,3]{1,0:T(1,128)S(1)}, f32[1,3]{1,0:T(1,128)S(1)}, u32[]{:S(2)}, u32[]{:S(2)}) collective-permute-start(f32[1,3]{1,0:T(1,128)S(1)} %add.287), channel_id=1, source_target_pairs={{0,4},{1,5},{2,6},{3,7},{4,0},{5,1},{6,2},{7,3},{8,12},{9,13},{10,... | collective-permute-start | bytes 44 | tf_op jit(solution)/shard_map/ppermute | solution.py:40
  65.3 1.2 %collective-permute-start.10 = (f32[1,3]{1,0:T(1,128)S(1)}, f32[1,3]{1,0:T(1,128)S(1)}, u32[]{:S(2)}, u32[]{:S(2)}) collective-permute-start(f32[1,3]{1,0:T(1,128)S(1)} %bitcast.144), channel_id=1, source_target_pairs={{0,1},{1,0},{2,3},{3,2},{4,5},{5,4},{6,7},{7,6},{8,9},{9,8},{10,11... | collective-permute-start | bytes 44 | tf_op jit(solution)/shard_map/ppermute | solution.py:40
  66.5 3.6 %collective-permute-start.11 = (f32[1,3]{1,0:T(1,128)S(1)}, f32[1,3]{1,0:T(1,128)S(1)}, u32[]{:S(2)}, u32[]{:S(2)}) collective-permute-start(f32[1,3]{1,0:T(1,128)S(1)} %bitcast_add_fusion), channel_id=1, source_target_pairs={{0,2},{1,3},{2,0},{3,1},{4,6},{5,7},{6,4},{7,5},{8,10},{9,11},{10,... | collective-permute-start | bytes 44 | tf_op jit(solution)/shard_map/ppermute | solution.py:40
  70.1 4.5 %collective-permute-start.12 = (f32[1,3]{1,0:T(1,128)S(1)}, f32[1,3]{1,0:T(1,128)S(1)}, u32[]{:S(2)}, u32[]{:S(2)}) collective-permute-start(f32[1,3]{1,0:T(1,128)S(1)} %add.297), channel_id=1, source_target_pairs={{0,4},{1,5},{2,6},{3,7},{4,0},{5,1},{6,2},{7,3},{8,12},{9,13},{10,... | collective-permute-start | bytes 44 | tf_op jit(solution)/shard_map/ppermute | solution.py:40
  78.5 22.4 %all-to-all-start.1 = ((f32[1,16,8,2048]{3,2,0,1:T(8,128)}), f32[1,16,8,2048]{3,2,0,1:T(8,128)S(1)}, u32[]{:S(2)}, u32[]{:S(2)}) async-start(f32[1,16,8,2048]{3,2,0,1:T(8,128)} %copy.12), calls=%async_computation.1 | async-start | bytes 2097152 | tf_op jit(solution)/shard_map/all_to_all | solution.py:155
  82.8 1.2 %collective-permute-start.13 = (f32[4,7]{1,0:T(4,128)S(1)}, f32[4,7]{1,0:T(4,128)S(1)}, u32[]{:S(2)}, u32[]{:S(2)}) collective-permute-start(f32[4,7]{1,0:T(4,128)S(1)} %dynamic_update_slice.5), channel_id=1, source_target_pairs={{0,1},{1,0},{2,3},{3,2},{4,5},{5,4},{6,7},{7,6},{8,9},{9,8},{10,11... | collective-permute-start | bytes 344 | tf_op jit(solution)/shard_map/ppermute | solution.py:40
  84.8 3.6 %collective-permute-start.14 = (f32[4,7]{1,0:T(4,128)S(1)}, f32[4,7]{1,0:T(4,128)S(1)}, u32[]{:S(2)}, u32[]{:S(2)}) collective-permute-start(f32[4,7]{1,0:T(4,128)S(1)} %add.301), channel_id=1, source_target_pairs={{0,2},{1,3},{2,0},{3,1},{4,6},{5,7},{6,4},{7,5},{8,10},{9,11},{10,... | collective-permute-start | bytes 344 | tf_op jit(solution)/shard_map/ppermute | solution.py:40
  88.4 4.5 %collective-permute-start.15 = (f32[4,7]{1,0:T(4,128)S(1)}, f32[4,7]{1,0:T(4,128)S(1)}, u32[]{:S(2)}, u32[]{:S(2)}) collective-permute-start(f32[4,7]{1,0:T(4,128)S(1)} %add.302), channel_id=1, source_target_pairs={{0,4},{1,5},{2,6},{3,7},{4,0},{5,1},{6,2},{7,3},{8,12},{9,13},{10,... | collective-permute-start | bytes 344 | tf_op jit(solution)/shard_map/ppermute | solution.py:40
  92.9 3.6 %collective-permute-start.16 = (f32[4,7]{1,0:T(4,128)S(1)}, f32[4,7]{1,0:T(4,128)S(1)}, u32[]{:S(2)}, u32[]{:S(2)}) collective-permute-start(f32[4,7]{1,0:T(4,128)S(1)} %add.303), channel_id=1, source_target_pairs={{0,8},{8,0},{16,24},{24,16},{1,9},{9,1},{17,25},{25,17},{2,10},{10... | collective-permute-start | bytes 344 | tf_op jit(solution)/shard_map/ppermute | solution.py:40
  96.5 3.6 %collective-permute-start.17 = (f32[4,7]{1,0:T(4,128)S(1)}, f32[4,7]{1,0:T(4,128)S(1)}, u32[]{:S(2)}, u32[]{:S(2)}) collective-permute-start(f32[4,7]{1,0:T(4,128)S(1)} %add.304), channel_id=1, source_target_pairs={{0,16},{8,24},{16,0},{24,8},{1,17},{9,25},{17,1},{25,9},{2,18},{10... | collective-permute-start | bytes 344 | tf_op jit(solution)/shard_map/ppermute | solution.py:40
  100.7 1.4 %copy-start.3 = (f32[4,3]{1,0:T(4,128)}, f32[4,3]{1,0:T(4,128)S(1)}, u32[]{:S(2)}) copy-start(f32[4,3]{1,0:T(4,128)S(1)} %get-tuple-element.46) | copy-start | bytes 148
